TPU v7x, 256 devices: a whole 4x4x8 slice. The times are simulated.
256 devices in a mesh: prow: 8 (over z_hi, core), pcol: 32 (over x, z_lo, y).
Axes of the slice: x: 4, y: 4, z: 8 (z_hi: 4, z_lo: 2; z = z_hi * 2 + z_lo), core: 2. Of those that a mesh axis runs over, the one named last changes fastest.
Arguments:
- slab: float32 [2048, 98304], P('pcol', 'prow'), may hold values from -6 to 6
- vectors: float32 [98304, 512], P(('prow', 'pcol')), may hold values from -0.01953125 to 0.01953125
- tfactors: float32 [4, 128, 128], replicated, as said below
Outputs:
- transformed: float32 [2048, 98304], P('pcol', 'prow')
Inputs may be any that keep to these rules, and one draw needn't show every extreme that they name: Each tfactors[k] is upper triangular with diagonal entries between 1 and 2.
All inputs are finite; a program needn't handle non-finite values.
Results may differ from a plain program's by a relative error of at most 0.0001.
Values sent between devices are 32-bit elements; how exact they have to be, the bound alone decides.
No kernel may reach another device: no remote copies, remote signals or barrier semaphores. Data moves between devices by JAX's collectives and lax.ppermute only.
A program may use at most 128 MiB of HBM per device.

v0:
```python
import jax
import jax.numpy as jnp
from jax import lax
from jax.sharding import PartitionSpec as P


def matmul(left, right):
    return jnp.dot(left, right, precision=lax.Precision.HIGHEST, preferred_element_type=jnp.float32)


def per_device(slab, vectors, tfactors):
    count = tfactors.shape[0]
    width = tfactors.shape[1]
    work = slab
    for k in reversed(range(count)):
        basis = lax.all_gather(vectors[:, k * width : (k + 1) * width], "pcol", axis=0, tiled=True)
        products = lax.psum(matmul(work, basis), "prow")
        work = work - matmul(matmul(products, tfactors[k].T), basis.T)
    return work


def solution(mesh):
    in_specs = (P("pcol", "prow"), P(("prow", "pcol"), None), P())
    out_specs = P("pcol", "prow")
    return jax.shard_map(
        per_device, mesh=mesh, in_specs=in_specs, out_specs=out_specs, check_vma=False
    )
```

profile of v0, /device:TPU:64, one launch (start us, length us, event | category | flops | bytes accessed | tf_op | source)
XLA Modules:
  0.0 726.7 jit_solution(4784247094145726816)
XLA Ops:
  6.5 0.0 all-gather.5.cloned.1.call-start
  6.5 2.1 fusion.12
  8.6 0.0 all-gather.5.cloned.1.call-update
  8.7 0.0 all-gather.7.cloned.1.call-start
  8.7 0.7 all-gather.7.cloned.1.call-update
  9.4 0.0 all-gather.9.cloned.1.call-start
  9.5 0.7 all-gather.9.cloned.1.call-update
  10.2 0.0 all-gather.11.cloned.1.call-start
  10.2 0.5 all-gather.11.cloned.1.call-update
  10.7 0.0 copy-start.2
  10.7 166.0 %all-gather.5.cloned.1.call-done = f32[12288,128]{1,0:T(8,128)} async-done(((f32[384,128]{1,0:T(8,128)}), f32[12288,128]{1,0:T(8,128)}) %all-gather.5.cloned.1.call-update) | async-done | bytes 6291472 | tf_op jit(solution)/shard_map/all_gather | solution.py:16
  176.7 6.4 fusion.13
  183.2 25.5 %psum.28 = f32[64,128]{1,0:T(8,128)S(1)} all-reduce(f32[64,128]{1,0:T(8,128)S(1)} %fusion.13), channel_id=1, replica_groups=mesh['prow'=8,'pcol'=32] {'prow'}, use_global_device_ids=true, to_apply=%region_0.0 | all-reduce | flops 8192 | bytes 65536 | tf_op jit(solution)/shard_map/psum | solution.py:17
  208.7 0.0 copy-done.2
  208.7 0.2 fusion.6
  208.9 9.4 %convolution_subtract_fusion.3 = f32[64,12288]{1,0:T(8,128)S(1)} fusion(f32[64,12288]{1,0:T(8,128)} %param.3, f32[64,128]{1,0:T(8,128)S(1)} %fusion.6, f32[12288,128]{1,0:T(8,128)} %all-gather.5.cloned.1.call-done), kind=kOutput, calls=%fused_computation.3 | convolution fusion | flops 1208745984 | bytes 12615680 | tf_op jit(solution)/shard_map/dot_general | solution.py:8
  218.4 0.0 copy-start.1
  218.4 125.8 %all-gather.7.cloned.1.call-done = f32[12288,128]{1,0:T(8,128)} async-done(((f32[384,128]{1,0:T(8,128)}), f32[12288,128]{1,0:T(8,128)}) %all-gather.7.cloned.1.call-update) | async-done | bytes 6291472 | tf_op jit(solution)/shard_map/all_gather | solution.py:16
  344.2 5.9 fusion.14
  350.2 0.0 copy-done.1
  350.2 25.2 %psum.29 = f32[64,128]{1,0:T(8,128)S(1)} all-reduce(f32[64,128]{1,0:T(8,128)S(1)} %fusion.14), channel_id=1, replica_groups=mesh['prow'=8,'pcol'=32] {'prow'}, use_global_device_ids=true, to_apply=%region_1.0 | all-reduce | flops 8192 | bytes 65536 | tf_op jit(solution)/shard_map/psum | solution.py:17
  375.3 0.2 fusion.4
  375.6 9.4 %convolution_subtract_fusion.2 = f32[64,12288]{1,0:T(8,128)S(1)} fusion(f32[64,12288]{1,0:T(8,128)} %copy-done.1, f32[64,128]{1,0:T(8,128)S(1)} %fusion.4, f32[12288,128]{1,0:T(8,128)} %all-gather.7.cloned.1.call-done), kind=kOutput, calls=%fused_computation.2 | convolution fusion | flops 1208745984 | bytes 12615680 | tf_op jit(solution)/shard_map/dot_general | solution.py:8
  385.0 126.0 %all-gather.9.cloned.1.call-done = f32[12288,128]{1,0:T(8,128)} async-done(((f32[384,128]{1,0:T(8,128)}), f32[12288,128]{1,0:T(8,128)}) %all-gather.9.cloned.1.call-update) | async-done | bytes 6291472 | tf_op jit(solution)/shard_map/all_gather | solution.py:16
  511.0 5.9 fusion.15
  516.9 25.4 %psum.30 = f32[64,128]{1,0:T(8,128)S(1)} all-reduce(f32[64,128]{1,0:T(8,128)S(1)} %fusion.15), channel_id=1, replica_groups=mesh['prow'=8,'pcol'=32] {'prow'}, use_global_device_ids=true, to_apply=%region_2.0 | all-reduce | flops 8192 | bytes 65536 | tf_op jit(solution)/shard_map/psum | solution.py:17
  542.3 0.2 fusion.2
  542.6 10.1 %convolution_subtract_fusion.1 = f32[64,12288]{1,0:T(8,128)} fusion(f32[64,12288]{1,0:T(8,128)S(1)} %convolution_subtract_fusion.2, f32[64,128]{1,0:T(8,128)S(1)} %fusion.2, f32[12288,128]{1,0:T(8,128)} %all-gather.9.cloned.1.call-done), kind=kOutput, calls=%fused_computation.1 | convolution fusion | flops 1208745984 | bytes 12615680 | tf_op jit(solution)/shard_map/dot_general | solution.py:8
  552.6 0.0 copy-start
  552.6 126.4 %all-gather.11.cloned.1.call-done = f32[12288,128]{1,0:T(8,128)} async-done(((f32[384,128]{1,0:T(8,128)}), f32[12288,128]{1,0:T(8,128)}) %all-gather.11.cloned.1.call-update) | async-done | bytes 6291472 | tf_op jit(solution)/shard_map/all_gather | solution.py:16
  679.0 6.4 fusion.16
  685.5 24.4 %psum.31 = f32[64,128]{1,0:T(8,128)S(1)} all-reduce(f32[64,128]{1,0:T(8,128)S(1)} %fusion.16), channel_id=1, replica_groups=mesh['prow'=8,'pcol'=32] {'prow'}, use_global_device_ids=true, to_apply=%region_3.0 | all-reduce | flops 8192 | bytes 65536 | tf_op jit(solution)/shard_map/psum | solution.py:17
  709.8 0.2 fusion
  710.1 0.0 copy-done
  710.1 10.1 %convolution_subtract_fusion = f32[64,12288]{1,0:T(8,128)} fusion(f32[64,12288]{1,0:T(8,128)S(1)} %copy-done, f32[64,128]{1,0:T(8,128)S(1)} %fusion, f32[12288,128]{1,0:T(8,128)} %all-gather.11.cloned.1.call-done), kind=kOutput, calls=%fused_computation | convolution fusion | flops 1208745984 | bytes 12615680 | tf_op jit(solution)/shard_map/dot_general | solution.py:8
Async XLA Ops:
  6.5 170.2 %all-gather.5.cloned.1.call-start = ((), (), s32[]{:S(2)}) async-start(), calls=%async_computation | async-start | bytes 6488064 | tf_op jit(solution)/shard_map/all_gather | solution.py:16
  8.7 335.5 %all-gather.7.cloned.1.call-start = ((), (), s32[]{:S(2)}) async-start(), calls=%async_computation.1 | async-start | bytes 6488064 | tf_op jit(solution)/shard_map/all_gather | solution.py:16
  9.4 501.6 %all-gather.9.cloned.1.call-start = ((), (), s32[]{:S(2)}) async-start(), calls=%async_computation.2 | async-start | bytes 6488064 | tf_op jit(solution)/shard_map/all_gather | solution.py:16
  10.2 668.9 %all-gather.11.cloned.1.call-start = ((), (), s32[]{:S(2)}) async-start(), calls=%async_computation.3 | async-start | bytes 6488064 | tf_op jit(solution)/shard_map/all_gather | solution.py:16
  10.7 198.0 %copy-start.2 = (f32[4,128,128]{2,1,0:T(8,128)S(1)}, f32[4,128,128]{2,1,0:T(8,128)}, u32[]{:S(2)}) copy-start(f32[4,128,128]{2,1,0:T(8,128)} %param.5) | copy-start | bytes 786436
  218.4 131.8 %copy-start.1 = (f32[64,12288]{1,0:T(8,128)}, f32[64,12288]{1,0:T(8,128)S(1)}, u32[]{:S(2)}) copy-start(f32[64,12288]{1,0:T(8,128)S(1)} %convolution_subtract_fusion.3) | copy-start | bytes 9437188
  552.6 157.4 %copy-start = (f32[64,12288]{1,0:T(8,128)S(1)}, f32[64,12288]{1,0:T(8,128)}, u32[]{:S(2)}) copy-start(f32[64,12288]{1,0:T(8,128)} %convolution_subtract_fusion.1) | copy-start | bytes 9437188
Sparse Core Ops, SparseCore 0:
  9.1 167.5 all-gather.4
  178.5 165.6 all-gather.6
  346.0 164.9 all-gather.8
  512.6 166.3 all-gather.10
where the time goes:
time: 730 us; the launch traced here: 727 us
  waiting for transfers between devices  546 us (75%)
  blocking collectives  100 us (14%)
  matrix products  64.7 us (9%)
  between operations  13.2 us (2%)
    all_gather x4, waiting for transfers between devices, per_device(): lax.all_gather(vectors[:, k * width:(k + 1) * width], 'pcol', axis=0, til...  544 us
    psum x4, blocking collectives, per_device(): products = lax.psum(matmul(work, basis), 'prow')  100 us
    dot_general x12, matrix products, matmul(): jnp.dot(left, right, precision=lax.Precision.HIGHEST, preferred_element_t...  64.7 us
  transfers between devices with their start and end apart: 4, of which 4 were waited for; matrix products, arithmetic and copies ran while one was open for 7% of the time, Pallas kernels for 0%

commit v1 on v0

v1 whole, which is shorter than its diff:
```python
import jax
import jax.numpy as jnp
from jax import lax
from jax.sharding import Mesh
from jax.sharding import PartitionSpec as P

PCOL_PARTS = (4, 2, 4)
GROUP = ("zl", "y")


def matmul(left, right):
    return jnp.dot(left, right, precision=lax.Precision.HIGHEST, preferred_element_type=jnp.float32)


def per_device(slab, vectors, tfactors):
    rows, cols = slab.shape
    depth = vectors.shape[0]
    count = tfactors.shape[0]
    width = tfactors.shape[1]
    nx = PCOL_PARTS[0]
    ng = PCOL_PARTS[1] * PCOL_PARTS[2]

    gram = lax.psum(matmul(vectors[:, width:].T, vectors[:, : (count - 1) * width]), ("prow", "x", "zl", "y"))

    basis = lax.all_gather(vectors, "x", axis=0, tiled=True)
    work = slab.reshape(rows, nx, ng, depth).transpose(2, 0, 1, 3)
    work = lax.all_to_all(work, GROUP, 0, 0, tiled=True).reshape(ng * rows, nx * depth)

    products = lax.psum(matmul(work, basis), ("zl", "y", "prow"))

    scaled = [None] * count
    for k in reversed(range(count)):
        part = products[:, k * width : (k + 1) * width]
        for j in range(k + 1, count):
            block = gram[(j - 1) * width : j * width, k * width : (k + 1) * width]
            part = part - matmul(scaled[j], block)
        scaled[k] = matmul(part, tfactors[k].T)
    scaled = jnp.concatenate(scaled, axis=1)

    work = work - matmul(scaled, basis.T)
    work = work.reshape(ng, rows, nx, depth)
    work = lax.all_to_all(work, GROUP, 0, 0, tiled=True)
    return work.transpose(1, 2, 0, 3).reshape(rows, cols)


def solution(mesh):
    devices = mesh.devices.reshape((mesh.shape["prow"],) + PCOL_PARTS)
    fine = Mesh(devices, ("prow", "x", "zl", "y"))
    cols = ("x", "zl", "y")
    in_specs = (P(cols, "prow"), P(("prow",) + cols, None), P())
    out_specs = P(cols, "prow")
    return jax.shard_map(per_device, mesh=fine, in_specs=in_specs, out_specs=out_specs, check_vma=False)
```

time: 730 us -> 593 us (0.81)
  waiting for transfers between devices: 546 us -> 475 us
  blocking collectives: 100 us -> 43.8 us
  matrix products: 64.7 us -> 35.6 us
  local copies, waits for them, and re-layouts: 2.13 us -> 17.1 us
    all_gather x4 -> x1, waiting for transfers between devices: 544 us -> 5.36 us  [per_device(): basis = lax.all_gather(vectors, 'x', axis=0, tiled=True)]
    psum x0 -> x2, waiting for transfers between devices: none -> 432 us  [the longest x1 255 us: per_device(): lax.psum(matmul(vectors[:, width:].T, vectors[:, :(count - 1) * width]),...]
    psum x4 -> x0, blocking collectives: 100 us -> none  [per_device(): products = lax.psum(matmul(work, basis), 'prow')]
    all_to_all x0 -> x1, blocking collectives: none -> 43.8 us  [per_device(): work = lax.all_to_all(work, GROUP, 0, 0, tiled=True)]
    all_to_all x0 -> x1, waiting for transfers between devices: none -> 36.5 us  [per_device(): lax.all_to_all(work, GROUP, 0, 0, tiled=True).reshape(ng * rows, nx * depth)]
    dot_general x12 -> x13, matrix products: 64.7 us -> 35.6 us  [matmul(): jnp.dot(left, right, precision=lax.Precision.HIGHEST, preferred_element_t...]
    unnamed x6 -> x9, local copies, waits for them, and re-layouts: 0.02 us -> 9.68 us
  transfers between devices with their start and end apart: 4 -> 4, of which waited for: 4 -> 4; matrix products, arithmetic and copies ran while one was open for 7% -> 1% of each run, Pallas kernels for 0% -> 0%
where the time goes in v1:
time: 593 us; the launch traced here: 590 us
  waiting for transfers between devices  475 us (80%)
  blocking collectives  43.8 us (7%)
  matrix products  35.6 us (6%)
  local copies, waits for them, and re-layouts  17.1 us (3%)
  between operations  13.2 us (2%)
  starting transfers between devices  6.12 us (1%)
    psum x1, waiting for transfers between devices, per_device(): lax.psum(matmul(vectors[:, width:].T, vectors[:, :(count - 1) * width]),...  255 us
    psum x1, waiting for transfers between devices, per_device(): products = lax.psum(matmul(work, basis), ('zl', 'y', 'prow'))  178 us
    all_to_all x1, blocking collectives, per_device(): work = lax.all_to_all(work, GROUP, 0, 0, tiled=True)  43.8 us
    all_to_all x1, waiting for transfers between devices, per_device(): lax.all_to_all(work, GROUP, 0, 0, tiled=True).reshape(ng * rows, nx * depth)  36.5 us
    dot_general x13, matrix products, matmul(): jnp.dot(left, right, precision=lax.Precision.HIGHEST, preferred_element_t...  35.6 us
  transfers between devices with their start and end apart: 4, of which 4 were waited for; matrix products, arithmetic and copies ran while one was open for 1% of the time, Pallas kernels for 0%

profile of v1, /device:TPU:64, one launch (start us, length us, event | category | flops | bytes accessed | tf_op | source)
XLA Modules:
  0.0 590.5 jit_solution(9328307342298171551)
XLA Ops:
  6.5 2.4 copy.6
  9.0 2.5 copy.10
  11.5 5.8 all-to-all-start
  17.3 0.0 all-gather.2.cloned.1.call-start
  17.3 0.7 all-gather.2.cloned.1.call-update
  18.0 0.0 all-reduce.3.cloned.1.call-start
  18.1 36.5 %all-to-all-done = f32[8,64,4,384]{3,2,1,0:T(4,128)S(1)} async-done(((f32[8,64,4,384]{3,2,1,0:T(4,128)}), f32[8,64,4,384]{3,2,1,0:T(4,128)S(1)}, u32[]{:S(2)}, u32[]{:S(2)}) %all-to-all-start) | async-done | bytes 3145760 | tf_op jit(solution)/shard_map/all_to_all | solution.py:27
  54.6 0.0 copy-start.1
  54.6 1.7 copy-done.1
  56.2 2.1 copy.7
  58.3 5.4 all-gather.2.cloned.1.call-done
  63.7 7.5 %fusion.30 = f32[512,512]{1,0:T(8,128)} fusion(f32[512,1536]{1,0:T(8,128)S(1)} %bitcast.37, f32[1536,512]{1,0:T(8,128)} %all-gather.2.cloned.1.call-done), kind=kOutput, calls=%fused_computation.38 | convolution fusion | flops 4831838208 | bytes 7340032 | tf_op jit(solution)/shard_map/dot_general | solution.py:12
  71.2 0.0 all-reduce.3.cloned.1.call-update
  71.2 0.2 all-reduce.5.cloned.1.call-start
  71.4 3.4 fusion.7
  74.8 0.0 all-reduce.5.cloned.1.call-update
  74.8 177.5 %all-reduce.3.cloned.1.call-done = f32[512,512]{1,0:T(8,128)} async-done(((f32[512,512]{1,0:T(8,128)}), f32[512,512]{1,0:T(8,128)}) %all-reduce.3.cloned.1.call-update) | async-done | bytes 1048592 | tf_op jit(solution)/shard_map/psum | solution.py:29
  252.3 1.3 fusion.10
  253.7 254.5 %all-reduce.5.cloned.1.call-done = f32[384,384]{1,0:T(8,128)} async-done(((f32[384,384]{1,0:T(8,128)}), f32[384,384]{1,0:T(8,128)}) %all-reduce.5.cloned.1.call-update) | async-done | bytes 589840 | tf_op jit(solution)/shard_map/psum | solution.py:23
  508.2 0.0 copy-start.2
  508.2 1.6 convolution_subtract_fusion.6
  509.8 0.0 copy-start
  509.9 1.4 fusion.22
  511.3 1.6 convolution_subtract_fusion.5
  512.8 1.4 convolution_subtract_fusion.4
  514.3 0.0 copy-done.2
  514.3 0.4 fusion.20
  514.7 1.6 convolution_subtract_fusion.3
  516.3 1.4 convolution_subtract_fusion.2
  517.7 1.4 convolution_subtract_fusion.1
  519.1 0.4 fusion.18
  519.5 0.0 copy-done
  519.5 12.2 %convolution_subtract_fusion = f32[512,1536]{1,0:T(8,128)} fusion(f32[512,1536]{1,0:T(8,128)S(1)} %bitcast.38, f32[1536,512]{1,0:T(8,128)S(1)} %copy-done, f32[512,128]{0,1:T(8,128)S(1)} %fusion.10, f32[512,128]{0,1:T(8,128)S(1)} %fusion.22, f32[512,128]{0,1:T(8,128)S(1)} %fusion.20, f32[512,128]{0,1:T(8,128)S(1)} %fusion.18), kind=kOutput, calls=%fused_computation | convolution fusion | flops 4833411072 | bytes 10485760 | tf_op jit(solution)/shard_map/dot_general | solution.py:12
  531.7 3.2 reshape.14
  534.9 43.8 %all_to_all.10 = f32[8,64,4,384]{3,2,1,0:T(4,128)S(1)} all-to-all(f32[8,64,4,384]{3,2,1,0:T(4,128)S(1)} %reshape.14), channel_id=1, replica_groups=mesh['prow'=8,'x'=4,'zl'=2,'y'=4] {'zl','y'}, dimensions={0} | all-to-all | bytes 6291456 | tf_op jit(solution)/shard_map/all_to_all | solution.py:42
  578.7 1.8 copy.5
  580.5 3.4 copy.8
Async XLA Ops:
  11.5 43.1 %all-to-all-start = ((f32[8,64,4,384]{3,2,1,0:T(4,128)}), f32[8,64,4,384]{3,2,1,0:T(4,128)S(1)}, u32[]{:S(2)}, u32[]{:S(2)}) async-start(f32[8,64,4,384]{3,2,1,0:T(4,128)} %bitcast.40), calls=%async_computation | async-start | bytes 6291456 | tf_op jit(solution)/shard_map/all_to_all | solution.py:27
  17.3 46.4 %all-gather.2.cloned.1.call-start = ((), (), s32[]{:S(2)}) async-start(), calls=%async_computation.2 | async-start | bytes 3932160 | tf_op jit(solution)/shard_map/all_gather | solution.py:25
  18.0 234.3 %all-reduce.3.cloned.1.call-start = ((), (), s32[]{:S(2)}) async-start(), calls=%async_computation.3 | async-start | bytes 2097152 | tf_op jit(solution)/shard_map/psum | solution.py:29
  54.6 1.7 copy-start.1
  71.2 437.0 %all-reduce.5.cloned.1.call-start = ((), (), s32[]{:S(2)}) async-start(), calls=%async_computation.4 | async-start | bytes 1179648 | tf_op jit(solution)/shard_map/psum | solution.py:23
  508.2 6.1 %copy-start.2 = (f32[4,128,128]{2,1,0:T(8,128)S(1)}, f32[4,128,128]{2,1,0:T(8,128)}, u32[]{:S(2)}) copy-start(f32[4,128,128]{2,1,0:T(8,128)} %param.5) | copy-start | bytes 786436
  509.8 9.7 %copy-start = (f32[1536,512]{1,0:T(8,128)S(1)}, f32[1536,512]{1,0:T(8,128)}, u32[]{:S(2)}) copy-start(f32[1536,512]{1,0:T(8,128)} %all-gather.2.cloned.1.call-done) | copy-start | bytes 9437188
Sparse Core Ops, SparseCore 0:
  19.9 43.7 all-gather.1
  71.3 180.9 all-reduce.2
  258.8 249.4 all-reduce.4

commit v2 on v1

v2 whole, which is shorter than its diff:
```python
import jax
import jax.numpy as jnp
from jax import lax
from jax.sharding import Mesh
from jax.sharding import PartitionSpec as P

PCOL_PARTS = (4, 2, 4)
GROUP = ("x", "zl")
PROW_SIZE = 8


def matmul(left, right):
    return jnp.dot(left, right, precision=lax.Precision.HIGHEST, preferred_element_type=jnp.float32)


def all_reduce(packed, outer, inner, outer_size, inner_size):
    size = packed.shape[0]
    parts = outer_size * inner_size
    chunk = -(-size // parts)
    packed = jnp.pad(packed, (0, chunk * parts - size)).reshape(outer_size, inner_size * chunk)
    total = jnp.sum(lax.all_to_all(packed, outer, 0, 0, tiled=True), axis=0).reshape(inner_size, chunk)
    total = jnp.sum(lax.all_to_all(total, inner, 0, 0, tiled=True), axis=0)
    total = lax.all_to_all(jnp.broadcast_to(total, (inner_size, chunk)), inner, 0, 0, tiled=True)
    total = jnp.broadcast_to(total.reshape(1, inner_size * chunk), (outer_size, inner_size * chunk))
    total = lax.all_to_all(total, outer, 0, 0, tiled=True)
    return total.reshape(-1)[:size]


def per_device(slab, vectors, tfactors):
    rows, cols = slab.shape
    count = tfactors.shape[0]
    width = tfactors.shape[1]
    ng = PCOL_PARTS[0] * PCOL_PARTS[1]
    nprow = PROW_SIZE

    basis = lax.all_gather(vectors, "y", axis=0, tiled=True)
    work = lax.all_to_all(slab, GROUP, 1, 0, tiled=True)

    products = matmul(work, basis)
    gram = matmul(basis[:, width:].T, basis[:, : (count - 1) * width])
    packed = jnp.concatenate([products.reshape(-1), gram.reshape(-1)])
    packed = all_reduce(packed, GROUP, "prow", ng, nprow)
    products = packed[: products.size].reshape(products.shape)
    gram = packed[products.size :].reshape(gram.shape)

    scaled = [None] * count
    for k in reversed(range(count)):
        part = products[:, k * width : (k + 1) * width]
        for j in range(k + 1, count):
            block = gram[(j - 1) * width : j * width, k * width : (k + 1) * width]
            part = part - matmul(scaled[j], block)
        scaled[k] = matmul(part, tfactors[k].T)
    scaled = jnp.concatenate(scaled, axis=1)

    work = work - matmul(scaled, basis.T)
    return lax.all_to_all(work, GROUP, 0, 1, tiled=True)


def solution(mesh):
    devices = mesh.devices.reshape((mesh.shape["prow"],) + PCOL_PARTS)
    fine = Mesh(devices, ("prow", "x", "zl", "y"))
    cols = ("x", "zl", "y")
    in_specs = (P(cols, "prow"), P(("prow",) + cols, None), P())
    out_specs = P(cols, "prow")
    return jax.shard_map(per_device, mesh=fine, in_specs=in_specs, out_specs=out_specs, check_vma=False)
```

time: 593 us -> 252 us (0.42)
  waiting for transfers between devices: 475 us -> 46.6 us
  blocking collectives: 43.8 us -> 119 us
  other arithmetic: 0 us -> 9.37 us
    psum x2 -> x0, waiting for transfers between devices: 432 us -> none  [the longest x1 255 us: per_device(): lax.psum(matmul(vectors[:, width:].T, vectors[:, :(count - 1) * width]),...]
    all_to_all x1 -> x5, blocking collectives: 43.8 us -> 119 us  [the longest x1 38.9 us: per_device(): return lax.all_to_all(work, GROUP, 0, 1, tiled=True)]
    all_gather x1, waiting for transfers between devices: 5.36 us -> 45.9 us  [per_device(): basis = lax.all_gather(vectors, 'y', axis=0, tiled=True)]
    all_to_all x1, waiting for transfers between devices: 36.5 us -> 0.01 us  [per_device(): work = lax.all_to_all(slab, GROUP, 1, 0, tiled=True)]
    unnamed x9, local copies, waits for them, and re-layouts: 9.68 us -> 1.45 us
    all_to_all x0 -> x1, other arithmetic: none -> 6.49 us  [all_reduce(): total = lax.all_to_all(total, outer, 0, 0, tiled=True)]
  transfers between devices with their start and end apart: 4 -> 2, of which waited for: 4 -> 1; matrix products, arithmetic and copies ran while one was open for 1% -> 4% of each run, Pallas kernels for 0% -> 0%
where the time goes in v2:
time: 252 us; the launch traced here: 248 us
  blocking collectives  119 us (47%)
  waiting for transfers between devices  46.6 us (18%)
  matrix products  38.4 us (15%)
  local copies, waits for them, and re-layouts  16 us (6%)
  between operations  13.5 us (5%)
  other arithmetic  9.37 us (4%)
  starting transfers between devices  5.69 us (2%)
    all_gather x1, waiting for transfers between devices, per_device(): basis = lax.all_gather(vectors, 'y', axis=0, tiled=True)  45.9 us
    all_to_all x1, blocking collectives, per_device(): return lax.all_to_all(work, GROUP, 0, 1, tiled=True)  38.9 us
    dot_general x13, matrix products, matmul(): jnp.dot(left, right, precision=lax.Precision.HIGHEST, preferred_element_t...  38.4 us
    all_to_all x1, blocking collectives, all_reduce(): lax.all_to_all(packed, outer, 0, 0, tiled=True)  27.4 us
    all_to_all x1, blocking collectives, all_reduce(): total = lax.all_to_all(total, outer, 0, 0, tiled=True)  23.8 us
    all_to_all x1, blocking collectives, all_reduce(): total = jnp.sum(lax.all_to_all(total, inner, 0, 0, tiled=True), axis=0)  14.6 us
    all_to_all x1, blocking collectives, all_reduce(): lax.all_to_all(jnp.broadcast_to(total, (inner_size, chunk)), inner, 0, 0,...  14.2 us
    all_to_all x1, other arithmetic, all_reduce(): total = lax.all_to_all(total, outer, 0, 0, tiled=True)  6.49 us
  transfers between devices with their start and end apart: 2, of which 1 were waited for; matrix products, arithmetic and copies ran while one was open for 4% of the time, Pallas kernels for 0%

profile of v2, /device:TPU:64, one launch (start us, length us, event | category | flops | bytes accessed | tf_op | source)
XLA Modules:
  0.0 248.5 jit_solution(4912600759069833126)
XLA Ops:
  6.5 3.8 %copy.22 = f32[8,8,8,1536]{3,2,0,1:T(8,128)} copy(f32[8,8,8,1536]{3,2,1,0:T(8,128)} %bitcast.47) | data formatting | bytes 6291456 | tf_op jit(solution)/shard_map/all_to_all | solution.py:37
  10.4 5.7 %all-to-all-start = ((f32[64,8,1536]{2,0,1:T(8,128)}), f32[64,8,1536]{2,0,1:T(8,128)}, u32[]{:S(2)}, u32[]{:S(2)}) async-start(f32[64,8,1536]{2,0,1:T(8,128)} %bitcast.41), calls=%async_computation | async-start | bytes 6291456 | tf_op jit(solution)/shard_map/all_to_all | solution.py:37
  16.0 0.0 all-gather.2.cloned.1.call-start
  16.1 0.7 all-gather.2.cloned.1.call-update
  16.7 45.9 %all-gather.2.cloned.1.call-done = f32[1536,512]{1,0:T(8,128)} async-done(((f32[384,512]{1,0:T(8,128)}), f32[1536,512]{1,0:T(8,128)}) %all-gather.2.cloned.1.call-update) | async-done | bytes 3145744 | tf_op jit(solution)/shard_map/all_gather | solution.py:36
  62.7 0.0 copy-start
  62.7 7.2 %fusion = f32[384,384]{1,0:T(8,128)} fusion(f32[1536,512]{1,0:T(8,128)} %all-gather.2.cloned.1.call-done), kind=kOutput, calls=%fused_computation.2 | convolution fusion | flops 2717908992 | bytes 5308416 | tf_op jit(solution)/shard_map/dot_general | solution.py:13
  69.9 1.9 reshape.45
  71.8 0.0 all-to-all-done
  71.8 0.0 copy-done
  71.8 0.0 copy-start.2
  71.8 7.1 %convolution_bitcast_fusion = f32[64,4,8,128]{3,2,1,0:T(8,128)S(1)} fusion(f32[512,1536]{1,0:T(8,128)} %bitcast.1, f32[1536,512]{1,0:T(8,128)S(1)} %copy-done), kind=kOutput, calls=%fused_computation.6 | convolution fusion | flops 4831838208 | bytes 7340032 | tf_op jit(solution)/shard_map/dot_general | solution.py:13
  79.0 0.3 copy.20
  79.2 0.0 copy-done.2
  79.2 0.1 pad_maximum_fusion
  79.4 27.4 %all_to_all.68 = f32[8,1,51200]{2,1,0:T(1,128)} all-to-all(f32[8,1,51200]{2,1,0:T(1,128)S(1)} %bitcast.45), channel_id=1, replica_groups=mesh['prow'=8,'x'=4,'zl'=2,'y'=4] {'x','zl'}, dimensions={0} | all-to-all | bytes 3276800 | tf_op jit(solution)/shard_map/all_to_all | solution.py:21
  106.8 2.6 %reduce_sum.18 = f32[51200]{0:T(1024)S(1)} reduce(f32[8,1,51200]{2,1,0:T(1,128)} %all_to_all.68, f32[]{:T(128)} %constant.1.clone.1), dimensions={0,1}, to_apply=%region_0.1 | reduce | flops 358400 | bytes 1843204 | tf_op jit(solution)/shard_map/reduce_sum | solution.py:21
  109.4 14.6 %all_to_all.69 = f32[8,1,6400]{2,1,0:T(1,128)S(1)} all-to-all(f32[8,1,6400]{2,1,0:T(1,128)S(1)} %bitcast.49), channel_id=1, replica_groups=mesh['prow'=8,'x'=4,'zl'=2,'y'=4] {'prow'}, dimensions={0} | all-to-all | bytes 409600 | tf_op jit(solution)/shard_map/all_to_all | solution.py:22
  124.0 0.2 reduce_sum.19
  124.2 0.1 broadcast_in_dim.10
  124.3 14.2 %all_to_all.70 = f32[8,1,6400]{2,1,0:T(1,128)S(1)} all-to-all(f32[8,1,6400]{2,1,0:T(1,128)S(1)} %broadcast_in_dim.10), channel_id=1, replica_groups=mesh['prow'=8,'x'=4,'zl'=2,'y'=4] {'prow'}, dimensions={0} | all-to-all | bytes 409600 | tf_op jit(solution)/shard_map/all_to_all | solution.py:23
  138.5 0.8 broadcast_in_dim.12
  139.3 23.8 %all_to_all.71 = f32[8,1,51200]{2,1,0:T(1,128)S(1)} all-to-all(f32[8,1,51200]{2,1,0:T(1,128)S(1)} %broadcast_in_dim.12), channel_id=1, replica_groups=mesh['prow'=8,'x'=4,'zl'=2,'y'=4] {'x','zl'}, dimensions={0} | all-to-all | bytes 3276800 | tf_op jit(solution)/shard_map/all_to_all | solution.py:25
  163.1 0.0 copy-start.1
  163.1 1.2 copy-done.1
  164.3 0.8 slice.83
  165.1 2.0 reshape.47
  167.1 0.0 copy-start.3
  167.1 6.5 %reduce.2 = f32[8,51200]{1,0:T(8,128)} reduce(f32[8,1,51200]{2,1,0:T(1,128)} %copy-done.1, f32[]{:T(128)} %constant.4), dimensions={1}, to_apply=%all_to_all.57.reduce_sub_computation | reduce | bytes 3276804 | tf_op jit(solution)/shard_map/all_to_all | solution.py:25
  173.6 3.0 %slice.61 = f32[800,512]{1,0:T(8,128)} reshape(f32[8,51200]{1,0:T(8,128)} %reduce.2) | data formatting | bytes 3276800 | tf_op jit(solution)/shard_map/slice | solution.py:43
  176.7 0.0 copy-done.3
  176.7 1.3 fusion.10
  178.0 1.6 convolution_subtract_fusion.6
  179.6 0.4 fusion.22
  180.0 1.6 convolution_subtract_fusion.5
  181.6 1.4 convolution_subtract_fusion.4
  183.0 0.4 fusion.20
  183.4 1.6 convolution_subtract_fusion.3
  185.0 1.4 convolution_subtract_fusion.2
  186.5 1.4 convolution_subtract_fusion.1
  187.9 0.4 fusion.18
  188.3 12.5 %convolution_subtract_fusion = f32[512,1536]{1,0:T(8,128)S(1)} fusion(f32[512,1536]{1,0:T(8,128)} %bitcast.1, f32[1536,512]{1,0:T(8,128)S(1)} %copy-done, f32[512,128]{0,1:T(8,128)S(1)} %fusion.10, f32[512,128]{0,1:T(8,128)S(1)} %fusion.22, f32[512,128]{0,1:T(8,128)S(1)} %fusion.20, f32[512,128]{0,1:T(8,128)S(1)} %fusion.18), kind=kOutput, calls=%fused_computation | convolution fusion | flops 4833411072 | bytes 10485760 | tf_op jit(solution)/shard_map/dot_general | solution.py:13
  200.8 38.9 %all_to_all.72 = f32[8,64,1536]{2,1,0:T(8,128)S(1)} all-to-all(f32[8,64,1536]{2,1,0:T(8,128)S(1)} %bitcast.43), channel_id=1, replica_groups=mesh['prow'=8,'x'=4,'zl'=2,'y'=4] {'x','zl'}, dimensions={0} | all-to-all | bytes 6291456 | tf_op jit(solution)/shard_map/all_to_all | solution.py:56
  239.7 1.9 copy.19
Async XLA Ops:
  10.4 61.5 %all-to-all-start = ((f32[64,8,1536]{2,0,1:T(8,128)}), f32[64,8,1536]{2,0,1:T(8,128)}, u32[]{:S(2)}, u32[]{:S(2)}) async-start(f32[64,8,1536]{2,0,1:T(8,128)} %bitcast.41), calls=%async_computation | async-start | bytes 6291456 | tf_op jit(solution)/shard_map/all_to_all | solution.py:37
  16.0 46.6 %all-gather.2.cloned.1.call-start = ((), (), s32[]{:S(2)}) async-start(), calls=%async_computation.6 | async-start | bytes 3932160 | tf_op jit(solution)/shard_map/all_gather | solution.py:36
  62.7 9.2 %copy-start = (f32[1536,512]{1,0:T(8,128)S(1)}, f32[1536,512]{1,0:T(8,128)}, u32[]{:S(2)}) copy-start(f32[1536,512]{1,0:T(8,128)} %all-gather.2.cloned.1.call-done) | copy-start | bytes 9437188
  71.8 7.4 %copy-start.2 = (f32[147456]{0:T(1024)S(1)}, f32[147456]{0:T(1024)}, u32[]{:S(2)}) copy-start(f32[147456]{0:T(1024)} %reshape.45) | copy-start | bytes 1769476
  163.1 1.2 copy-start.1
  167.1 9.5 %copy-start.3 = (f32[4,128,128]{2,1,0:T(8,128)S(1)}, f32[4,128,128]{2,1,0:T(8,128)}, u32[]{:S(2)}) copy-start(f32[4,128,128]{2,1,0:T(8,128)} %param.5) | copy-start | bytes 786436
Sparse Core Ops, SparseCore 0:
  18.7 43.9 all-gather.1

commit v3 on v2

--- a/solution.py
+++ b/solution.py
@@ -10,7 +10,7 @@
 
 
 def matmul(left, right):
-    return jnp.dot(left, right, precision=lax.Precision.HIGHEST, preferred_element_type=jnp.float32)
+    return jnp.dot(left, right, precision=lax.Precision.HIGH, preferred_element_type=jnp.float32)
 
 
 def all_reduce(packed, outer, inner, outer_size, inner_size):
@@ -37,17 +37,19 @@
     work = lax.all_to_all(slab, GROUP, 1, 0, tiled=True)
 
     products = matmul(work, basis)
-    gram = matmul(basis[:, width:].T, basis[:, : (count - 1) * width])
-    packed = jnp.concatenate([products.reshape(-1), gram.reshape(-1)])
+    grams = [matmul(basis[:, j * width : (j + 1) * width].T, basis[:, : j * width]) for j in range(1, count)]
+    packed = jnp.concatenate([products.reshape(-1)] + [g.reshape(-1) for g in grams])
     packed = all_reduce(packed, GROUP, "prow", ng, nprow)
-    products = packed[: products.size].reshape(products.shape)
-    gram = packed[products.size :].reshape(gram.shape)
+    products, offset = packed[: products.size].reshape(products.shape), products.size
+    for j in range(1, count):
+        size = grams[j - 1].size
+        grams[j - 1], offset = packed[offset : offset + size].reshape(grams[j - 1].shape), offset + size
 
     scaled = [None] * count
     for k in reversed(range(count)):
         part = products[:, k * width : (k + 1) * width]
         for j in range(k + 1, count):
-            block = gram[(j - 1) * width : j * width, k * width : (k + 1) * width]
+            block = grams[j - 1][:, k * width : (k + 1) * width]
             part = part - matmul(scaled[j], block)
         scaled[k] = matmul(part, tfactors[k].T)
     scaled = jnp.concatenate(scaled, axis=1)

time: 252 us -> 231 us (0.917)
  matrix products: 38.4 us -> 27 us
  blocking collectives: 119 us -> 114 us
    dot_general x13 -> x15, matrix products: 38.4 us -> 27 us  [matmul(): jnp.dot(left, right, precision=lax.Precision.HIGH, preferred_element_type...]
    reshape x2, local copies, waits for them, and re-layouts: 3.94 us -> 0.06 us  [the longest x1 0.05 us: per_device(): packed[offset:offset + size].reshape(grams[j - 1].shape)]
    slice x2 -> x3, local copies, waits for them, and re-layouts: 3.9 us -> 6.42 us  [the longest x2 3.65 us: per_device(): packed[offset:offset + size].reshape(grams[j - 1].shape)]
  transfers between devices with their start and end apart: 2 -> 2, of which waited for: 1 -> 1; matrix products, arithmetic and copies ran while one was open for 4% -> 3% of each run, Pallas kernels for 0% -> 0%
where the time goes in v3:
time: 231 us; the launch traced here: 229 us
  blocking collectives  114 us (49%)
  waiting for transfers between devices  46.6 us (20%)
  matrix products  27 us (12%)
  local copies, waits for them, and re-layouts  14 us (6%)
  between operations  13.6 us (6%)
  other arithmetic  8.53 us (4%)
  starting transfers between devices  5.69 us (2%)
    all_gather x1, waiting for transfers between devices, per_device(): basis = lax.all_gather(vectors, 'y', axis=0, tiled=True)  45.9 us
    all_to_all x1, blocking collectives, per_device(): return lax.all_to_all(work, GROUP, 0, 1, tiled=True)  38.7 us
    dot_general x15, matrix products, matmul(): jnp.dot(left, right, precision=lax.Precision.HIGH, preferred_element_type...  27 us
    all_to_all x1, blocking collectives, all_reduce(): lax.all_to_all(packed, outer, 0, 0, tiled=True)  25.2 us
    all_to_all x1, blocking collectives, all_reduce(): total = lax.all_to_all(total, outer, 0, 0, tiled=True)  22.1 us
    all_to_all x1, blocking collectives, all_reduce(): total = jnp.sum(lax.all_to_all(total, inner, 0, 0, tiled=True), axis=0)  14.1 us
    all_to_all x1, blocking collectives, all_reduce(): lax.all_to_all(jnp.broadcast_to(total, (inner_size, chunk)), inner, 0, 0,...  13.7 us
    all_to_all x1, other arithmetic, all_reduce(): total = lax.all_to_all(total, outer, 0, 0, tiled=True)  5.89 us
  transfers between devices with their start and end apart: 2, of which 1 were waited for; matrix products, arithmetic and copies ran while one was open for 3% of the time, Pallas kernels for 0%

profile of v3, /device:TPU:64, one launch (start us, length us, event | category | flops | bytes accessed | tf_op | source)
XLA Modules:
  0.0 229.3 jit_solution(17273348831804631790)
XLA Ops:
  6.5 3.8 %copy.23 = f32[8,8,8,1536]{3,2,0,1:T(8,128)} copy(f32[8,8,8,1536]{3,2,1,0:T(8,128)} %bitcast.54) | data formatting | bytes 6291456 | tf_op jit(solution)/shard_map/all_to_all | solution.py:37
  10.4 5.7 %all-to-all-start = ((f32[64,8,1536]{2,0,1:T(8,128)}), f32[64,8,1536]{2,0,1:T(8,128)}, u32[]{:S(2)}, u32[]{:S(2)}) async-start(f32[64,8,1536]{2,0,1:T(8,128)} %bitcast.47), calls=%async_computation | async-start | bytes 6291456 | tf_op jit(solution)/shard_map/all_to_all | solution.py:37
  16.0 0.0 all-gather.2.cloned.1.call-start
  16.1 0.7 all-gather.2.cloned.1.call-update
  16.7 45.9 %all-gather.2.cloned.1.call-done = f32[1536,512]{1,0:T(8,128)} async-done(((f32[384,512]{1,0:T(8,128)}), f32[1536,512]{1,0:T(8,128)}) %all-gather.2.cloned.1.call-update) | async-done | bytes 3145744 | tf_op jit(solution)/shard_map/all_gather | solution.py:36
  62.7 2.5 %fusion.4 = f32[16,2,8,128]{3,2,1,0:T(8,128)S(1)} fusion(f32[1536,512]{1,0:T(8,128)} %all-gather.2.cloned.1.call-done), kind=kOutput, calls=%fused_computation.15 | convolution fusion | flops 301989888 | bytes 2490368 | tf_op jit(solution)/shard_map/dot_general | solution.py:13
  65.1 0.0 copy-start
  65.1 0.7 copy.21
  65.9 3.1 %fusion = f32[128,384]{1,0:T(8,128)S(1)} fusion(f32[1536,512]{1,0:T(8,128)} %all-gather.2.cloned.1.call-done), kind=kOutput, calls=%fused_computation.2 | convolution fusion | flops 452984832 | bytes 3342336 | tf_op jit(solution)/shard_map/dot_general | solution.py:13
  69.0 0.0 copy-done
  69.0 0.8 convolution_bitcast_fusion
  69.8 0.0 all-to-all-done
  69.8 0.0 copy-start.1
  69.8 4.6 %convolution_bitcast_fusion.1 = f32[64,4,8,128]{3,2,1,0:T(8,128)S(1)} fusion(f32[512,1536]{1,0:T(8,128)} %bitcast.1, f32[1536,512]{1,0:T(8,128)S(1)} %copy-done), kind=kOutput, calls=%fused_computation.8 | convolution fusion | flops 2415919104 | bytes 7340032 | tf_op jit(solution)/shard_map/dot_general | solution.py:13
  74.4 0.3 copy.20
  74.7 0.0 copy-done.1
  74.7 0.1 pad_maximum_fusion
  74.8 25.2 %all_to_all.68 = f32[8,1,45056]{2,1,0:T(1,128)} all-to-all(f32[8,1,45056]{2,1,0:T(1,128)S(1)} %bitcast.52), channel_id=1, replica_groups=mesh['prow'=8,'x'=4,'zl'=2,'y'=4] {'x','zl'}, dimensions={0} | all-to-all | bytes 2883584 | tf_op jit(solution)/shard_map/all_to_all | solution.py:21
  100.0 2.4 %reduce_sum.18 = f32[45056]{0:T(1024)S(1)} reduce(f32[8,1,45056]{2,1,0:T(1,128)} %all_to_all.68, f32[]{:T(128)} %constant.1.clone.1), dimensions={0,1}, to_apply=%region_0.1 | reduce | flops 315392 | bytes 1622020 | tf_op jit(solution)/shard_map/reduce_sum | solution.py:21
  102.5 14.1 %all_to_all.69 = f32[8,1,5632]{2,1,0:T(1,128)S(1)} all-to-all(f32[8,1,5632]{2,1,0:T(1,128)S(1)} %bitcast.55), channel_id=1, replica_groups=mesh['prow'=8,'x'=4,'zl'=2,'y'=4] {'prow'}, dimensions={0} | all-to-all | bytes 360448 | tf_op jit(solution)/shard_map/all_to_all | solution.py:22
  116.6 0.1 reduce_sum.19
  116.7 0.1 broadcast_in_dim.10
  116.8 13.7 %all_to_all.70 = f32[8,1,5632]{2,1,0:T(1,128)S(1)} all-to-all(f32[8,1,5632]{2,1,0:T(1,128)S(1)} %broadcast_in_dim.10), channel_id=1, replica_groups=mesh['prow'=8,'x'=4,'zl'=2,'y'=4] {'prow'}, dimensions={0} | all-to-all | bytes 360448 | tf_op jit(solution)/shard_map/all_to_all | solution.py:23
  130.5 0.7 broadcast_in_dim.12
  131.2 22.1 %all_to_all.71 = f32[8,1,45056]{2,1,0:T(1,128)} all-to-all(f32[8,1,45056]{2,1,0:T(1,128)S(1)} %broadcast_in_dim.12), channel_id=1, replica_groups=mesh['prow'=8,'x'=4,'zl'=2,'y'=4] {'x','zl'}, dimensions={0} | all-to-all | bytes 2883584 | tf_op jit(solution)/shard_map/all_to_all | solution.py:25
  153.3 5.9 %reduce.2 = f32[8,45056]{1,0:T(8,128)} reduce(f32[8,1,45056]{2,1,0:T(1,128)} %all_to_all.71, f32[]{:T(128)} %constant.4), dimensions={1}, to_apply=%all_to_all.57.reduce_sub_computation | reduce | bytes 2883588 | tf_op jit(solution)/shard_map/all_to_all | solution.py:25
  159.2 2.8 %slice.86 = f32[704,512]{1,0:T(8,128)} reshape(f32[8,45056]{1,0:T(8,128)} %reduce.2) | data formatting | bytes 2883584 | tf_op jit(solution)/shard_map/slice | solution.py:43
  162.0 2.7 %slice.95 = f32[1408,256]{1,0:T(8,128)} reshape(f32[8,45056]{1,0:T(8,128)} %reduce.2) | data formatting | bytes 2883584 | tf_op jit(solution)/shard_map/slice | solution.py:46
  164.7 0.9 slice.114
  165.7 0.0 copy-start.2
  165.7 1.3 fusion.18
  167.0 1.3 convolution_subtract_fusion.6
  168.4 1.1 fusion.30
  169.5 1.4 convolution_subtract_fusion.5
  170.9 0.4 convolution_subtract_fusion.4
  171.3 0.0 copy-done.2
  171.3 0.3 fusion.28
  171.6 1.4 convolution_subtract_fusion.3
  172.9 1.2 convolution_subtract_fusion.2
  174.2 0.4 convolution_subtract_fusion.1
  174.6 0.3 fusion.26
  174.9 7.0 %convolution_subtract_fusion = f32[512,1536]{1,0:T(8,128)S(1)} fusion(f32[512,1536]{1,0:T(8,128)} %bitcast.1, f32[1536,512]{1,0:T(8,128)S(1)} %copy-done, f32[512,128]{0,1:T(8,128)S(1)} %fusion.18, f32[512,128]{0,1:T(8,128)S(1)} %fusion.30, f32[512,128]{0,1:T(8,128)S(1)} %fusion.28, f32[512,128]{0,1:T(8,128)S(1)} %fusion.26), kind=kOutput, calls=%fused_computation | convolution fusion | flops 2417491968 | bytes 10485760 | tf_op jit(solution)/shard_map/dot_general | solution.py:13
  181.9 38.7 %all_to_all.72 = f32[8,64,1536]{2,1,0:T(8,128)S(1)} all-to-all(f32[8,64,1536]{2,1,0:T(8,128)S(1)} %bitcast.49), channel_id=1, replica_groups=mesh['prow'=8,'x'=4,'zl'=2,'y'=4] {'x','zl'}, dimensions={0} | all-to-all | bytes 6291456 | tf_op jit(solution)/shard_map/all_to_all | solution.py:58
  220.5 1.9 copy.19
  (2 shorter events, 0.1 us)
Async XLA Ops:
  10.4 59.4 %all-to-all-start = ((f32[64,8,1536]{2,0,1:T(8,128)}), f32[64,8,1536]{2,0,1:T(8,128)}, u32[]{:S(2)}, u32[]{:S(2)}) async-start(f32[64,8,1536]{2,0,1:T(8,128)} %bitcast.47), calls=%async_computation | async-start | bytes 6291456 | tf_op jit(solution)/shard_map/all_to_all | solution.py:37
  16.0 46.6 %all-gather.2.cloned.1.call-start = ((), (), s32[]{:S(2)}) async-start(), calls=%async_computation.6 | async-start | bytes 3932160 | tf_op jit(solution)/shard_map/all_gather | solution.py:36
  65.1 3.8 %copy-start = (f32[1536,512]{1,0:T(8,128)S(1)}, f32[1536,512]{1,0:T(8,128)}, u32[]{:S(2)}) copy-start(f32[1536,512]{1,0:T(8,128)} %all-gather.2.cloned.1.call-done) | copy-start | bytes 9437188
  69.8 4.9 %copy-start.1 = (f32[16,2,8,128]{3,1,2,0:T(2,128)S(1)}, f32[16,2,8,128]{3,1,2,0:T(2,128)}, u32[]{:S(2)}) copy-start(f32[16,2,8,128]{3,1,2,0:T(2,128)} %copy.21) | copy-start | bytes 393220
  165.7 5.6 %copy-start.2 = (f32[4,128,128]{2,1,0:T(8,128)S(1)}, f32[4,128,128]{2,1,0:T(8,128)}, u32[]{:S(2)}) copy-start(f32[4,128,128]{2,1,0:T(8,128)} %param.5) | copy-start | bytes 786436
Sparse Core Ops, SparseCore 0:
  18.7 43.9 all-gather.1

commit v4 on v3

--- a/solution.py
+++ b/solution.py
@@ -15,14 +15,14 @@
 
 def all_reduce(packed, outer, inner, outer_size, inner_size):
     size = packed.shape[0]
-    parts = outer_size * inner_size
-    chunk = -(-size // parts)
-    packed = jnp.pad(packed, (0, chunk * parts - size)).reshape(outer_size, inner_size * chunk)
-    total = jnp.sum(lax.all_to_all(packed, outer, 0, 0, tiled=True), axis=0).reshape(inner_size, chunk)
-    total = jnp.sum(lax.all_to_all(total, inner, 0, 0, tiled=True), axis=0)
-    total = lax.all_to_all(jnp.broadcast_to(total, (inner_size, chunk)), inner, 0, 0, tiled=True)
-    total = jnp.broadcast_to(total.reshape(1, inner_size * chunk), (outer_size, inner_size * chunk))
-    total = lax.all_to_all(total, outer, 0, 0, tiled=True)
+    chunk = -(-size // outer_size)
+    packed = jnp.pad(packed, (0, chunk * outer_size - size)).reshape(outer_size, chunk)
+    total = jnp.sum(lax.all_to_all(packed, outer, 0, 0, tiled=True), axis=0)
+    bit = 1
+    while bit < inner_size:
+        total = total + lax.ppermute(total, inner, [(i, i ^ bit) for i in range(inner_size)])
+        bit *= 2
+    total = lax.all_to_all(jnp.broadcast_to(total, (outer_size, chunk)), outer, 0, 0, tiled=True)
     return total.reshape(-1)[:size]
 
 

time: 231 us -> 230 us (level)
  blocking collectives: 114 us -> 92.3 us
  waiting for transfers between devices: 46.6 us -> 63.1 us
  starting transfers between devices: 5.69 us -> 11.2 us
    all_to_all x4 -> x2, blocking collectives: 75.1 us -> 52.4 us  [the longest x1 27.2 us: all_reduce(): lax.all_to_all(jnp.broadcast_to(total, (outer_size, chunk)), outer, 0, 0,...]
    ppermute x0 -> x3, waiting for transfers between devices: none -> 16.5 us  [all_reduce(): lax.ppermute(total, inner, [(i, i ^ bit) for i in range(inner_size)])]
    ppermute x0 -> x3, starting transfers between devices: none -> 5.49 us  [all_reduce(): lax.ppermute(total, inner, [(i, i ^ bit) for i in range(inner_size)])]
  transfers between devices with their start and end apart: 2 -> 5, of which waited for: 1 -> 4; matrix products, arithmetic and copies ran while one was open for 3% -> 3% of each run, Pallas kernels for 0% -> 0%
where the time goes in v4:
time: 230 us
  blocking collectives  92.3 us (40%)
  waiting for transfers between devices  63.1 us (27%)
  matrix products  27 us (12%)
  local copies, waits for them, and re-layouts  14 us (6%)
  between operations  13.6 us (6%)
  starting transfers between devices  11.2 us (5%)
  other arithmetic  8.46 us (4%)
    all_gather x1, waiting for transfers between devices, per_device(): basis = lax.all_gather(vectors, 'y', axis=0, tiled=True)  45.9 us
    all_to_all x1, blocking collectives, per_device(): return lax.all_to_all(work, GROUP, 0, 1, tiled=True)  39.9 us
    all_to_all x1, blocking collectives, all_reduce(): lax.all_to_all(jnp.broadcast_to(total, (outer_size, chunk)), outer, 0, 0,...  27.2 us
    dot_general x15, matrix products, matmul(): jnp.dot(left, right, precision=lax.Precision.HIGH, preferred_element_type...  27 us
    all_to_all x1, blocking collectives, all_reduce(): total = jnp.sum(lax.all_to_all(packed, outer, 0, 0, tiled=True), axis=0)  25.2 us
    ppermute x3, waiting for transfers between devices, all_reduce(): lax.ppermute(total, inner, [(i, i ^ bit) for i in range(inner_size)])  16.5 us
    all_to_all x1, other arithmetic, all_reduce(): lax.all_to_all(jnp.broadcast_to(total, (outer_size, chunk)), outer, 0, 0,...  5.89 us
    all_to_all x1, starting transfers between devices, per_device(): work = lax.all_to_all(slab, GROUP, 1, 0, tiled=True)  5.65 us
  transfers between devices with their start and end apart: 5, of which 4 were waited for; matrix products, arithmetic and copies ran while one was open for 3% of the time, Pallas kernels for 0%

profile of v4, /device:TPU:64, one launch (start us, length us, event | category | flops | bytes accessed | tf_op | source)
XLA Modules:
  0.0 229.7 jit_solution(15131078966655906689)
XLA Ops:
  6.5 3.8 %copy.20 = f32[8,8,8,1536]{3,2,0,1:T(8,128)} copy(f32[8,8,8,1536]{3,2,1,0:T(8,128)} %bitcast.52) | data formatting | bytes 6291456 | tf_op jit(solution)/shard_map/all_to_all | solution.py:37
  10.4 5.7 %all-to-all-start = ((f32[64,8,1536]{2,0,1:T(8,128)}), f32[64,8,1536]{2,0,1:T(8,128)}, u32[]{:S(2)}, u32[]{:S(2)}) async-start(f32[64,8,1536]{2,0,1:T(8,128)} %bitcast.45), calls=%async_computation | async-start | bytes 6291456 | tf_op jit(solution)/shard_map/all_to_all | solution.py:37
  16.0 0.0 all-gather.2.cloned.1.call-start
  16.1 0.7 all-gather.2.cloned.1.call-update
  16.7 45.9 %all-gather.2.cloned.1.call-done = f32[1536,512]{1,0:T(8,128)} async-done(((f32[384,512]{1,0:T(8,128)}), f32[1536,512]{1,0:T(8,128)}) %all-gather.2.cloned.1.call-update) | async-done | bytes 3145744 | tf_op jit(solution)/shard_map/all_gather | solution.py:36
  62.7 2.5 %fusion.4 = f32[16,2,8,128]{3,2,1,0:T(8,128)S(1)} fusion(f32[1536,512]{1,0:T(8,128)} %all-gather.2.cloned.1.call-done), kind=kOutput, calls=%fused_computation.15 | convolution fusion | flops 301989888 | bytes 2490368 | tf_op jit(solution)/shard_map/dot_general | solution.py:13
  65.1 0.0 copy-start
  65.1 0.7 copy.18
  65.9 3.1 %fusion = f32[128,384]{1,0:T(8,128)S(1)} fusion(f32[1536,512]{1,0:T(8,128)} %all-gather.2.cloned.1.call-done), kind=kOutput, calls=%fused_computation.2 | convolution fusion | flops 452984832 | bytes 3342336 | tf_op jit(solution)/shard_map/dot_general | solution.py:13
  69.0 0.0 copy-done
  69.0 0.8 convolution_bitcast_fusion
  69.8 0.0 all-to-all-done
  69.8 0.0 copy-start.1
  69.8 4.6 %convolution_bitcast_fusion.1 = f32[64,4,8,128]{3,2,1,0:T(8,128)S(1)} fusion(f32[512,1536]{1,0:T(8,128)} %bitcast.1, f32[1536,512]{1,0:T(8,128)S(1)} %copy-done), kind=kOutput, calls=%fused_computation.8 | convolution fusion | flops 2415919104 | bytes 7340032 | tf_op jit(solution)/shard_map/dot_general | solution.py:13
  74.4 0.3 copy.17
  74.7 0.0 copy-done.1
  74.7 0.1 pad_maximum_fusion
  74.8 25.2 %all_to_all.53 = f32[8,1,45056]{2,1,0:T(1,128)} all-to-all(f32[8,1,45056]{2,1,0:T(1,128)S(1)} %bitcast.50), channel_id=1, replica_groups=mesh['prow'=8,'x'=4,'zl'=2,'y'=4] {'x','zl'}, dimensions={0} | all-to-all | bytes 2883584 | tf_op jit(solution)/shard_map/all_to_all | solution.py:20
  100.0 2.4 %reduce_sum.9 = f32[45056]{0:T(1024)S(1)} reduce(f32[8,1,45056]{2,1,0:T(1,128)} %all_to_all.53, f32[]{:T(128)} %constant.1.clone.1), dimensions={0,1}, to_apply=%region_0.1 | reduce | flops 315392 | bytes 1622020 | tf_op jit(solution)/shard_map/reduce_sum | solution.py:20
  102.5 0.1 collective-permute-start
  102.6 1.4 collective-permute-done
  104.0 0.5 collective-permute-start.1
  104.5 8.0 %collective-permute-done.1 = f32[45056]{0:T(1024)S(1)} collective-permute-done((f32[45056]{0:T(1024)S(1)}, f32[45056]{0:T(1024)S(1)}, u32[]{:S(2)}, u32[]{:S(2)}) %collective-permute-start.1) | collective-permute-done | bytes 180256 | tf_op jit(solution)/shard_map/ppermute | solution.py:23
  112.5 4.9 %collective-permute-start.2 = (f32[45056]{0:T(1024)S(1)}, f32[45056]{0:T(1024)S(1)}, u32[]{:S(2)}, u32[]{:S(2)}) collective-permute-start(f32[45056]{0:T(1024)S(1)} %add.10), channel_id=1, source_target_pairs={{0,128},{32,160},{64,192},{96,224},{128,0},{160,32},{192,64},{224,... | collective-permute-start | bytes 540680 | tf_op jit(solution)/shard_map/ppermute | solution.py:23
  117.4 7.1 %collective-permute-done.2 = f32[45056]{0:T(1024)S(1)} collective-permute-done((f32[45056]{0:T(1024)S(1)}, f32[45056]{0:T(1024)S(1)}, u32[]{:S(2)}, u32[]{:S(2)}) %collective-permute-start.2) | collective-permute-done | bytes 180256 | tf_op jit(solution)/shard_map/ppermute | solution.py:23
  124.6 0.7 broadcast_in_dim.3
  125.3 27.2 %all_to_all.54 = f32[8,1,45056]{2,1,0:T(1,128)} all-to-all(f32[8,1,45056]{2,1,0:T(1,128)S(1)} %broadcast_in_dim.3), channel_id=1, replica_groups=mesh['prow'=8,'x'=4,'zl'=2,'y'=4] {'x','zl'}, dimensions={0} | all-to-all | bytes 2883584 | tf_op jit(solution)/shard_map/all_to_all | solution.py:25
  152.5 5.9 %reduce.1 = f32[8,45056]{1,0:T(8,128)} reduce(f32[8,1,45056]{2,1,0:T(1,128)} %all_to_all.54, f32[]{:T(128)} %constant.4), dimensions={1}, to_apply=%all_to_all.44.reduce_sub_computation | reduce | bytes 2883588 | tf_op jit(solution)/shard_map/all_to_all | solution.py:25
  158.4 2.8 %slice.86 = f32[704,512]{1,0:T(8,128)} reshape(f32[8,45056]{1,0:T(8,128)} %reduce.1) | data formatting | bytes 2883584 | tf_op jit(solution)/shard_map/slice | solution.py:43
  161.2 2.7 %slice.95 = f32[1408,256]{1,0:T(8,128)} reshape(f32[8,45056]{1,0:T(8,128)} %reduce.1) | data formatting | bytes 2883584 | tf_op jit(solution)/shard_map/slice | solution.py:46
  163.9 0.9 slice.114
  164.9 0.0 copy-start.2
  164.9 1.3 fusion.18
  166.2 1.3 convolution_subtract_fusion.6
  167.5 1.1 fusion.30
  168.6 1.4 convolution_subtract_fusion.5
  170.0 0.4 convolution_subtract_fusion.4
  170.4 0.0 copy-done.2
  170.4 0.3 fusion.28
  170.7 1.4 convolution_subtract_fusion.3
  172.1 1.2 convolution_subtract_fusion.2
  173.3 0.4 convolution_subtract_fusion.1
  173.7 0.3 fusion.26
  174.0 7.0 %convolution_subtract_fusion = f32[512,1536]{1,0:T(8,128)S(1)} fusion(f32[512,1536]{1,0:T(8,128)} %bitcast.1, f32[1536,512]{1,0:T(8,128)S(1)} %copy-done, f32[512,128]{0,1:T(8,128)S(1)} %fusion.18, f32[512,128]{0,1:T(8,128)S(1)} %fusion.30, f32[512,128]{0,1:T(8,128)S(1)} %fusion.28, f32[512,128]{0,1:T(8,128)S(1)} %fusion.26), kind=kOutput, calls=%fused_computation | convolution fusion | flops 2417491968 | bytes 10485760 | tf_op jit(solution)/shard_map/dot_general | solution.py:13
  181.0 39.9 %all_to_all.55 = f32[8,64,1536]{2,1,0:T(8,128)S(1)} all-to-all(f32[8,64,1536]{2,1,0:T(8,128)S(1)} %bitcast.47), channel_id=1, replica_groups=mesh['prow'=8,'x'=4,'zl'=2,'y'=4] {'x','zl'}, dimensions={0} | all-to-all | bytes 6291456 | tf_op jit(solution)/shard_map/all_to_all | solution.py:58
  220.9 1.9 copy.16
  (5 shorter events, 0.1 us)
Async XLA Ops:
  10.4 59.4 %all-to-all-start = ((f32[64,8,1536]{2,0,1:T(8,128)}), f32[64,8,1536]{2,0,1:T(8,128)}, u32[]{:S(2)}, u32[]{:S(2)}) async-start(f32[64,8,1536]{2,0,1:T(8,128)} %bitcast.45), calls=%async_computation | async-start | bytes 6291456 | tf_op jit(solution)/shard_map/all_to_all | solution.py:37
  16.0 46.6 %all-gather.2.cloned.1.call-start = ((), (), s32[]{:S(2)}) async-start(), calls=%async_computation.4 | async-start | bytes 3932160 | tf_op jit(solution)/shard_map/all_gather | solution.py:36
  65.1 3.8 %copy-start = (f32[1536,512]{1,0:T(8,128)S(1)}, f32[1536,512]{1,0:T(8,128)}, u32[]{:S(2)}) copy-start(f32[1536,512]{1,0:T(8,128)} %all-gather.2.cloned.1.call-done) | copy-start | bytes 9437188
  69.8 4.9 %copy-start.1 = (f32[16,2,8,128]{3,1,2,0:T(2,128)S(1)}, f32[16,2,8,128]{3,1,2,0:T(2,128)}, u32[]{:S(2)}) copy-start(f32[16,2,8,128]{3,1,2,0:T(2,128)} %copy.18) | copy-start | bytes 393220
  102.5 1.5 collective-permute-start
  104.0 8.4 %collective-permute-start.1 = (f32[45056]{0:T(1024)S(1)}, f32[45056]{0:T(1024)S(1)}, u32[]{:S(2)}, u32[]{:S(2)}) collective-permute-start(f32[45056]{0:T(1024)S(1)} %add.9), channel_id=1, source_target_pairs={{0,64},{32,96},{64,0},{96,32},{128,192},{160,224},{192,128},{224,1... | collective-permute-start | bytes 540680 | tf_op jit(solution)/shard_map/ppermute | solution.py:23
  112.5 12.1 %collective-permute-start.2 = (f32[45056]{0:T(1024)S(1)}, f32[45056]{0:T(1024)S(1)}, u32[]{:S(2)}, u32[]{:S(2)}) collective-permute-start(f32[45056]{0:T(1024)S(1)} %add.10), channel_id=1, source_target_pairs={{0,128},{32,160},{64,192},{96,224},{128,0},{160,32},{192,64},{224,... | collective-permute-start | bytes 540680 | tf_op jit(solution)/shard_map/ppermute | solution.py:23
  164.9 5.6 %copy-start.2 = (f32[4,128,128]{2,1,0:T(8,128)S(1)}, f32[4,128,128]{2,1,0:T(8,128)}, u32[]{:S(2)}) copy-start(f32[4,128,128]{2,1,0:T(8,128)} %param.5) | copy-start | bytes 786436
Sparse Core Ops, SparseCore 0:
  18.7 43.9 all-gather.1

commit v5 on v4

--- a/solution.py
+++ b/solution.py
@@ -26,6 +26,20 @@
     return total.reshape(-1)[:size]
 
 
+def gather_ring(block, axis, size):
+    right = [(i, (i + 1) % size) for i in range(size)]
+    left = [(i, (i - 1) % size) for i in range(size)]
+    from_left = lax.ppermute(block, axis, right)
+    from_right = lax.ppermute(block, axis, left)
+    half = block.shape[0] // 2
+    far_first = lax.ppermute(from_left[:half], axis, right)
+    far_second = lax.ppermute(from_right[half:], axis, left)
+    ordered = jnp.concatenate([block, from_right, far_first, far_second, from_left], axis=0)
+    shift = lax.axis_index(axis) * block.shape[0]
+    ordered = jnp.concatenate([ordered, ordered], axis=0)
+    return lax.dynamic_slice_in_dim(ordered, (size * block.shape[0] - shift) % (size * block.shape[0]), size * block.shape[0], axis=0)
+
+
 def per_device(slab, vectors, tfactors):
     rows, cols = slab.shape
     count = tfactors.shape[0]
@@ -33,7 +47,7 @@
     ng = PCOL_PARTS[0] * PCOL_PARTS[1]
     nprow = PROW_SIZE
 
-    basis = lax.all_gather(vectors, "y", axis=0, tiled=True)
+    basis = gather_ring(vectors, "y", PCOL_PARTS[2])
     work = lax.all_to_all(slab, GROUP, 1, 0, tiled=True)
 
     products = matmul(work, basis)

time: 230 us -> 214 us (0.930); the launches traced: 230 us -> 211 us
  waiting for transfers between devices: 63.1 us -> 38.6 us
  local copies, waits for them, and re-layouts: 14 us -> 28 us
  between operations: 13.6 us -> 0.31 us
  starting transfers between devices: 11.2 us -> 18.1 us
  blocking collectives: 92.3 us -> 86.7 us
  matrix products: 27 us -> 30.4 us
    all_gather x1 -> x0, waiting for transfers between devices: 45.9 us -> none  [per_device(): basis = lax.all_gather(vectors, 'y', axis=0, tiled=True)]
    ppermute x0 -> x4, waiting for transfers between devices: none -> 21.9 us  [the longest x1 17.2 us: gather_ring(): from_left = lax.ppermute(block, axis, right)]
    unnamed x8 -> x25, local copies, waits for them, and re-layouts: 1 us -> 10.9 us
    ppermute x0 -> x4, starting transfers between devices: none -> 6.47 us  [the longest x1 2.93 us: gather_ring(): far_second = lax.ppermute(from_right[half:], axis, left)]
    dot_general x15, matrix products: 27 us -> 30.4 us  [matmul(): jnp.dot(left, right, precision=lax.Precision.HIGH, preferred_element_type...]
    all_to_all x1, blocking collectives: 25.2 us -> 22.4 us  [all_reduce(): total = jnp.sum(lax.all_to_all(packed, outer, 0, 0, tiled=True), axis=0)]
    dot_general x0 -> x1, local copies, waits for them, and re-layouts: none -> 2.56 us  [matmul(): jnp.dot(left, right, precision=lax.Precision.HIGH, preferred_element_type...]
  transfers between devices with their start and end apart: 5 -> 8, of which waited for: 4 -> 6; matrix products, arithmetic and copies ran while one was open for 3% -> 6% of each run, Pallas kernels for 0% -> 0%
where the time goes in v5:
time: 214 us; the launch traced here: 211 us
  blocking collectives  86.7 us (41%)
  waiting for transfers between devices  38.6 us (18%)
  matrix products  30.4 us (14%)
  local copies, waits for them, and re-layouts  28 us (13%)
  starting transfers between devices  18.1 us (8%)
  other arithmetic  8.46 us (4%)
    all_to_all x1, blocking collectives, per_device(): return lax.all_to_all(work, GROUP, 0, 1, tiled=True)  38.7 us
    dot_general x15, matrix products, matmul(): jnp.dot(left, right, precision=lax.Precision.HIGH, preferred_element_type...  30.4 us
    all_to_all x1, blocking collectives, all_reduce(): lax.all_to_all(jnp.broadcast_to(total, (outer_size, chunk)), outer, 0, 0,...  25.6 us
    all_to_all x1, blocking collectives, all_reduce(): total = jnp.sum(lax.all_to_all(packed, outer, 0, 0, tiled=True), axis=0)  22.4 us
    ppermute x1, waiting for transfers between devices, gather_ring(): from_left = lax.ppermute(block, axis, right)  17.2 us
    ppermute x3, waiting for transfers between devices, all_reduce(): lax.ppermute(total, inner, [(i, i ^ bit) for i in range(inner_size)])  16.7 us
    unnamed x25, local copies, waits for them, and re-layouts  10.9 us
    ppermute x3, starting transfers between devices, all_reduce(): lax.ppermute(total, inner, [(i, i ^ bit) for i in range(inner_size)])  5.93 us
  transfers between devices with their start and end apart: 8, of which 6 were waited for; matrix products, arithmetic and copies ran while one was open for 6% of the time, Pallas kernels for 0%

profile of v5, /device:TPU:64, one launch (start us, length us, event | category | flops | bytes accessed | tf_op | source)
XLA Modules:
  0.0 210.6 jit_solution(6740416400809364229)
XLA Ops:
  0.0 3.8 %copy.22 = f32[8,8,8,1536]{3,2,0,1:T(8,128)} copy(f32[8,8,8,1536]{3,2,1,0:T(8,128)} %bitcast.55) | data formatting | bytes 6291456 | tf_op jit(solution)/shard_map/all_to_all | solution.py:51
  3.8 5.7 %all-to-all-start = ((f32[64,8,1536]{2,0,1:T(8,128)}), f32[64,8,1536]{2,0,1:T(8,128)S(1)}, u32[]{:S(2)}, u32[]{:S(2)}) async-start(f32[64,8,1536]{2,0,1:T(8,128)} %bitcast.47), calls=%async_computation | async-start | bytes 6291456 | tf_op jit(solution)/shard_map/all_to_all | solution.py:51
  9.5 1.6 collective-permute-start.1
  11.1 1.7 collective-permute-start
  12.7 17.2 %collective-permute-done.1 = f32[384,512]{1,0:T(8,128)S(1)} collective-permute-done((f32[384,512]{1,0:T(8,128)}, f32[384,512]{1,0:T(8,128)S(1)}, u32[]{:S(2)}, u32[]{:S(2)}) %collective-permute-start.1) | collective-permute-done | bytes 786464 | tf_op jit(solution)/shard_map/ppermute | solution.py:32
  30.0 0.9 copy-done.1
  30.8 0.8 slice.112
  31.6 0.3 collective-permute-start.2
  31.9 0.0 collective-permute-done
  31.9 0.9 copy-done.3
  32.8 0.8 slice.113
  33.6 2.9 %collective-permute-start.3 = (f32[192,512]{1,0:T(8,128)}, f32[192,512]{1,0:T(8,128)}, u32[]{:S(2)}, u32[]{:S(2)}) collective-permute-start(f32[192,512]{1,0:T(8,128)} %slice.113), channel_id=1, source_target_pairs={{0,3},{1,0},{2,1},{3,2},{4,7},{5,4},{6,5},{7,6},{8,11},{9,8},{10,9... | collective-permute-start | bytes 1179656 | tf_op jit(solution)/shard_map/ppermute | solution.py:36
  36.6 1.3 constant_dynamic-update-slice_fusion.9
  37.9 0.0 copy-start.4
  37.9 1.3 constant_dynamic-update-slice_fusion.8
  39.1 3.6 %collective-permute-done.2 = f32[192,512]{1,0:T(8,128)S(1)} collective-permute-done((f32[192,512]{1,0:T(8,128)}, f32[192,512]{1,0:T(8,128)S(1)}, u32[]{:S(2)}, u32[]{:S(2)}) %collective-permute-start.2) | collective-permute-done | bytes 393248 | tf_op jit(solution)/shard_map/ppermute | solution.py:35
  42.8 1.0 collective-permute-done.3
  43.8 1.0 constant_dynamic-update-slice_fusion.6
  44.9 0.0 copy-done.2
  44.9 0.1 constant_dynamic-update-slice_fusion.5
  44.9 0.0 copy-done.5
  44.9 0.1 constant_dynamic-update-slice_fusion.4
  45.0 0.0 copy-done.4
  45.0 0.1 constant_dynamic-update-slice_fusion.3
  45.1 1.0 constant_dynamic-update-slice_fusion.1
  46.1 0.1 constant_dynamic-update-slice_fusion
  46.2 2.7 %copy-done = f32[3072,512]{1,0:T(8,128)} copy-done((f32[3072,512]{1,0:T(8,128)}, f32[3072,512]{1,0:T(8,128)S(1)}, u32[]{:S(2)}) %copy-start) | copy-done | bytes 6291480
  48.9 1.2 fusion.3
  50.1 2.7 %fusion.10 = f32[16,2,8,128]{3,2,1,0:T(8,128)S(1)} fusion(f32[3072,512]{1,0:T(8,128)} %copy-done, s32[]{:T(128)S(6)} %select_n.11, s32[]{:T(128)S(6)} %add.24), kind=kOutput, calls=%fused_computation.18 | convolution fusion | flops 301989888 | bytes 2491904 | tf_op jit(solution)/shard_map/dot_general | solution.py:13
  52.9 0.1 copy.20
  52.9 2.4 %convolution_bitcast_fusion = f32[16384]{0:T(1024)S(1)} fusion(f32[3072,512]{1,0:T(8,128)} %copy-done, s32[]{:T(128)S(6)} %select_n.11, s32[]{:T(128)S(6)} %add.23), kind=kOutput, calls=%fused_computation.7 | convolution fusion | flops 150994944 | bytes 1639936 | tf_op jit(solution)/shard_map/dot_general | solution.py:13
  55.4 0.0 all-to-all-done
  55.4 8.0 %fusion.7 = f32[512,512]{0,1:T(8,128)} fusion(f32[512,1536]{1,0:T(8,128)S(1)} %bitcast.45, f32[3072,512]{1,0:T(8,128)} %copy-done, s32[]{:T(128)S(6)} %select_n.11), kind=kOutput, calls=%fused_computation.11 | convolution fusion | flops 2415919104 | bytes 7340036 | tf_op jit(solution)/shard_map/dot_general | solution.py:13
  63.4 2.6 %copy.13 = f32[512,512]{1,0:T(8,128)} copy(f32[512,512]{0,1:T(8,128)} %fusion.7) | data formatting | bytes 2097152 | tf_op jit(solution)/shard_map/dot_general | solution.py:13
  65.9 1.5 copy.19
  67.4 0.1 pad_maximum_fusion
  67.5 22.4 %all_to_all.53 = f32[8,1,45056]{2,1,0:T(1,128)} all-to-all(f32[8,1,45056]{2,1,0:T(1,128)S(1)} %bitcast.52), channel_id=1, replica_groups=mesh['prow'=8,'x'=4,'zl'=2,'y'=4] {'x','zl'}, dimensions={0} | all-to-all | bytes 2883584 | tf_op jit(solution)/shard_map/all_to_all | solution.py:20
  90.0 2.4 %reduce_sum.9 = f32[45056]{0:T(1024)S(1)} reduce(f32[8,1,45056]{2,1,0:T(1,128)} %all_to_all.53, f32[]{:T(128)} %constant.20.clone.1), dimensions={0,1}, to_apply=%region_0.1 | reduce | flops 315392 | bytes 1622020 | tf_op jit(solution)/shard_map/reduce_sum | solution.py:20
  92.4 0.1 collective-permute-start.4
  92.5 1.4 collective-permute-done.4
  93.9 0.1 collective-permute-start.5
  94.0 8.2 %collective-permute-done.5 = f32[45056]{0:T(1024)S(1)} collective-permute-done((f32[45056]{0:T(1024)S(1)}, f32[45056]{0:T(1024)S(1)}, u32[]{:S(2)}, u32[]{:S(2)}) %collective-permute-start.5) | collective-permute-done | bytes 180256 | tf_op jit(solution)/shard_map/ppermute | solution.py:23
  102.3 5.7 %collective-permute-start.6 = (f32[45056]{0:T(1024)S(1)}, f32[45056]{0:T(1024)S(1)}, u32[]{:S(2)}, u32[]{:S(2)}) collective-permute-start(f32[45056]{0:T(1024)S(1)} %add.19), channel_id=1, source_target_pairs={{0,128},{32,160},{64,192},{96,224},{128,0},{160,32},{192,64},{224,... | collective-permute-start | bytes 540680 | tf_op jit(solution)/shard_map/ppermute | solution.py:23
  108.0 7.1 %collective-permute-done.6 = f32[45056]{0:T(1024)S(1)} collective-permute-done((f32[45056]{0:T(1024)S(1)}, f32[45056]{0:T(1024)S(1)}, u32[]{:S(2)}, u32[]{:S(2)}) %collective-permute-start.6) | collective-permute-done | bytes 180256 | tf_op jit(solution)/shard_map/ppermute | solution.py:23
  115.1 0.7 broadcast_in_dim.3
  115.9 25.6 %all_to_all.54 = f32[8,1,45056]{2,1,0:T(1,128)} all-to-all(f32[8,1,45056]{2,1,0:T(1,128)S(1)} %broadcast_in_dim.3), channel_id=1, replica_groups=mesh['prow'=8,'x'=4,'zl'=2,'y'=4] {'x','zl'}, dimensions={0} | all-to-all | bytes 2883584 | tf_op jit(solution)/shard_map/all_to_all | solution.py:25
  141.5 5.9 %reduce.1 = f32[8,45056]{1,0:T(8,128)} reduce(f32[8,1,45056]{2,1,0:T(1,128)} %all_to_all.54, f32[]{:T(128)} %constant.22), dimensions={1}, to_apply=%all_to_all.44.reduce_sub_computation | reduce | bytes 2883588 | tf_op jit(solution)/shard_map/all_to_all | solution.py:25
  147.4 2.8 %slice.94 = f32[704,512]{1,0:T(8,128)} reshape(f32[8,45056]{1,0:T(8,128)} %reduce.1) | data formatting | bytes 2883584 | tf_op jit(solution)/shard_map/slice | solution.py:57
  150.2 2.7 %slice.103 = f32[1408,256]{1,0:T(8,128)} reshape(f32[8,45056]{1,0:T(8,128)} %reduce.1) | data formatting | bytes 2883584 | tf_op jit(solution)/shard_map/slice | solution.py:60
  152.9 0.9 slice.118
  153.9 0.0 copy-start.6
  153.9 1.3 fusion.24
  155.1 1.3 convolution_subtract_fusion.6
  156.5 1.1 fusion.36
  157.6 1.4 convolution_subtract_fusion.5
  159.0 0.4 convolution_subtract_fusion.4
  159.4 0.3 fusion.34
  159.7 1.4 convolution_subtract_fusion.3
  161.1 1.2 convolution_subtract_fusion.2
  162.3 0.4 convolution_subtract_fusion.1
  162.7 0.3 fusion.32
  163.0 7.0 %convolution_subtract_fusion = f32[512,1536]{1,0:T(8,128)S(1)} fusion(f32[512,1536]{1,0:T(8,128)S(1)} %bitcast.46, f32[3072,512]{1,0:T(8,128)} %copy-done, s32[]{:T(128)S(6)} %select_n.11, f32[512,128]{0,1:T(8,128)S(1)} %fusion.24, f32[512,128]{0,1:T(8,128)S(1)} %fusion.36, f32[512,128]{0,1:T(8,128)S(1)} %fusion.34, f32[512,128]{0,1:T(8,128)S(1)} %fusion.32), kind=kOutput, calls=%fused_computation | convolution fusion | flops 2417491968 | bytes 10485764 | tf_op jit(solution)/shard_map/dot_general | solution.py:13
  170.0 38.7 %all_to_all.55 = f32[8,64,1536]{2,1,0:T(8,128)S(1)} all-to-all(f32[8,64,1536]{2,1,0:T(8,128)S(1)} %bitcast.49), channel_id=1, replica_groups=mesh['prow'=8,'x'=4,'zl'=2,'y'=4] {'x','zl'}, dimensions={0} | all-to-all | bytes 6291456 | tf_op jit(solution)/shard_map/all_to_all | solution.py:72
  208.7 1.9 copy.18
  (13 shorter events, 0.2 us)
Async XLA Ops:
  3.8 51.6 %all-to-all-start = ((f32[64,8,1536]{2,0,1:T(8,128)}), f32[64,8,1536]{2,0,1:T(8,128)S(1)}, u32[]{:S(2)}, u32[]{:S(2)}) async-start(f32[64,8,1536]{2,0,1:T(8,128)} %bitcast.47), calls=%async_computation | async-start | bytes 6291456 | tf_op jit(solution)/shard_map/all_to_all | solution.py:51
  9.5 20.5 %collective-permute-start.1 = (f32[384,512]{1,0:T(8,128)}, f32[384,512]{1,0:T(8,128)S(1)}, u32[]{:S(2)}, u32[]{:S(2)}) collective-permute-start(f32[384,512]{1,0:T(8,128)} %param.4), channel_id=1, source_target_pairs={{0,1},{1,2},{2,3},{3,0},{4,5},{5,6},{6,7},{7,4},{8,9},{9,10},{10,1... | collective-permute-start | bytes 2359304 | tf_op jit(solution)/shard_map/ppermute | solution.py:32
  11.1 20.9 %collective-permute-start = (f32[384,512]{1,0:T(8,128)}, f32[384,512]{1,0:T(8,128)S(1)}, u32[]{:S(2)}, u32[]{:S(2)}) collective-permute-start(f32[384,512]{1,0:T(8,128)} %param.4), channel_id=1, source_target_pairs={{0,3},{1,0},{2,1},{3,2},{4,7},{5,4},{6,5},{7,6},{8,11},{9,8},{10,9... | collective-permute-start | bytes 2359304 | tf_op jit(solution)/shard_map/ppermute | solution.py:33
  30.0 0.9 copy-start.1
  31.6 11.2 %collective-permute-start.2 = (f32[192,512]{1,0:T(8,128)}, f32[192,512]{1,0:T(8,128)S(1)}, u32[]{:S(2)}, u32[]{:S(2)}) collective-permute-start(f32[192,512]{1,0:T(8,128)} %slice.112), channel_id=1, source_target_pairs={{0,1},{1,2},{2,3},{3,0},{4,5},{5,6},{6,7},{7,4},{8,9},{9,10},{10,1... | collective-permute-start | bytes 1179656 | tf_op jit(solution)/shard_map/ppermute | solution.py:35
  31.9 0.9 copy-start.3
  33.6 10.2 %collective-permute-start.3 = (f32[192,512]{1,0:T(8,128)}, f32[192,512]{1,0:T(8,128)}, u32[]{:S(2)}, u32[]{:S(2)}) collective-permute-start(f32[192,512]{1,0:T(8,128)} %slice.113), channel_id=1, source_target_pairs={{0,3},{1,0},{2,1},{3,2},{4,7},{5,4},{6,5},{7,6},{8,11},{9,8},{10,9... | collective-permute-start | bytes 1179656 | tf_op jit(solution)/shard_map/ppermute | solution.py:36
  36.6 8.3 %copy-start.2 = (f32[384,512]{1,0:T(8,128)S(1)}, f32[384,512]{1,0:T(8,128)}, u32[]{:S(2)}) copy-start(f32[384,512]{1,0:T(8,128)} %copy-done.1) | copy-start | bytes 2359300
  36.6 8.4 %copy-start.5 = (f32[384,512]{1,0:T(8,128)S(1)}, f32[384,512]{1,0:T(8,128)}, u32[]{:S(2)}) copy-start(f32[384,512]{1,0:T(8,128)} %param.4) | copy-start | bytes 2359300
  37.9 7.1 %copy-start.4 = (f32[384,512]{1,0:T(8,128)S(1)}, f32[384,512]{1,0:T(8,128)}, u32[]{:S(2)}) copy-start(f32[384,512]{1,0:T(8,128)} %copy-done.3) | copy-start | bytes 2359300
  46.2 2.7 %copy-start = (f32[3072,512]{1,0:T(8,128)}, f32[3072,512]{1,0:T(8,128)S(1)}, u32[]{:S(2)}) copy-start(f32[3072,512]{1,0:T(8,128)S(1)} %constant_dynamic-update-slice_fusion) | copy-start | bytes 18874372
  92.4 1.5 collective-permute-start.4
  93.9 8.3 %collective-permute-start.5 = (f32[45056]{0:T(1024)S(1)}, f32[45056]{0:T(1024)S(1)}, u32[]{:S(2)}, u32[]{:S(2)}) collective-permute-start(f32[45056]{0:T(1024)S(1)} %add.18), channel_id=1, source_target_pairs={{0,64},{32,96},{64,0},{96,32},{128,192},{160,224},{192,128},{224,1... | collective-permute-start | bytes 540680 | tf_op jit(solution)/shard_map/ppermute | solution.py:23
  102.3 12.8 %collective-permute-start.6 = (f32[45056]{0:T(1024)S(1)}, f32[45056]{0:T(1024)S(1)}, u32[]{:S(2)}, u32[]{:S(2)}) collective-permute-start(f32[45056]{0:T(1024)S(1)} %add.19), channel_id=1, source_target_pairs={{0,128},{32,160},{64,192},{96,224},{128,0},{160,32},{192,64},{224,... | collective-permute-start | bytes 540680 | tf_op jit(solution)/shard_map/ppermute | solution.py:23
  153.9 5.6 %copy-start.6 = (f32[4,128,128]{2,1,0:T(8,128)S(1)}, f32[4,128,128]{2,1,0:T(8,128)}, u32[]{:S(2)}) copy-start(f32[4,128,128]{2,1,0:T(8,128)} %param.5) | copy-start | bytes 786436

commit v6 on v5

--- a/solution.py
+++ b/solution.py
@@ -14,16 +14,16 @@
 
 
 def all_reduce(packed, outer, inner, outer_size, inner_size):
-    size = packed.shape[0]
-    chunk = -(-size // outer_size)
-    packed = jnp.pad(packed, (0, chunk * outer_size - size)).reshape(outer_size, chunk)
+    rows, lanes = packed.shape
+    chunk = -(-rows // (8 * outer_size)) * 8
+    packed = jnp.pad(packed, ((0, chunk * outer_size - rows), (0, 0))).reshape(outer_size, chunk, lanes)
     total = jnp.sum(lax.all_to_all(packed, outer, 0, 0, tiled=True), axis=0)
     bit = 1
     while bit < inner_size:
         total = total + lax.ppermute(total, inner, [(i, i ^ bit) for i in range(inner_size)])
         bit *= 2
-    total = lax.all_to_all(jnp.broadcast_to(total, (outer_size, chunk)), outer, 0, 0, tiled=True)
-    return total.reshape(-1)[:size]
+    total = lax.all_to_all(jnp.broadcast_to(total, (outer_size, chunk, lanes)), outer, 0, 0, tiled=True)
+    return total.reshape(outer_size * chunk, lanes)[:rows]
 
 
 def gather_ring(block, axis, size):
@@ -50,21 +50,24 @@
     basis = gather_ring(vectors, "y", PCOL_PARTS[2])
     work = lax.all_to_all(slab, GROUP, 1, 0, tiled=True)
 
-    products = matmul(work, basis)
-    grams = [matmul(basis[:, j * width : (j + 1) * width].T, basis[:, : j * width]) for j in range(1, count)]
-    packed = jnp.concatenate([products.reshape(-1)] + [g.reshape(-1) for g in grams])
-    packed = all_reduce(packed, GROUP, "prow", ng, nprow)
-    products, offset = packed[: products.size].reshape(products.shape), products.size
+    blocks = [basis[:, k * width : (k + 1) * width] for k in range(count)]
+    products = [matmul(work, blocks[k]) for k in range(count)]
+    grams = [matmul(blocks[j].T, basis[:, : j * width]) for j in range(1, count)]
+    grams = [g[:, k * width : (k + 1) * width] for j, g in enumerate(grams, 1) for k in range(j)]
+    packed = all_reduce(jnp.concatenate(products + grams, axis=0), GROUP, "prow", ng, nprow)
+    span = products[0].shape[0]
+    products = [packed[k * span : (k + 1) * span] for k in range(count)]
+    offset = count * span
+    gram = {}
     for j in range(1, count):
-        size = grams[j - 1].size
-        grams[j - 1], offset = packed[offset : offset + size].reshape(grams[j - 1].shape), offset + size
+        for k in range(j):
+            gram[j, k], offset = packed[offset : offset + width], offset + width
 
     scaled = [None] * count
     for k in reversed(range(count)):
-        part = products[:, k * width : (k + 1) * width]
+        part = products[k]
         for j in range(k + 1, count):
-            block = grams[j - 1][:, k * width : (k + 1) * width]
-            part = part - matmul(scaled[j], block)
+            part = part - matmul(scaled[j], gram[j, k])
         scaled[k] = matmul(part, tfactors[k].T)
     scaled = jnp.concatenate(scaled, axis=1)
 

time: 214 us -> 197 us (0.921)
  other arithmetic: 8.46 us -> 1.52 us
  local copies, waits for them, and re-layouts: 28 us -> 21.4 us
  matrix products: 30.4 us -> 28.1 us
    slice x3 -> x0, local copies, waits for them, and re-layouts: 6.41 us -> none  [the longest x2 3.62 us: per_device(): packed[offset:offset + size].reshape(grams[j - 1].shape)]
    all_to_all x1 -> x0, other arithmetic: 5.89 us -> none  [all_reduce(): lax.all_to_all(jnp.broadcast_to(total, (outer_size, chunk)), outer, 0, 0,...]
    concatenate x0 -> x2, local copies, waits for them, and re-layouts: none -> 3.74 us  [per_device(): jnp.concatenate(products + grams, axis=0)]
    dot_general x1 -> x0, local copies, waits for them, and re-layouts: 2.56 us -> none  [matmul(): jnp.dot(left, right, precision=lax.Precision.HIGH, preferred_element_type...]
    dot_general x15 -> x18, matrix products: 30.4 us -> 28.1 us  [matmul(): jnp.dot(left, right, precision=lax.Precision.HIGH, preferred_element_type...]
    unnamed x25 -> x29, local copies, waits for them, and re-layouts: 10.9 us -> 10.2 us
  transfers between devices with their start and end apart: 8 -> 8, of which waited for: 6 -> 6; matrix products, arithmetic and copies ran while one was open for 6% -> 5% of each run, Pallas kernels for 0% -> 0%
where the time goes in v6:
time: 197 us; the launch traced here: 195 us
  blocking collectives  86.8 us (44%)
  waiting for transfers between devices  38.6 us (20%)
  matrix products  28.1 us (14%)
  local copies, waits for them, and re-layouts  21.4 us (11%)
  starting transfers between devices  18.1 us (9%)
    all_to_all x1, blocking collectives, per_device(): return lax.all_to_all(work, GROUP, 0, 1, tiled=True)  38.7 us
    dot_general x18, matrix products, matmul(): jnp.dot(left, right, precision=lax.Precision.HIGH, preferred_element_type...  28.1 us
    all_to_all x1, blocking collectives, all_reduce(): lax.all_to_all(jnp.broadcast_to(total, (outer_size, chunk, lanes)), outer...  25.5 us
    all_to_all x1, blocking collectives, all_reduce(): total = jnp.sum(lax.all_to_all(packed, outer, 0, 0, tiled=True), axis=0)  22.6 us
    ppermute x1, waiting for transfers between devices, gather_ring(): from_left = lax.ppermute(block, axis, right)  17.2 us
    ppermute x3, waiting for transfers between devices, all_reduce(): lax.ppermute(total, inner, [(i, i ^ bit) for i in range(inner_size)])  16.7 us
    unnamed x29, local copies, waits for them, and re-layouts  10.2 us
    ppermute x3, starting transfers between devices, all_reduce(): lax.ppermute(total, inner, [(i, i ^ bit) for i in range(inner_size)])  5.93 us
  transfers between devices with their start and end apart: 8, of which 6 were waited for; matrix products, arithmetic and copies ran while one was open for 5% of the time, Pallas kernels for 0%

profile of v6, /device:TPU:64, one launch (start us, length us, event | category | flops | bytes accessed | tf_op | source)
XLA Modules:
  0.0 194.8 jit_solution(12093324313924933387)
XLA Ops:
  0.0 3.8 %copy.27 = f32[8,8,8,1536]{3,2,0,1:T(8,128)} copy(f32[8,8,8,1536]{3,2,1,0:T(8,128)} %bitcast.70) | data formatting | bytes 6291456 | tf_op jit(solution)/shard_map/all_to_all | solution.py:51
  3.8 5.7 %all-to-all-start = ((f32[64,8,1536]{2,0,1:T(8,128)}), f32[64,8,1536]{2,0,1:T(8,128)S(1)}, u32[]{:S(2)}, u32[]{:S(2)}) async-start(f32[64,8,1536]{2,0,1:T(8,128)} %bitcast.58), calls=%async_computation | async-start | bytes 6291456 | tf_op jit(solution)/shard_map/all_to_all | solution.py:51
  9.5 1.6 collective-permute-start.1
  11.1 1.7 collective-permute-start
  12.7 17.2 %collective-permute-done.1 = f32[384,512]{1,0:T(8,128)S(1)} collective-permute-done((f32[384,512]{1,0:T(8,128)}, f32[384,512]{1,0:T(8,128)S(1)}, u32[]{:S(2)}, u32[]{:S(2)}) %collective-permute-start.1) | collective-permute-done | bytes 786464 | tf_op jit(solution)/shard_map/ppermute | solution.py:32
  30.0 0.9 copy-done.2
  30.9 0.8 slice.109
  31.7 0.3 collective-permute-start.2
  32.0 0.0 collective-permute-done
  32.0 0.9 copy-done.4
  32.9 0.8 slice.110
  33.7 2.9 %collective-permute-start.3 = (f32[192,512]{1,0:T(8,128)}, f32[192,512]{1,0:T(8,128)}, u32[]{:S(2)}, u32[]{:S(2)}) collective-permute-start(f32[192,512]{1,0:T(8,128)} %slice.110), channel_id=1, source_target_pairs={{0,3},{1,0},{2,1},{3,2},{4,7},{5,4},{6,5},{7,6},{8,11},{9,8},{10,9... | collective-permute-start | bytes 1179656 | tf_op jit(solution)/shard_map/ppermute | solution.py:36
  36.6 1.3 constant_dynamic-update-slice_fusion.9
  37.9 0.0 copy-start.5
  37.9 1.3 constant_dynamic-update-slice_fusion.8
  39.2 3.6 %collective-permute-done.2 = f32[192,512]{1,0:T(8,128)S(1)} collective-permute-done((f32[192,512]{1,0:T(8,128)}, f32[192,512]{1,0:T(8,128)S(1)}, u32[]{:S(2)}, u32[]{:S(2)}) %collective-permute-start.2) | collective-permute-done | bytes 393248 | tf_op jit(solution)/shard_map/ppermute | solution.py:35
  42.8 1.0 collective-permute-done.3
  43.9 1.0 constant_dynamic-update-slice_fusion.6
  44.9 0.0 copy-done.3
  44.9 0.1 constant_dynamic-update-slice_fusion.5
  45.0 0.1 constant_dynamic-update-slice_fusion.4
  45.1 0.1 constant_dynamic-update-slice_fusion.3
  45.2 1.0 constant_dynamic-update-slice_fusion.1
  46.2 0.1 constant_dynamic-update-slice_fusion
  46.3 1.6 fusion.3
  47.9 1.0 copy-done
  48.9 2.3 %fusion.1 = f32[128,384]{0,1:T(8,128)S(1)} fusion(f32[3072,512]{1,0:T(8,128)S(1)} %constant_dynamic-update-slice_fusion, s32[]{:T(128)S(6)} %select_n.11, s32[]{:T(128)S(6)} %add.23), kind=kOutput, calls=%fused_computation.3 | convolution fusion | flops 452984832 | bytes 3343872 | tf_op jit(solution)/shard_map/dot_general | solution.py:13
  51.2 0.0 all-to-all-done
  51.2 3.8 %fusion.8 = f32[2816,128]{0,1:T(8,128)} fusion(f32[512,1536]{1,0:T(8,128)S(1)} %bitcast.53, f32[3072,512]{1,0:T(8,128)} %copy-done, s32[]{:T(128)S(6)} %select_n.11), kind=kOutput, calls=%fused_computation.17 | convolution fusion | flops 603979776 | bytes 4194308 | tf_op jit(solution)/shard_map/dot_general | solution.py:13
  54.9 3.5 %fusion.7 = f32[2816,128]{0,1:T(8,128)} fusion(f32[2816,128]{0,1:T(8,128)} %fusion.8, f32[512,1536]{1,0:T(8,128)S(1)} %bitcast.54, f32[3072,512]{1,0:T(8,128)} %copy-done, s32[]{:T(128)S(6)} %select_n.11, s32[]{:T(128)S(6)} %add.21), kind=kOutput, calls=%fused_computation.15 | convolution fusion | flops 603979776 | bytes 4194312 | tf_op jit(solution)/shard_map/dot_general | solution.py:13
  58.5 0.0 copy-done.1
  58.5 2.4 %fusion.6 = f32[2816,128]{0,1:T(8,128)} fusion(f32[2816,128]{0,1:T(8,128)} %fusion.7, f32[512,1536]{1,0:T(8,128)S(1)} %bitcast.55, f32[3072,512]{1,0:T(8,128)S(1)} %copy-done.1, s32[]{:T(128)S(6)} %select_n.11, s32[]{:T(128)S(6)} %add.22), kind=kOutput, calls=%fused_computation.13 | convolution fusion | flops 603979776 | bytes 4194312 | tf_op jit(solution)/shard_map/dot_general | solution.py:13
  60.9 2.4 %fusion.5 = f32[2816,128]{0,1:T(8,128)} fusion(f32[2816,128]{0,1:T(8,128)} %fusion.6, f32[512,1536]{1,0:T(8,128)S(1)} %bitcast.56, f32[3072,512]{1,0:T(8,128)S(1)} %copy-done.1, s32[]{:T(128)S(6)} %select_n.11, s32[]{:T(128)S(6)} %add.23), kind=kOutput, calls=%fused_computation.11 | convolution fusion | flops 603979776 | bytes 4194312 | tf_op jit(solution)/shard_map/dot_general | solution.py:13
  63.3 1.7 convolution_dynamic-update-slice_fusion
  65.0 0.6 slice_dynamic-update-slice_fusion.4
  65.6 0.6 slice_dynamic-update-slice_fusion.3
  66.2 0.6 slice_dynamic-update-slice_fusion.2
  66.9 0.6 slice_dynamic-update-slice_fusion.1
  67.5 0.6 slice_dynamic-update-slice_fusion
  68.1 3.1 %copy.19 = f32[2816,128]{1,0:T(8,128)} copy(f32[2816,128]{0,1:T(8,128)} %slice_dynamic-update-slice_fusion) | data formatting | bytes 2883584 | tf_op jit(solution)/shard_map/concatenate | solution.py:57
  71.2 22.6 %all_to_all.48 = f32[8,352,128]{2,1,0:T(8,128)} all-to-all(f32[8,352,128]{2,1,0:T(8,128)} %bitcast.61), channel_id=1, replica_groups=mesh['prow'=8,'x'=4,'zl'=2,'y'=4] {'x','zl'}, dimensions={0} | all-to-all | bytes 2883584 | tf_op jit(solution)/shard_map/all_to_all | solution.py:20
  93.9 1.4 reduce_sum.9
  95.3 0.0 copy-start.7
  95.3 0.1 collective-permute-start.4
  95.4 1.4 collective-permute-done.4
  96.9 0.1 collective-permute-start.5
  97.0 8.2 %collective-permute-done.5 = f32[352,128]{1,0:T(8,128)S(1)} collective-permute-done((f32[352,128]{1,0:T(8,128)S(1)}, f32[352,128]{1,0:T(8,128)S(1)}, u32[]{:S(2)}, u32[]{:S(2)}) %collective-permute-start.5) | collective-permute-done | bytes 180256 | tf_op jit(solution)/shard_map/ppermute | solution.py:23
  105.2 5.7 %collective-permute-start.6 = (f32[352,128]{1,0:T(8,128)S(1)}, f32[352,128]{1,0:T(8,128)S(1)}, u32[]{:S(2)}, u32[]{:S(2)}) collective-permute-start(f32[352,128]{1,0:T(8,128)S(1)} %add.19), channel_id=1, source_target_pairs={{0,128},{32,160},{64,192},{96,224},{128,0},{160,32},{192,64},{224,... | collective-permute-start | bytes 540680 | tf_op jit(solution)/shard_map/ppermute | solution.py:23
  111.0 7.1 %collective-permute-done.6 = f32[352,128]{1,0:T(8,128)S(1)} collective-permute-done((f32[352,128]{1,0:T(8,128)S(1)}, f32[352,128]{1,0:T(8,128)S(1)}, u32[]{:S(2)}, u32[]{:S(2)}) %collective-permute-start.6) | collective-permute-done | bytes 180256 | tf_op jit(solution)/shard_map/ppermute | solution.py:23
  118.1 0.1 broadcast_in_dim.3
  118.2 25.5 %all_to_all.49 = f32[8,352,128]{2,1,0:T(8,128)S(1)} all-to-all(f32[8,352,128]{2,1,0:T(8,128)S(1)} %broadcast_in_dim.3), channel_id=1, replica_groups=mesh['prow'=8,'x'=4,'zl'=2,'y'=4] {'x','zl'}, dimensions={0} | all-to-all | bytes 2883584 | tf_op jit(solution)/shard_map/all_to_all | solution.py:25
  143.7 0.3 fusion.24
  144.0 0.4 fusion.34
  144.4 0.3 fusion.26
  144.7 0.4 fusion.32
  145.1 0.4 convolution_subtract_fusion.3
  145.4 0.3 fusion.38
  145.7 0.4 fusion.29
  146.1 0.4 convolution_subtract_fusion.2
  146.5 0.4 convolution_subtract_fusion.1
  146.9 0.3 fusion.36
  147.2 7.0 %convolution_subtract_fusion = f32[512,1536]{1,0:T(8,128)S(1)} fusion(f32[512,1536]{1,0:T(8,128)S(1)} %bitcast.57, f32[3072,512]{1,0:T(8,128)} %copy-done, s32[]{:T(128)S(6)} %select_n.11, f32[512,128]{0,1:T(8,128)S(1)} %fusion.24, f32[512,128]{0,1:T(8,128)S(1)} %fusion.26, f32[512,128]{0,1:T(8,128)S(1)} %fusion.38, f32[512,128]{0,1:T(8,128)S(1)} %fusion.36), kind=kOutput, calls=%fused_computation | convolution fusion | flops 2417491968 | bytes 10485764 | tf_op jit(solution)/shard_map/dot_general | solution.py:13
  154.2 38.7 %all_to_all.50 = f32[8,64,1536]{2,1,0:T(8,128)S(1)} all-to-all(f32[8,64,1536]{2,1,0:T(8,128)S(1)} %bitcast.60), channel_id=1, replica_groups=mesh['prow'=8,'x'=4,'zl'=2,'y'=4] {'x','zl'}, dimensions={0} | all-to-all | bytes 6291456 | tf_op jit(solution)/shard_map/all_to_all | solution.py:75
  192.9 1.9 copy.25
  (14 shorter events, 0.1 us)
Async XLA Ops:
  3.8 47.3 %all-to-all-start = ((f32[64,8,1536]{2,0,1:T(8,128)}), f32[64,8,1536]{2,0,1:T(8,128)S(1)}, u32[]{:S(2)}, u32[]{:S(2)}) async-start(f32[64,8,1536]{2,0,1:T(8,128)} %bitcast.58), calls=%async_computation | async-start | bytes 6291456 | tf_op jit(solution)/shard_map/all_to_all | solution.py:51
  9.5 20.5 %collective-permute-start.1 = (f32[384,512]{1,0:T(8,128)}, f32[384,512]{1,0:T(8,128)S(1)}, u32[]{:S(2)}, u32[]{:S(2)}) collective-permute-start(f32[384,512]{1,0:T(8,128)} %param.4), channel_id=1, source_target_pairs={{0,1},{1,2},{2,3},{3,0},{4,5},{5,6},{6,7},{7,4},{8,9},{9,10},{10,1... | collective-permute-start | bytes 2359304 | tf_op jit(solution)/shard_map/ppermute | solution.py:32
  11.1 20.9 %collective-permute-start = (f32[384,512]{1,0:T(8,128)}, f32[384,512]{1,0:T(8,128)S(1)}, u32[]{:S(2)}, u32[]{:S(2)}) collective-permute-start(f32[384,512]{1,0:T(8,128)} %param.4), channel_id=1, source_target_pairs={{0,3},{1,0},{2,1},{3,2},{4,7},{5,4},{6,5},{7,6},{8,11},{9,8},{10,9... | collective-permute-start | bytes 2359304 | tf_op jit(solution)/shard_map/ppermute | solution.py:33
  30.0 0.9 copy-start.2
  31.7 11.2 %collective-permute-start.2 = (f32[192,512]{1,0:T(8,128)}, f32[192,512]{1,0:T(8,128)S(1)}, u32[]{:S(2)}, u32[]{:S(2)}) collective-permute-start(f32[192,512]{1,0:T(8,128)} %slice.109), channel_id=1, source_target_pairs={{0,1},{1,2},{2,3},{3,0},{4,5},{5,6},{6,7},{7,4},{8,9},{9,10},{10,1... | collective-permute-start | bytes 1179656 | tf_op jit(solution)/shard_map/ppermute | solution.py:35
  32.0 0.9 copy-start.4
  33.7 10.2 %collective-permute-start.3 = (f32[192,512]{1,0:T(8,128)}, f32[192,512]{1,0:T(8,128)}, u32[]{:S(2)}, u32[]{:S(2)}) collective-permute-start(f32[192,512]{1,0:T(8,128)} %slice.110), channel_id=1, source_target_pairs={{0,3},{1,0},{2,1},{3,2},{4,7},{5,4},{6,5},{7,6},{8,11},{9,8},{10,9... | collective-permute-start | bytes 1179656 | tf_op jit(solution)/shard_map/ppermute | solution.py:36
  36.6 8.3 %copy-start.3 = (f32[384,512]{1,0:T(8,128)S(1)}, f32[384,512]{1,0:T(8,128)}, u32[]{:S(2)}) copy-start(f32[384,512]{1,0:T(8,128)} %copy-done.2) | copy-start | bytes 2359300
  36.6 8.4 %copy-start.6 = (f32[384,512]{1,0:T(8,128)S(1)}, f32[384,512]{1,0:T(8,128)}, u32[]{:S(2)}) copy-start(f32[384,512]{1,0:T(8,128)} %param.4) | copy-start | bytes 2359300
  37.9 7.1 %copy-start.5 = (f32[384,512]{1,0:T(8,128)S(1)}, f32[384,512]{1,0:T(8,128)}, u32[]{:S(2)}) copy-start(f32[384,512]{1,0:T(8,128)} %copy-done.4) | copy-start | bytes 2359300
  46.2 2.6 %copy-start = (f32[3072,512]{1,0:T(8,128)}, f32[3072,512]{1,0:T(8,128)S(1)}, u32[]{:S(2)}) copy-start(f32[3072,512]{1,0:T(8,128)S(1)} %constant_dynamic-update-slice_fusion) | copy-start | bytes 18874372
  51.2 7.3 %copy-start.1 = (f32[3072,512]{1,0:T(8,128)S(1)}, f32[3072,512]{1,0:T(8,128)}, u32[]{:S(2)}) copy-start(f32[3072,512]{1,0:T(8,128)} %copy-done) | copy-start | bytes 18874372
  95.3 48.4 %copy-start.7 = (f32[4,128,128]{2,1,0:T(8,128)S(1)}, f32[4,128,128]{2,1,0:T(8,128)}, u32[]{:S(2)}) copy-start(f32[4,128,128]{2,1,0:T(8,128)} %param.5) | copy-start | bytes 786436
  95.3 1.5 collective-permute-start.4
  96.9 8.3 %collective-permute-start.5 = (f32[352,128]{1,0:T(8,128)S(1)}, f32[352,128]{1,0:T(8,128)S(1)}, u32[]{:S(2)}, u32[]{:S(2)}) collective-permute-start(f32[352,128]{1,0:T(8,128)S(1)} %add.18), channel_id=1, source_target_pairs={{0,64},{32,96},{64,0},{96,32},{128,192},{160,224},{192,128},{224,1... | collective-permute-start | bytes 540680 | tf_op jit(solution)/shard_map/ppermute | solution.py:23
  105.2 12.8 %collective-permute-start.6 = (f32[352,128]{1,0:T(8,128)S(1)}, f32[352,128]{1,0:T(8,128)S(1)}, u32[]{:S(2)}, u32[]{:S(2)}) collective-permute-start(f32[352,128]{1,0:T(8,128)S(1)} %add.19), channel_id=1, source_target_pairs={{0,128},{32,160},{64,192},{96,224},{128,0},{160,32},{192,64},{224,... | collective-permute-start | bytes 540680 | tf_op jit(solution)/shard_map/ppermute | solution.py:23

commit v7 on v6

--- a/solution.py
+++ b/solution.py
@@ -50,18 +50,19 @@
     basis = gather_ring(vectors, "y", PCOL_PARTS[2])
     work = lax.all_to_all(slab, GROUP, 1, 0, tiled=True)
 
-    blocks = [basis[:, k * width : (k + 1) * width] for k in range(count)]
-    products = [matmul(work, blocks[k]) for k in range(count)]
-    grams = [matmul(blocks[j].T, basis[:, : j * width]) for j in range(1, count)]
-    grams = [g[:, k * width : (k + 1) * width] for j, g in enumerate(grams, 1) for k in range(j)]
-    packed = all_reduce(jnp.concatenate(products + grams, axis=0), GROUP, "prow", ng, nprow)
-    span = products[0].shape[0]
-    products = [packed[k * span : (k + 1) * span] for k in range(count)]
-    offset = count * span
-    gram = {}
+    products = matmul(work, basis)
+    grams = jnp.concatenate([matmul(basis[:, j * width : (j + 1) * width].T, basis[:, : j * width]) for j in range(1, count)], axis=1)
+    lanes = products.shape[1]
+    packed = jnp.concatenate([products, grams.reshape(-1, lanes)], axis=0)
+    half = lanes // 2
+    packed = jnp.concatenate([all_reduce(packed[:, :half], GROUP, "prow", ng, nprow), all_reduce(packed[:, half:], GROUP, "prow", ng, nprow)], axis=1)
+    span = products.shape[0]
+    products = [packed[:span, k * width : (k + 1) * width] for k in range(count)]
+    grams = packed[span:].reshape(grams.shape)
+    gram, offset = {}, 0
     for j in range(1, count):
         for k in range(j):
-            gram[j, k], offset = packed[offset : offset + width], offset + width
+            gram[j, k], offset = grams[:, offset : offset + width], offset + width
 
     scaled = [None] * count
     for k in reversed(range(count)):

time: 197 us -> 202 us (1.025)
  blocking collectives: 86.8 us -> 70.7 us
  starting transfers between devices: 18.1 us -> 33.5 us
  waiting for transfers between devices: 38.6 us -> 46.9 us
  matrix products: 28.1 us -> 23.9 us
  other arithmetic: 1.52 us -> 5.09 us
    all_to_all x0 -> x2, starting transfers between devices: none -> 12.2 us  [the longest x1 7.96 us: all_reduce(): lax.all_to_all(jnp.broadcast_to(total, (outer_size, chunk, lanes)), outer...]
    ppermute x3 -> x6, waiting for transfers between devices: 16.7 us -> 24.9 us  [all_reduce(): lax.ppermute(total, inner, [(i, i ^ bit) for i in range(inner_size)])]
    all_to_all x1, blocking collectives: 22.6 us -> 14.8 us  [all_reduce(): total = jnp.sum(lax.all_to_all(packed, outer, 0, 0, tiled=True), axis=0)]
    all_to_all x1, blocking collectives: 25.5 us -> 17.7 us  [all_reduce(): lax.all_to_all(jnp.broadcast_to(total, (outer_size, chunk, lanes)), outer...]
    dot_general x18 -> x15, matrix products: 28.1 us -> 23.9 us  [matmul(): jnp.dot(left, right, precision=lax.Precision.HIGH, preferred_element_type...]
    concatenate x2 -> x0, local copies, waits for them, and re-layouts: 3.74 us -> none  [per_device(): jnp.concatenate(products + grams, axis=0)]
    ppermute x3 -> x6, starting transfers between devices: 5.93 us -> 9.26 us  [all_reduce(): lax.ppermute(total, inner, [(i, i ^ bit) for i in range(inner_size)])]
    concatenate x0 -> x3, other arithmetic: none -> 2.69 us  [the longest x1 1.71 us: per_device(): jnp.concatenate([all_reduce(packed[:, :half], GROUP, 'prow', ng, nprow),...]
  transfers between devices with their start and end apart: 8 -> 13, of which waited for: 6 -> 9; matrix products, arithmetic and copies ran while one was open for 5% -> 7% of each run, Pallas kernels for 0% -> 0%
where the time goes in v7:
time: 202 us; the launch traced here: 200 us
  blocking collectives  70.7 us (35%)
  waiting for transfers between devices  46.9 us (23%)
  starting transfers between devices  33.5 us (17%)
  matrix products  23.9 us (12%)
  local copies, waits for them, and re-layouts  19.4 us (10%)
  other arithmetic  5.09 us (3%)
    all_to_all x1, blocking collectives, per_device(): return lax.all_to_all(work, GROUP, 0, 1, tiled=True)  38.2 us
    ppermute x6, waiting for transfers between devices, all_reduce(): lax.ppermute(total, inner, [(i, i ^ bit) for i in range(inner_size)])  24.9 us
    dot_general x15, matrix products, matmul(): jnp.dot(left, right, precision=lax.Precision.HIGH, preferred_element_type...  23.9 us
    all_to_all x1, blocking collectives, all_reduce(): lax.all_to_all(jnp.broadcast_to(total, (outer_size, chunk, lanes)), outer...  17.7 us
    ppermute x1, waiting for transfers between devices, gather_ring(): from_left = lax.ppermute(block, axis, right)  17.2 us
    all_to_all x1, blocking collectives, all_reduce(): total = jnp.sum(lax.all_to_all(packed, outer, 0, 0, tiled=True), axis=0)  14.8 us
    ppermute x6, starting transfers between devices, all_reduce(): lax.ppermute(total, inner, [(i, i ^ bit) for i in range(inner_size)])  9.26 us
    unnamed x25, local copies, waits for them, and re-layouts  9.08 us
  transfers between devices with their start and end apart: 13, of which 9 were waited for; matrix products, arithmetic and copies ran while one was open for 7% of the time, Pallas kernels for 0%

profile of v7, /device:TPU:64, one launch (start us, length us, event | category | flops | bytes accessed | tf_op | source)
XLA Modules:
  0.0 199.9 jit_solution(5479026378721414743)
XLA Ops:
  0.0 3.8 %copy.11 = f32[8,8,8,1536]{3,2,0,1:T(8,128)} copy(f32[8,8,8,1536]{3,2,1,0:T(8,128)} %bitcast.45) | data formatting | bytes 6291456 | tf_op jit(solution)/shard_map/all_to_all | solution.py:51
  3.8 5.7 %all-to-all-start = ((f32[64,8,1536]{2,0,1:T(8,128)}), f32[64,8,1536]{2,0,1:T(8,128)S(1)}, u32[]{:S(2)}, u32[]{:S(2)}) async-start(f32[64,8,1536]{2,0,1:T(8,128)} %bitcast.37), calls=%async_computation | async-start | bytes 6291456 | tf_op jit(solution)/shard_map/all_to_all | solution.py:51
  9.5 1.6 collective-permute-start.1
  11.1 1.7 collective-permute-start
  12.7 17.2 %collective-permute-done.1 = f32[384,512]{1,0:T(8,128)S(1)} collective-permute-done((f32[384,512]{1,0:T(8,128)}, f32[384,512]{1,0:T(8,128)S(1)}, u32[]{:S(2)}, u32[]{:S(2)}) %collective-permute-start.1) | collective-permute-done | bytes 786464 | tf_op jit(solution)/shard_map/ppermute | solution.py:32
  30.0 0.9 copy-done.2
  30.9 0.8 slice.100
  31.6 0.3 collective-permute-start.2
  31.9 0.0 collective-permute-done
  31.9 0.9 copy-done.4
  32.8 0.8 slice.101
  33.6 2.9 %collective-permute-start.3 = (f32[192,512]{1,0:T(8,128)}, f32[192,512]{1,0:T(8,128)}, u32[]{:S(2)}, u32[]{:S(2)}) collective-permute-start(f32[192,512]{1,0:T(8,128)} %slice.101), channel_id=1, source_target_pairs={{0,3},{1,0},{2,1},{3,2},{4,7},{5,4},{6,5},{7,6},{8,11},{9,8},{10,9... | collective-permute-start | bytes 1179656 | tf_op jit(solution)/shard_map/ppermute | solution.py:36
  36.6 1.3 constant_dynamic-update-slice_fusion.9
  37.9 1.2 constant_dynamic-update-slice_fusion.8
  39.1 3.7 %collective-permute-done.2 = f32[192,512]{1,0:T(8,128)S(1)} collective-permute-done((f32[192,512]{1,0:T(8,128)}, f32[192,512]{1,0:T(8,128)S(1)}, u32[]{:S(2)}, u32[]{:S(2)}) %collective-permute-start.2) | collective-permute-done | bytes 393248 | tf_op jit(solution)/shard_map/ppermute | solution.py:35
  42.8 1.0 collective-permute-done.3
  43.9 1.0 constant_dynamic-update-slice_fusion.6
  44.9 1.2 constant_dynamic-update-slice_fusion.5
  46.1 0.1 constant_dynamic-update-slice_fusion.4
  46.1 0.1 constant_dynamic-update-slice_fusion.3
  46.2 1.0 constant_dynamic-update-slice_fusion.1
  47.3 0.1 constant_dynamic-update-slice_fusion
  47.4 1.1 fusion.19
  48.4 1.1 fusion.5
  49.5 0.5 copy-done
  50.0 1.2 fusion.3
  51.3 0.9 reshape.24
  52.2 4.6 %fusion.7 = f32[512,512]{1,0:T(8,128)S(1)} fusion(f32[512,1536]{1,0:T(8,128)S(1)} %bitcast.39, f32[3072,512]{1,0:T(8,128)} %copy-done, s32[]{:T(128)S(6)} %select_n.11), kind=kOutput, calls=%fused_computation.11 | convolution fusion | flops 2415919104 | bytes 7340036 | tf_op jit(solution)/shard_map/dot_general | solution.py:13
  56.8 1.0 fusion.22
  57.7 14.8 %all_to_all.58 = f32[8,88,256]{2,1,0:T(8,128)} all-to-all(f32[8,88,256]{2,1,0:T(8,128)S(1)} %bitcast.47), channel_id=1, replica_groups=mesh['prow'=8,'x'=4,'zl'=2,'y'=4] {'x','zl'}, dimensions={0} | all-to-all | bytes 1441792 | tf_op jit(solution)/shard_map/all_to_all | solution.py:20
  72.5 4.2 %all-to-all-start.3 = ((f32[8,88,256]{2,1,0:T(8,128)}), f32[8,88,256]{2,1,0:T(8,128)}, u32[]{:S(2)}, u32[]{:S(2)}) async-start(f32[8,88,256]{2,1,0:T(8,128)} %bitcast.46), calls=%async_computation.3 | async-start | bytes 1441792 | tf_op jit(solution)/shard_map/all_to_all | solution.py:20
  76.7 1.2 reduce_sum.18
  77.9 0.1 collective-permute-start.4
  78.0 1.3 collective-permute-done.4
  79.3 0.3 collective-permute-start.5
  79.6 5.7 %collective-permute-done.5 = f32[88,256]{1,0:T(8,128)S(1)} collective-permute-done((f32[88,256]{1,0:T(8,128)S(1)}, f32[88,256]{1,0:T(8,128)S(1)}, u32[]{:S(2)}, u32[]{:S(2)}) %collective-permute-start.5) | collective-permute-done | bytes 90144 | tf_op jit(solution)/shard_map/ppermute | solution.py:23
  85.3 5.1 %collective-permute-start.6 = (f32[88,256]{1,0:T(8,128)S(1)}, f32[88,256]{1,0:T(8,128)S(1)}, u32[]{:S(2)}, u32[]{:S(2)}) collective-permute-start(f32[88,256]{1,0:T(8,128)S(1)} %add.28), channel_id=1, source_target_pairs={{0,128},{32,160},{64,192},{96,224},{128,0},{160,32},{192,64},{224,... | collective-permute-start | bytes 270344 | tf_op jit(solution)/shard_map/ppermute | solution.py:23
  90.4 4.8 %collective-permute-done.6 = f32[88,256]{1,0:T(8,128)S(1)} collective-permute-done((f32[88,256]{1,0:T(8,128)S(1)}, f32[88,256]{1,0:T(8,128)S(1)}, u32[]{:S(2)}, u32[]{:S(2)}) %collective-permute-start.6) | collective-permute-done | bytes 90144 | tf_op jit(solution)/shard_map/ppermute | solution.py:23
  95.2 0.9 broadcast_in_dim.6
  96.2 8.0 %all-to-all-start.2 = ((f32[8,88,256]{2,1,0:T(8,128)}), f32[8,88,256]{2,1,0:T(8,128)}, u32[]{:S(2)}, u32[]{:S(2)}) async-start(f32[8,88,256]{2,1,0:T(8,128)} %broadcast_in_dim.6), calls=%async_computation.2 | async-start | bytes 1441792 | tf_op jit(solution)/shard_map/all_to_all | solution.py:25
  104.1 1.2 reduce_sum.19
  105.3 0.1 collective-permute-start.7
  105.4 1.3 collective-permute-done.7
  106.7 0.1 collective-permute-start.8
  106.8 5.7 %collective-permute-done.8 = f32[88,256]{1,0:T(8,128)S(1)} collective-permute-done((f32[88,256]{1,0:T(8,128)S(1)}, f32[88,256]{1,0:T(8,128)S(1)}, u32[]{:S(2)}, u32[]{:S(2)}) %collective-permute-start.8) | collective-permute-done | bytes 90144 | tf_op jit(solution)/shard_map/ppermute | solution.py:23
  112.4 3.6 %collective-permute-start.9 = (f32[88,256]{1,0:T(8,128)S(1)}, f32[88,256]{1,0:T(8,128)S(1)}, u32[]{:S(2)}, u32[]{:S(2)}) collective-permute-start(f32[88,256]{1,0:T(8,128)S(1)} %add.31), channel_id=1, source_target_pairs={{0,128},{32,160},{64,192},{96,224},{128,0},{160,32},{192,64},{224,... | collective-permute-start | bytes 270344 | tf_op jit(solution)/shard_map/ppermute | solution.py:23
  116.0 6.2 %collective-permute-done.9 = f32[88,256]{1,0:T(8,128)S(1)} collective-permute-done((f32[88,256]{1,0:T(8,128)S(1)}, f32[88,256]{1,0:T(8,128)S(1)}, u32[]{:S(2)}, u32[]{:S(2)}) %collective-permute-start.9) | collective-permute-done | bytes 90144 | tf_op jit(solution)/shard_map/ppermute | solution.py:23
  122.3 17.7 %all_to_all.59 = f32[8,88,256]{2,1,0:T(8,128)S(1)} all-to-all(f32[8,88,256]{2,1,0:T(8,128)S(1)} %broadcast_in_dim.7), channel_id=1, replica_groups=mesh['prow'=8,'x'=4,'zl'=2,'y'=4] {'x','zl'}, dimensions={0} | all-to-all | bytes 1441792 | tf_op jit(solution)/shard_map/all_to_all | solution.py:25
  140.0 0.9 copy-done.1
  140.9 1.7 pad_maximum_fusion.1
  142.6 1.1 reshape.29
  143.7 1.2 fusion.23
  144.9 0.4 fusion.33
  145.3 1.2 fusion.25
  146.5 0.4 fusion.31
  146.9 1.3 convolution_subtract_fusion.3
  148.3 1.1 fusion.37
  149.4 0.4 fusion.28
  149.8 1.3 convolution_subtract_fusion.2
  151.2 0.4 convolution_subtract_fusion.1
  151.6 1.1 fusion.35
  152.7 7.0 %convolution_subtract_fusion = f32[512,1536]{1,0:T(8,128)S(1)} fusion(f32[512,1536]{1,0:T(8,128)S(1)} %bitcast.40, f32[3072,512]{1,0:T(8,128)} %copy-done, s32[]{:T(128)S(6)} %select_n.11, f32[512,128]{0,1:T(8,128)S(1)} %fusion.23, f32[512,128]{0,1:T(8,128)S(1)} %fusion.25, f32[512,128]{0,1:T(8,128)S(1)} %fusion.37, f32[512,128]{0,1:T(8,128)S(1)} %fusion.35), kind=kOutput, calls=%fused_computation | convolution fusion | flops 2417491968 | bytes 10485764 | tf_op jit(solution)/shard_map/dot_general | solution.py:13
  159.7 38.2 %all_to_all.60 = f32[8,64,1536]{2,1,0:T(8,128)S(1)} all-to-all(f32[8,64,1536]{2,1,0:T(8,128)S(1)} %bitcast.41), channel_id=1, replica_groups=mesh['prow'=8,'x'=4,'zl'=2,'y'=4] {'x','zl'}, dimensions={0} | all-to-all | bytes 6291456 | tf_op jit(solution)/shard_map/all_to_all | solution.py:76
  197.9 1.9 copy.9
  (25 shorter events, 0.2 us)
Async XLA Ops:
  3.8 48.3 %all-to-all-start = ((f32[64,8,1536]{2,0,1:T(8,128)}), f32[64,8,1536]{2,0,1:T(8,128)S(1)}, u32[]{:S(2)}, u32[]{:S(2)}) async-start(f32[64,8,1536]{2,0,1:T(8,128)} %bitcast.37), calls=%async_computation | async-start | bytes 6291456 | tf_op jit(solution)/shard_map/all_to_all | solution.py:51
  9.5 20.5 %collective-permute-start.1 = (f32[384,512]{1,0:T(8,128)}, f32[384,512]{1,0:T(8,128)S(1)}, u32[]{:S(2)}, u32[]{:S(2)}) collective-permute-start(f32[384,512]{1,0:T(8,128)} %param.4), channel_id=1, source_target_pairs={{0,1},{1,2},{2,3},{3,0},{4,5},{5,6},{6,7},{7,4},{8,9},{9,10},{10,1... | collective-permute-start | bytes 2359304 | tf_op jit(solution)/shard_map/ppermute | solution.py:32
  11.1 20.9 %collective-permute-start = (f32[384,512]{1,0:T(8,128)}, f32[384,512]{1,0:T(8,128)S(1)}, u32[]{:S(2)}, u32[]{:S(2)}) collective-permute-start(f32[384,512]{1,0:T(8,128)} %param.4), channel_id=1, source_target_pairs={{0,3},{1,0},{2,1},{3,2},{4,7},{5,4},{6,5},{7,6},{8,11},{9,8},{10,9... | collective-permute-start | bytes 2359304 | tf_op jit(solution)/shard_map/ppermute | solution.py:33
  30.0 0.9 copy-start.2
  31.6 11.2 %collective-permute-start.2 = (f32[192,512]{1,0:T(8,128)}, f32[192,512]{1,0:T(8,128)S(1)}, u32[]{:S(2)}, u32[]{:S(2)}) collective-permute-start(f32[192,512]{1,0:T(8,128)} %slice.100), channel_id=1, source_target_pairs={{0,1},{1,2},{2,3},{3,0},{4,5},{5,6},{6,7},{7,4},{8,9},{9,10},{10,1... | collective-permute-start | bytes 1179656 | tf_op jit(solution)/shard_map/ppermute | solution.py:35
  31.9 0.9 copy-start.4
  33.6 10.2 %collective-permute-start.3 = (f32[192,512]{1,0:T(8,128)}, f32[192,512]{1,0:T(8,128)}, u32[]{:S(2)}, u32[]{:S(2)}) collective-permute-start(f32[192,512]{1,0:T(8,128)} %slice.101), channel_id=1, source_target_pairs={{0,3},{1,0},{2,1},{3,2},{4,7},{5,4},{6,5},{7,6},{8,11},{9,8},{10,9... | collective-permute-start | bytes 1179656 | tf_op jit(solution)/shard_map/ppermute | solution.py:36
  36.6 9.5 %copy-start.6 = (f32[384,512]{1,0:T(8,128)S(1)}, f32[384,512]{1,0:T(8,128)}, u32[]{:S(2)}) copy-start(f32[384,512]{1,0:T(8,128)} %param.4) | copy-start | bytes 2359300
  36.6 9.6 %copy-start.5 = (f32[384,512]{1,0:T(8,128)S(1)}, f32[384,512]{1,0:T(8,128)}, u32[]{:S(2)}) copy-start(f32[384,512]{1,0:T(8,128)} %copy-done.4) | copy-start | bytes 2359300
  36.6 10.7 %copy-start.3 = (f32[384,512]{1,0:T(8,128)S(1)}, f32[384,512]{1,0:T(8,128)}, u32[]{:S(2)}) copy-start(f32[384,512]{1,0:T(8,128)} %copy-done.2) | copy-start | bytes 2359300
  47.3 2.7 %copy-start = (f32[3072,512]{1,0:T(8,128)}, f32[3072,512]{1,0:T(8,128)S(1)}, u32[]{:S(2)}) copy-start(f32[3072,512]{1,0:T(8,128)S(1)} %constant_dynamic-update-slice_fusion) | copy-start | bytes 18874372
  52.2 4.6 %copy-start.7 = (f32[192,512]{1,0:T(8,128)S(1)}, f32[192,512]{1,0:T(8,128)}, u32[]{:S(2)}) copy-start(f32[192,512]{1,0:T(8,128)} %reshape.24) | copy-start | bytes 1179652
  72.5 22.7 %all-to-all-start.3 = ((f32[8,88,256]{2,1,0:T(8,128)}), f32[8,88,256]{2,1,0:T(8,128)}, u32[]{:S(2)}, u32[]{:S(2)}) async-start(f32[8,88,256]{2,1,0:T(8,128)} %bitcast.46), calls=%async_computation.3 | async-start | bytes 1441792 | tf_op jit(solution)/shard_map/all_to_all | solution.py:20
  77.9 1.4 collective-permute-start.4
  79.3 5.9 %collective-permute-start.5 = (f32[88,256]{1,0:T(8,128)S(1)}, f32[88,256]{1,0:T(8,128)S(1)}, u32[]{:S(2)}, u32[]{:S(2)}) collective-permute-start(f32[88,256]{1,0:T(8,128)S(1)} %add.27), channel_id=1, source_target_pairs={{0,64},{32,96},{64,0},{96,32},{128,192},{160,224},{192,128},{224,1... | collective-permute-start | bytes 270344 | tf_op jit(solution)/shard_map/ppermute | solution.py:23
  85.3 10.0 %collective-permute-start.6 = (f32[88,256]{1,0:T(8,128)S(1)}, f32[88,256]{1,0:T(8,128)S(1)}, u32[]{:S(2)}, u32[]{:S(2)}) collective-permute-start(f32[88,256]{1,0:T(8,128)S(1)} %add.28), channel_id=1, source_target_pairs={{0,128},{32,160},{64,192},{96,224},{128,0},{160,32},{192,64},{224,... | collective-permute-start | bytes 270344 | tf_op jit(solution)/shard_map/ppermute | solution.py:23
  96.2 26.1 %all-to-all-start.2 = ((f32[8,88,256]{2,1,0:T(8,128)}), f32[8,88,256]{2,1,0:T(8,128)}, u32[]{:S(2)}, u32[]{:S(2)}) async-start(f32[8,88,256]{2,1,0:T(8,128)} %broadcast_in_dim.6), calls=%async_computation.2 | async-start | bytes 1441792 | tf_op jit(solution)/shard_map/all_to_all | solution.py:25
  105.3 1.4 collective-permute-start.7
  106.7 5.8 %collective-permute-start.8 = (f32[88,256]{1,0:T(8,128)S(1)}, f32[88,256]{1,0:T(8,128)S(1)}, u32[]{:S(2)}, u32[]{:S(2)}) collective-permute-start(f32[88,256]{1,0:T(8,128)S(1)} %add.30), channel_id=1, source_target_pairs={{0,64},{32,96},{64,0},{96,32},{128,192},{160,224},{192,128},{224,1... | collective-permute-start | bytes 270344 | tf_op jit(solution)/shard_map/ppermute | solution.py:23
  112.4 9.8 %collective-permute-start.9 = (f32[88,256]{1,0:T(8,128)S(1)}, f32[88,256]{1,0:T(8,128)S(1)}, u32[]{:S(2)}, u32[]{:S(2)}) collective-permute-start(f32[88,256]{1,0:T(8,128)S(1)} %add.31), channel_id=1, source_target_pairs={{0,128},{32,160},{64,192},{96,224},{128,0},{160,32},{192,64},{224,... | collective-permute-start | bytes 270344 | tf_op jit(solution)/shard_map/ppermute | solution.py:23
  140.0 0.9 copy-start.1

commit v8 on v7

--- a/solution.py
+++ b/solution.py
@@ -54,8 +54,7 @@
     grams = jnp.concatenate([matmul(basis[:, j * width : (j + 1) * width].T, basis[:, : j * width]) for j in range(1, count)], axis=1)
     lanes = products.shape[1]
     packed = jnp.concatenate([products, grams.reshape(-1, lanes)], axis=0)
-    half = lanes // 2
-    packed = jnp.concatenate([all_reduce(packed[:, :half], GROUP, "prow", ng, nprow), all_reduce(packed[:, half:], GROUP, "prow", ng, nprow)], axis=1)
+    packed = all_reduce(packed, GROUP, "prow", ng, nprow)
     span = products.shape[0]
     products = [packed[:span, k * width : (k + 1) * width] for k in range(count)]
     grams = packed[span:].reshape(grams.shape)

time: 202 us -> 191 us (0.946)
  blocking collectives: 70.7 us -> 86.6 us
  starting transfers between devices: 33.5 us -> 18.2 us
  waiting for transfers between devices: 46.9 us -> 38.7 us
  other arithmetic: 5.09 us -> 1.71 us
    all_to_all x2 -> x0, starting transfers between devices: 12.2 us -> none  [the longest x1 7.96 us: all_reduce(): lax.all_to_all(jnp.broadcast_to(total, (outer_size, chunk, lanes)), outer...]
    ppermute x6 -> x3, waiting for transfers between devices: 24.9 us -> 16.7 us  [all_reduce(): lax.ppermute(total, inner, [(i, i ^ bit) for i in range(inner_size)])]
    all_to_all x1, blocking collectives: 17.7 us -> 25.5 us  [all_reduce(): lax.all_to_all(jnp.broadcast_to(total, (outer_size, chunk, lanes)), outer...]
    all_to_all x1, blocking collectives: 14.8 us -> 22.4 us  [all_reduce(): total = jnp.sum(lax.all_to_all(packed, outer, 0, 0, tiled=True), axis=0)]
    ppermute x6 -> x3, starting transfers between devices: 9.26 us -> 6.11 us  [all_reduce(): lax.ppermute(total, inner, [(i, i ^ bit) for i in range(inner_size)])]
  transfers between devices with their start and end apart: 13 -> 8, of which waited for: 9 -> 6; matrix products, arithmetic and copies ran while one was open for 7% -> 6% of each run, Pallas kernels for 0% -> 0%
where the time goes in v8:
time: 191 us; the launch traced here: 189 us
  blocking collectives  86.6 us (45%)
  waiting for transfers between devices  38.7 us (20%)
  matrix products  24 us (13%)
  local copies, waits for them, and re-layouts  19.6 us (10%)
  starting transfers between devices  18.2 us (10%)
    all_to_all x1, blocking collectives, per_device(): return lax.all_to_all(work, GROUP, 0, 1, tiled=True)  38.7 us
    all_to_all x1, blocking collectives, all_reduce(): lax.all_to_all(jnp.broadcast_to(total, (outer_size, chunk, lanes)), outer...  25.5 us
    dot_general x15, matrix products, matmul(): jnp.dot(left, right, precision=lax.Precision.HIGH, preferred_element_type...  24 us
    all_to_all x1, blocking collectives, all_reduce(): total = jnp.sum(lax.all_to_all(packed, outer, 0, 0, tiled=True), axis=0)  22.4 us
    ppermute x1, waiting for transfers between devices, gather_ring(): from_left = lax.ppermute(block, axis, right)  17.2 us
    ppermute x3, waiting for transfers between devices, all_reduce(): lax.ppermute(total, inner, [(i, i ^ bit) for i in range(inner_size)])  16.7 us
    unnamed x25, local copies, waits for them, and re-layouts  9.34 us
    ppermute x3, starting transfers between devices, all_reduce(): lax.ppermute(total, inner, [(i, i ^ bit) for i in range(inner_size)])  6.11 us
  transfers between devices with their start and end apart: 8, of which 6 were waited for; matrix products, arithmetic and copies ran while one was open for 6% of the time, Pallas kernels for 0%

profile of v8, /device:TPU:64, one launch (start us, length us, event | category | flops | bytes accessed | tf_op | source)
XLA Modules:
  0.0 189.1 jit_solution(13509307486756295943)
XLA Ops:
  0.0 3.8 %copy.11 = f32[8,8,8,1536]{3,2,0,1:T(8,128)} copy(f32[8,8,8,1536]{3,2,1,0:T(8,128)} %bitcast.46) | data formatting | bytes 6291456 | tf_op jit(solution)/shard_map/all_to_all | solution.py:51
  3.8 5.7 %all-to-all-start = ((f32[64,8,1536]{2,0,1:T(8,128)}), f32[64,8,1536]{2,0,1:T(8,128)S(1)}, u32[]{:S(2)}, u32[]{:S(2)}) async-start(f32[64,8,1536]{2,0,1:T(8,128)} %bitcast.35), calls=%async_computation | async-start | bytes 6291456 | tf_op jit(solution)/shard_map/all_to_all | solution.py:51
  9.5 1.6 collective-permute-start.1
  11.1 1.7 collective-permute-start
  12.7 17.2 %collective-permute-done.1 = f32[384,512]{1,0:T(8,128)S(1)} collective-permute-done((f32[384,512]{1,0:T(8,128)}, f32[384,512]{1,0:T(8,128)S(1)}, u32[]{:S(2)}, u32[]{:S(2)}) %collective-permute-start.1) | collective-permute-done | bytes 786464 | tf_op jit(solution)/shard_map/ppermute | solution.py:32
  30.0 0.0 copy-start.2
  30.0 0.9 copy-done.2
  30.9 0.8 slice.92
  31.7 0.3 collective-permute-start.2
  32.0 0.0 collective-permute-done
  32.0 0.0 copy-start.4
  32.0 0.9 copy-done.4
  32.9 0.8 slice.93
  33.7 2.9 %collective-permute-start.3 = (f32[192,512]{1,0:T(8,128)}, f32[192,512]{1,0:T(8,128)}, u32[]{:S(2)}, u32[]{:S(2)}) collective-permute-start(f32[192,512]{1,0:T(8,128)} %slice.93), channel_id=1, source_target_pairs={{0,3},{1,0},{2,1},{3,2},{4,7},{5,4},{6,5},{7,6},{8,11},{9,8},{10,9... | collective-permute-start | bytes 1179656 | tf_op jit(solution)/shard_map/ppermute | solution.py:36
  36.6 0.0 copy-start.6
  36.6 1.3 constant_dynamic-update-slice_fusion.9
  37.9 1.2 constant_dynamic-update-slice_fusion.8
  39.1 3.7 %collective-permute-done.2 = f32[192,512]{1,0:T(8,128)S(1)} collective-permute-done((f32[192,512]{1,0:T(8,128)}, f32[192,512]{1,0:T(8,128)S(1)}, u32[]{:S(2)}, u32[]{:S(2)}) %collective-permute-start.2) | collective-permute-done | bytes 393248 | tf_op jit(solution)/shard_map/ppermute | solution.py:35
  42.8 1.0 collective-permute-done.3
  43.9 1.0 constant_dynamic-update-slice_fusion.6
  44.9 1.2 constant_dynamic-update-slice_fusion.5
  46.1 0.0 copy-done.6
  46.1 0.1 constant_dynamic-update-slice_fusion.4
  46.2 0.0 copy-done.5
  46.2 0.1 constant_dynamic-update-slice_fusion.3
  46.3 1.0 constant_dynamic-update-slice_fusion.1
  47.3 0.0 copy-done.3
  47.3 0.1 constant_dynamic-update-slice_fusion
  47.4 0.0 copy-start
  47.4 1.1 fusion.19
  48.5 1.1 fusion.5
  49.6 0.5 copy-done
  50.0 1.2 fusion.3
  51.3 0.9 reshape.18
  52.2 0.0 all-to-all-done
  52.2 4.6 %fusion.7 = f32[512,512]{1,0:T(8,128)S(1)} fusion(f32[512,1536]{1,0:T(8,128)S(1)} %bitcast.37, f32[3072,512]{1,0:T(8,128)} %copy-done, s32[]{:T(128)S(6)} %select_n.11), kind=kOutput, calls=%fused_computation.10 | convolution fusion | flops 2415919104 | bytes 7340036 | tf_op jit(solution)/shard_map/dot_general | solution.py:13
  56.8 0.0 copy-done.7
  56.8 0.1 pad_maximum_fusion
  56.9 22.4 %all_to_all.48 = f32[8,88,512]{2,1,0:T(8,128)} all-to-all(f32[8,88,512]{2,1,0:T(8,128)S(1)} %bitcast.45), channel_id=1, replica_groups=mesh['prow'=8,'x'=4,'zl'=2,'y'=4] {'x','zl'}, dimensions={0} | all-to-all | bytes 2883584 | tf_op jit(solution)/shard_map/all_to_all | solution.py:20
  79.4 1.5 reduce_sum.9
  80.9 0.1 collective-permute-start.4
  81.0 1.4 collective-permute-done.4
  82.4 0.1 collective-permute-start.5
  82.5 8.2 %collective-permute-done.5 = f32[88,512]{1,0:T(8,128)S(1)} collective-permute-done((f32[88,512]{1,0:T(8,128)S(1)}, f32[88,512]{1,0:T(8,128)S(1)}, u32[]{:S(2)}, u32[]{:S(2)}) %collective-permute-start.5) | collective-permute-done | bytes 180256 | tf_op jit(solution)/shard_map/ppermute | solution.py:23
  90.8 5.9 %collective-permute-start.6 = (f32[88,512]{1,0:T(8,128)S(1)}, f32[88,512]{1,0:T(8,128)S(1)}, u32[]{:S(2)}, u32[]{:S(2)}) collective-permute-start(f32[88,512]{1,0:T(8,128)S(1)} %add.19), channel_id=1, source_target_pairs={{0,128},{32,160},{64,192},{96,224},{128,0},{160,32},{192,64},{224,... | collective-permute-start | bytes 540680 | tf_op jit(solution)/shard_map/ppermute | solution.py:23
  96.7 7.1 %collective-permute-done.6 = f32[88,512]{1,0:T(8,128)S(1)} collective-permute-done((f32[88,512]{1,0:T(8,128)S(1)}, f32[88,512]{1,0:T(8,128)S(1)}, u32[]{:S(2)}, u32[]{:S(2)}) %collective-permute-start.6) | collective-permute-done | bytes 180256 | tf_op jit(solution)/shard_map/ppermute | solution.py:23
  103.8 0.2 broadcast_in_dim.3
  104.0 25.5 %all_to_all.49 = f32[8,88,512]{2,1,0:T(8,128)S(1)} all-to-all(f32[8,88,512]{2,1,0:T(8,128)S(1)} %broadcast_in_dim.3), channel_id=1, replica_groups=mesh['prow'=8,'x'=4,'zl'=2,'y'=4] {'x','zl'}, dimensions={0} | all-to-all | bytes 2883584 | tf_op jit(solution)/shard_map/all_to_all | solution.py:25
  129.5 1.1 copy-done.1
  130.6 0.8 slice.98
  131.4 1.1 reshape.21
  132.5 1.2 fusion.22
  133.7 0.4 fusion.32
  134.1 1.2 fusion.24
  135.4 0.4 fusion.30
  135.8 1.3 convolution_subtract_fusion.3
  137.1 1.1 fusion.36
  138.2 0.4 fusion.27
  138.6 1.3 convolution_subtract_fusion.2
  140.0 0.4 convolution_subtract_fusion.1
  140.4 1.1 fusion.34
  141.5 7.0 %convolution_subtract_fusion = f32[512,1536]{1,0:T(8,128)S(1)} fusion(f32[512,1536]{1,0:T(8,128)S(1)} %bitcast.38, f32[3072,512]{1,0:T(8,128)} %copy-done, s32[]{:T(128)S(6)} %select_n.11, f32[512,128]{0,1:T(8,128)S(1)} %fusion.22, f32[512,128]{0,1:T(8,128)S(1)} %fusion.24, f32[512,128]{0,1:T(8,128)S(1)} %fusion.36, f32[512,128]{0,1:T(8,128)S(1)} %fusion.34), kind=kOutput, calls=%fused_computation | convolution fusion | flops 2417491968 | bytes 10485764 | tf_op jit(solution)/shard_map/dot_general | solution.py:13
  148.5 38.7 %all_to_all.50 = f32[8,64,1536]{2,1,0:T(8,128)S(1)} all-to-all(f32[8,64,1536]{2,1,0:T(8,128)S(1)} %bitcast.39), channel_id=1, replica_groups=mesh['prow'=8,'x'=4,'zl'=2,'y'=4] {'x','zl'}, dimensions={0} | all-to-all | bytes 6291456 | tf_op jit(solution)/shard_map/all_to_all | solution.py:75
  187.2 1.9 %copy.9 = f32[8,8,8,1536]{3,2,0,1:T(8,128)} copy(f32[8,8,8,1536]{3,2,1,0:T(8,128)S(1)} %bitcast.36) | data formatting | bytes 6291456 | tf_op jit(solution)/shard_map/all_to_all | solution.py:75
  (10 shorter events, 0.2 us)
Async XLA Ops:
  3.8 48.3 %all-to-all-start = ((f32[64,8,1536]{2,0,1:T(8,128)}), f32[64,8,1536]{2,0,1:T(8,128)S(1)}, u32[]{:S(2)}, u32[]{:S(2)}) async-start(f32[64,8,1536]{2,0,1:T(8,128)} %bitcast.35), calls=%async_computation | async-start | bytes 6291456 | tf_op jit(solution)/shard_map/all_to_all | solution.py:51
  9.5 20.5 %collective-permute-start.1 = (f32[384,512]{1,0:T(8,128)}, f32[384,512]{1,0:T(8,128)S(1)}, u32[]{:S(2)}, u32[]{:S(2)}) collective-permute-start(f32[384,512]{1,0:T(8,128)} %param.4), channel_id=1, source_target_pairs={{0,1},{1,2},{2,3},{3,0},{4,5},{5,6},{6,7},{7,4},{8,9},{9,10},{10,1... | collective-permute-start | bytes 2359304 | tf_op jit(solution)/shard_map/ppermute | solution.py:32
  11.1 20.9 %collective-permute-start = (f32[384,512]{1,0:T(8,128)}, f32[384,512]{1,0:T(8,128)S(1)}, u32[]{:S(2)}, u32[]{:S(2)}) collective-permute-start(f32[384,512]{1,0:T(8,128)} %param.4), channel_id=1, source_target_pairs={{0,3},{1,0},{2,1},{3,2},{4,7},{5,4},{6,5},{7,6},{8,11},{9,8},{10,9... | collective-permute-start | bytes 2359304 | tf_op jit(solution)/shard_map/ppermute | solution.py:33
  30.0 0.9 copy-start.2
  31.7 11.2 %collective-permute-start.2 = (f32[192,512]{1,0:T(8,128)}, f32[192,512]{1,0:T(8,128)S(1)}, u32[]{:S(2)}, u32[]{:S(2)}) collective-permute-start(f32[192,512]{1,0:T(8,128)} %slice.92), channel_id=1, source_target_pairs={{0,1},{1,2},{2,3},{3,0},{4,5},{5,6},{6,7},{7,4},{8,9},{9,10},{10,1... | collective-permute-start | bytes 1179656 | tf_op jit(solution)/shard_map/ppermute | solution.py:35
  32.0 0.9 copy-start.4
  33.7 10.2 %collective-permute-start.3 = (f32[192,512]{1,0:T(8,128)}, f32[192,512]{1,0:T(8,128)}, u32[]{:S(2)}, u32[]{:S(2)}) collective-permute-start(f32[192,512]{1,0:T(8,128)} %slice.93), channel_id=1, source_target_pairs={{0,3},{1,0},{2,1},{3,2},{4,7},{5,4},{6,5},{7,6},{8,11},{9,8},{10,9... | collective-permute-start | bytes 1179656 | tf_op jit(solution)/shard_map/ppermute | solution.py:36
  36.6 9.5 %copy-start.6 = (f32[384,512]{1,0:T(8,128)S(1)}, f32[384,512]{1,0:T(8,128)}, u32[]{:S(2)}) copy-start(f32[384,512]{1,0:T(8,128)} %param.4) | copy-start | bytes 2359300
  36.6 9.6 %copy-start.5 = (f32[384,512]{1,0:T(8,128)S(1)}, f32[384,512]{1,0:T(8,128)}, u32[]{:S(2)}) copy-start(f32[384,512]{1,0:T(8,128)} %copy-done.4) | copy-start | bytes 2359300
  36.6 10.7 %copy-start.3 = (f32[384,512]{1,0:T(8,128)S(1)}, f32[384,512]{1,0:T(8,128)}, u32[]{:S(2)}) copy-start(f32[384,512]{1,0:T(8,128)} %copy-done.2) | copy-start | bytes 2359300
  47.4 2.6 %copy-start = (f32[3072,512]{1,0:T(8,128)}, f32[3072,512]{1,0:T(8,128)S(1)}, u32[]{:S(2)}) copy-start(f32[3072,512]{1,0:T(8,128)S(1)} %constant_dynamic-update-slice_fusion) | copy-start | bytes 18874372
  52.2 4.6 %copy-start.7 = (f32[192,512]{1,0:T(8,128)S(1)}, f32[192,512]{1,0:T(8,128)}, u32[]{:S(2)}) copy-start(f32[192,512]{1,0:T(8,128)} %reshape.18) | copy-start | bytes 1179652
  80.9 1.5 collective-permute-start.4
  82.4 8.3 %collective-permute-start.5 = (f32[88,512]{1,0:T(8,128)S(1)}, f32[88,512]{1,0:T(8,128)S(1)}, u32[]{:S(2)}, u32[]{:S(2)}) collective-permute-start(f32[88,512]{1,0:T(8,128)S(1)} %add.18), channel_id=1, source_target_pairs={{0,64},{32,96},{64,0},{96,32},{128,192},{160,224},{192,128},{224,1... | collective-permute-start | bytes 540680 | tf_op jit(solution)/shard_map/ppermute | solution.py:23
  90.8 13.0 %collective-permute-start.6 = (f32[88,512]{1,0:T(8,128)S(1)}, f32[88,512]{1,0:T(8,128)S(1)}, u32[]{:S(2)}, u32[]{:S(2)}) collective-permute-start(f32[88,512]{1,0:T(8,128)S(1)} %add.19), channel_id=1, source_target_pairs={{0,128},{32,160},{64,192},{96,224},{128,0},{160,32},{192,64},{224,... | collective-permute-start | bytes 540680 | tf_op jit(solution)/shard_map/ppermute | solution.py:23
  129.5 1.1 copy-start.1

commit v9 on v8

--- a/solution.py
+++ b/solution.py
@@ -71,8 +71,14 @@
         scaled[k] = matmul(part, tfactors[k].T)
     scaled = jnp.concatenate(scaled, axis=1)
 
-    work = work - matmul(scaled, basis.T)
-    return lax.all_to_all(work, GROUP, 0, 1, tiled=True)
+    work = work.reshape(ng, rows, -1)
+    scaled = scaled.reshape(ng, rows, -1)
+    half = rows // 2
+    outs = []
+    for part in (slice(0, half), slice(half, rows)):
+        piece = work[:, part] - matmul(scaled[:, part].reshape(ng * half, -1), basis.T).reshape(ng, half, -1)
+        outs.append(lax.all_to_all(piece, GROUP, 0, 2, tiled=True).reshape(half, cols))
+    return jnp.concatenate(outs, axis=0)
 
 
 def solution(mesh):

time: 191 us -> 200 us (1.047)
  blocking collectives: 86.6 us -> 48 us
  waiting for transfers between devices: 38.7 us -> 70.8 us
  starting transfers between devices: 18.2 us -> 26.1 us
  other arithmetic: 1.71 us -> 4.62 us
  matrix products: 24 us -> 26.5 us
    all_to_all x1 -> x0, blocking collectives: 38.7 us -> none  [per_device(): return lax.all_to_all(work, GROUP, 0, 1, tiled=True)]
    all_to_all x0 -> x2, waiting for transfers between devices: none -> 32.2 us  [per_device(): lax.all_to_all(piece, GROUP, 0, 2, tiled=True).reshape(half, cols)]
    all_to_all x0 -> x2, starting transfers between devices: none -> 7.88 us  [per_device(): lax.all_to_all(piece, GROUP, 0, 2, tiled=True).reshape(half, cols)]
    concatenate x0 -> x2, other arithmetic: none -> 2.91 us  [the longest x1 1.87 us: per_device(): return jnp.concatenate(outs, axis=0)]
    concatenate x0 -> x1, local copies, waits for them, and re-layouts: none -> 2.56 us  [per_device(): scaled = jnp.concatenate(scaled, axis=1)]
    dot_general x15 -> x16, matrix products: 24 us -> 26.5 us  [matmul(): jnp.dot(left, right, precision=lax.Precision.HIGH, preferred_element_type...]
    unnamed x25 -> x31, local copies, waits for them, and re-layouts: 9.34 us -> 8.68 us
  transfers between devices with their start and end apart: 8 -> 10, of which waited for: 6 -> 8; matrix products, arithmetic and copies ran while one was open for 6% -> 9% of each run, Pallas kernels for 0% -> 0%
where the time goes in v9:
time: 200 us; the launch traced here: 197 us
  waiting for transfers between devices  70.8 us (35%)
  blocking collectives  48 us (24%)
  matrix products  26.5 us (13%)
  starting transfers between devices  26.1 us (13%)
  local copies, waits for them, and re-layouts  20.4 us (10%)
  other arithmetic  4.62 us (2%)
    all_to_all x2, waiting for transfers between devices, per_device(): lax.all_to_all(piece, GROUP, 0, 2, tiled=True).reshape(half, cols)  32.2 us
    dot_general x16, matrix products, matmul(): jnp.dot(left, right, precision=lax.Precision.HIGH, preferred_element_type...  26.5 us
    all_to_all x1, blocking collectives, all_reduce(): lax.all_to_all(jnp.broadcast_to(total, (outer_size, chunk, lanes)), outer...  25.5 us
    all_to_all x1, blocking collectives, all_reduce(): total = jnp.sum(lax.all_to_all(packed, outer, 0, 0, tiled=True), axis=0)  22.4 us
    ppermute x1, waiting for transfers between devices, gather_ring(): from_left = lax.ppermute(block, axis, right)  17.2 us
    ppermute x3, waiting for transfers between devices, all_reduce(): lax.ppermute(total, inner, [(i, i ^ bit) for i in range(inner_size)])  16.7 us
    unnamed x31, local copies, waits for them, and re-layouts  8.68 us
    all_to_all x2, starting transfers between devices, per_device(): lax.all_to_all(piece, GROUP, 0, 2, tiled=True).reshape(half, cols)  7.88 us
  transfers between devices with their start and end apart: 10, of which 8 were waited for; matrix products, arithmetic and copies ran while one was open for 9% of the time, Pallas kernels for 0%

profile of v9, /device:TPU:64, one launch (start us, length us, event | category | flops | bytes accessed | tf_op | source)
XLA Modules:
  0.0 196.7 jit_solution(12122892583457331127)
XLA Ops:
  0.0 3.8 %copy.19 = f32[8,8,8,1536]{3,2,0,1:T(8,128)} copy(f32[8,8,8,1536]{3,2,1,0:T(8,128)} %bitcast.72) | data formatting | bytes 6291456 | tf_op jit(solution)/shard_map/all_to_all | solution.py:51
  3.8 5.7 %all-to-all-start = ((f32[64,8,1536]{2,0,1:T(8,128)}), f32[64,8,1536]{2,0,1:T(8,128)S(1)}, u32[]{:S(2)}, u32[]{:S(2)}) async-start(f32[64,8,1536]{2,0,1:T(8,128)} %bitcast.57), calls=%async_computation | async-start | bytes 6291456 | tf_op jit(solution)/shard_map/all_to_all | solution.py:51
  9.5 1.6 collective-permute-start.1
  11.1 1.7 collective-permute-start
  12.7 17.2 %collective-permute-done.1 = f32[384,512]{1,0:T(8,128)S(1)} collective-permute-done((f32[384,512]{1,0:T(8,128)}, f32[384,512]{1,0:T(8,128)S(1)}, u32[]{:S(2)}, u32[]{:S(2)}) %collective-permute-start.1) | collective-permute-done | bytes 786464 | tf_op jit(solution)/shard_map/ppermute | solution.py:32
  30.0 0.9 copy-done.2
  30.8 0.8 slice.109
  31.6 0.3 collective-permute-start.2
  31.9 0.0 collective-permute-done
  31.9 0.9 copy-done.4
  32.8 0.8 slice.110
  33.6 2.9 %collective-permute-start.3 = (f32[192,512]{1,0:T(8,128)}, f32[192,512]{1,0:T(8,128)}, u32[]{:S(2)}, u32[]{:S(2)}) collective-permute-start(f32[192,512]{1,0:T(8,128)} %slice.110), channel_id=1, source_target_pairs={{0,3},{1,0},{2,1},{3,2},{4,7},{5,4},{6,5},{7,6},{8,11},{9,8},{10,9... | collective-permute-start | bytes 1179656 | tf_op jit(solution)/shard_map/ppermute | solution.py:36
  36.6 1.3 constant_dynamic-update-slice_fusion.9
  37.9 1.3 constant_dynamic-update-slice_fusion.8
  39.1 3.6 %collective-permute-done.2 = f32[192,512]{1,0:T(8,128)S(1)} collective-permute-done((f32[192,512]{1,0:T(8,128)}, f32[192,512]{1,0:T(8,128)S(1)}, u32[]{:S(2)}, u32[]{:S(2)}) %collective-permute-start.2) | collective-permute-done | bytes 393248 | tf_op jit(solution)/shard_map/ppermute | solution.py:35
  42.8 1.1 collective-permute-done.3
  43.9 1.0 constant_dynamic-update-slice_fusion.6
  44.9 0.0 copy-done.3
  44.9 0.1 constant_dynamic-update-slice_fusion.5
  45.0 0.1 constant_dynamic-update-slice_fusion.4
  45.0 0.1 constant_dynamic-update-slice_fusion.3
  45.1 1.0 constant_dynamic-update-slice_fusion.1
  46.2 0.1 constant_dynamic-update-slice_fusion
  46.2 1.1 fusion.23
  47.3 1.1 fusion.16
  48.4 1.2 fusion.14
  49.7 0.9 reshape.36
  50.5 0.0 all-to-all-done
  50.6 4.6 %fusion.18 = f32[512,512]{1,0:T(8,128)S(1)} fusion(f32[512,1536]{1,0:T(8,128)S(1)} %bitcast.58, f32[3072,512]{1,0:T(8,128)} %copy-done, s32[]{:T(128)S(6)} %select_n.11), kind=kOutput, calls=%fused_computation.17 | convolution fusion | flops 2415919104 | bytes 7340036 | tf_op jit(solution)/shard_map/dot_general | solution.py:13
  55.2 0.1 pad_maximum_fusion.1
  55.3 22.4 %all_to_all.59 = f32[8,88,512]{2,1,0:T(8,128)} all-to-all(f32[8,88,512]{2,1,0:T(8,128)S(1)} %bitcast.69), channel_id=1, replica_groups=mesh['prow'=8,'x'=4,'zl'=2,'y'=4] {'x','zl'}, dimensions={0} | all-to-all | bytes 2883584 | tf_op jit(solution)/shard_map/all_to_all | solution.py:20
  77.7 1.5 reduce_sum.9
  79.2 0.1 collective-permute-start.4
  79.3 1.4 collective-permute-done.4
  80.8 0.1 collective-permute-start.5
  80.9 8.2 %collective-permute-done.5 = f32[88,512]{1,0:T(8,128)S(1)} collective-permute-done((f32[88,512]{1,0:T(8,128)S(1)}, f32[88,512]{1,0:T(8,128)S(1)}, u32[]{:S(2)}, u32[]{:S(2)}) %collective-permute-start.5) | collective-permute-done | bytes 180256 | tf_op jit(solution)/shard_map/ppermute | solution.py:23
  89.2 5.9 %collective-permute-start.6 = (f32[88,512]{1,0:T(8,128)S(1)}, f32[88,512]{1,0:T(8,128)S(1)}, u32[]{:S(2)}, u32[]{:S(2)}) collective-permute-start(f32[88,512]{1,0:T(8,128)S(1)} %add.19), channel_id=1, source_target_pairs={{0,128},{32,160},{64,192},{96,224},{128,0},{160,32},{192,64},{224,... | collective-permute-start | bytes 540680 | tf_op jit(solution)/shard_map/ppermute | solution.py:23
  95.1 7.1 %collective-permute-done.6 = f32[88,512]{1,0:T(8,128)S(1)} collective-permute-done((f32[88,512]{1,0:T(8,128)S(1)}, f32[88,512]{1,0:T(8,128)S(1)}, u32[]{:S(2)}, u32[]{:S(2)}) %collective-permute-start.6) | collective-permute-done | bytes 180256 | tf_op jit(solution)/shard_map/ppermute | solution.py:23
  102.2 0.2 broadcast_in_dim.3
  102.3 25.5 %all_to_all.60 = f32[8,88,512]{2,1,0:T(8,128)S(1)} all-to-all(f32[8,88,512]{2,1,0:T(8,128)S(1)} %broadcast_in_dim.3), channel_id=1, replica_groups=mesh['prow'=8,'x'=4,'zl'=2,'y'=4] {'x','zl'}, dimensions={0} | all-to-all | bytes 2883584 | tf_op jit(solution)/shard_map/all_to_all | solution.py:25
  127.9 0.8 slice.115
  128.7 0.4 copy-done.1
  129.1 1.1 fusion.28
  130.2 1.9 reshape.39
  132.1 1.3 fusion.38
  133.4 1.2 fusion.30
  134.6 1.2 fusion.36
  135.9 1.4 convolution_subtract_fusion.2
  137.3 0.3 fusion.42
  137.6 0.4 fusion.33
  138.0 1.3 convolution_subtract_fusion.1
  139.3 0.4 convolution_subtract_fusion
  139.7 0.3 fusion.40
  140.0 1.0 pad_maximum_fusion.2
  141.1 2.6 %copy.9 = f32[512,512]{1,0:T(8,128)} copy(f32[512,512]{0,1:T(8,128)} %pad_maximum_fusion.2) | data formatting | bytes 2097152 | tf_op jit(solution)/shard_map/concatenate | solution.py:72
  143.6 4.7 %fusion.7 = f32[8,32,1536]{2,1,0:T(8,128)} fusion(f32[3072,512]{1,0:T(8,128)} %copy-done, s32[]{:T(128)S(6)} %select_n.11, f32[8,64,1536]{2,1,0:T(8,128)S(1)} %bitcast.59, f32[8,64,512]{2,1,0:T(8,128)} %bitcast.70), kind=kOutput, calls=%fused_computation.7 | convolution fusion | flops 1208352768 | bytes 6815748 | tf_op jit(solution)/shard_map/dot_general | solution.py:13
  148.3 4.3 %all-to-all-start.4 = ((f32[8,32,1536]{2,1,0:T(8,128)}), f32[8,32,1536]{2,1,0:T(8,128)}, u32[]{:S(2)}, u32[]{:S(2)}) async-start(f32[8,32,1536]{2,1,0:T(8,128)} %fusion.7), calls=%async_computation.4 | async-start | bytes 3145728 | tf_op jit(solution)/shard_map/all_to_all | solution.py:80
  152.6 4.8 %fusion.4 = f32[8,32,1536]{2,1,0:T(8,128)} fusion(f32[3072,512]{1,0:T(8,128)} %copy-done, s32[]{:T(128)S(6)} %select_n.11, f32[8,64,1536]{2,1,0:T(8,128)S(1)} %bitcast.60, f32[8,64,512]{2,1,0:T(8,128)} %bitcast.71), kind=kOutput, calls=%fused_computation.6 | convolution fusion | flops 1208352768 | bytes 6815748 | tf_op jit(solution)/shard_map/dot_general | solution.py:13
  157.4 14.5 %all-to-all-done.4 = f32[8,32,1536]{2,1,0:T(8,128)} async-done(((f32[8,32,1536]{2,1,0:T(8,128)}), f32[8,32,1536]{2,1,0:T(8,128)}, u32[]{:S(2)}, u32[]{:S(2)}) %all-to-all-start.4) | async-done | bytes 1572896 | tf_op jit(solution)/shard_map/all_to_all | solution.py:80
  171.9 3.6 %all-to-all-start.3 = ((f32[8,32,1536]{2,1,0:T(8,128)}), f32[8,32,1536]{2,1,0:T(8,128)S(1)}, u32[]{:S(2)}, u32[]{:S(2)}) async-start(f32[8,32,1536]{2,1,0:T(8,128)} %fusion.4), calls=%async_computation.3 | async-start | bytes 3145728 | tf_op jit(solution)/shard_map/all_to_all | solution.py:80
  175.5 1.5 copy.15
  177.0 17.7 %all-to-all-done.3 = f32[8,32,1536]{2,1,0:T(8,128)S(1)} async-done(((f32[8,32,1536]{2,1,0:T(8,128)}), f32[8,32,1536]{2,1,0:T(8,128)S(1)}, u32[]{:S(2)}, u32[]{:S(2)}) %all-to-all-start.3) | async-done | bytes 1572896 | tf_op jit(solution)/shard_map/all_to_all | solution.py:80
  194.7 0.1 copy.14
  194.9 1.9 pad_maximum_fusion
  (22 shorter events, 0.2 us)
Async XLA Ops:
  3.8 46.7 %all-to-all-start = ((f32[64,8,1536]{2,0,1:T(8,128)}), f32[64,8,1536]{2,0,1:T(8,128)S(1)}, u32[]{:S(2)}, u32[]{:S(2)}) async-start(f32[64,8,1536]{2,0,1:T(8,128)} %bitcast.57), calls=%async_computation | async-start | bytes 6291456 | tf_op jit(solution)/shard_map/all_to_all | solution.py:51
  9.5 20.5 %collective-permute-start.1 = (f32[384,512]{1,0:T(8,128)}, f32[384,512]{1,0:T(8,128)S(1)}, u32[]{:S(2)}, u32[]{:S(2)}) collective-permute-start(f32[384,512]{1,0:T(8,128)} %param.4), channel_id=1, source_target_pairs={{0,1},{1,2},{2,3},{3,0},{4,5},{5,6},{6,7},{7,4},{8,9},{9,10},{10,1... | collective-permute-start | bytes 2359304 | tf_op jit(solution)/shard_map/ppermute | solution.py:32
  11.1 20.9 %collective-permute-start = (f32[384,512]{1,0:T(8,128)}, f32[384,512]{1,0:T(8,128)S(1)}, u32[]{:S(2)}, u32[]{:S(2)}) collective-permute-start(f32[384,512]{1,0:T(8,128)} %param.4), channel_id=1, source_target_pairs={{0,3},{1,0},{2,1},{3,2},{4,7},{5,4},{6,5},{7,6},{8,11},{9,8},{10,9... | collective-permute-start | bytes 2359304 | tf_op jit(solution)/shard_map/ppermute | solution.py:33
  30.0 0.9 copy-start.2
  31.6 11.2 %collective-permute-start.2 = (f32[192,512]{1,0:T(8,128)}, f32[192,512]{1,0:T(8,128)S(1)}, u32[]{:S(2)}, u32[]{:S(2)}) collective-permute-start(f32[192,512]{1,0:T(8,128)} %slice.109), channel_id=1, source_target_pairs={{0,1},{1,2},{2,3},{3,0},{4,5},{5,6},{6,7},{7,4},{8,9},{9,10},{10,1... | collective-permute-start | bytes 1179656 | tf_op jit(solution)/shard_map/ppermute | solution.py:35
  31.9 0.9 copy-start.4
  33.6 10.2 %collective-permute-start.3 = (f32[192,512]{1,0:T(8,128)}, f32[192,512]{1,0:T(8,128)}, u32[]{:S(2)}, u32[]{:S(2)}) collective-permute-start(f32[192,512]{1,0:T(8,128)} %slice.110), channel_id=1, source_target_pairs={{0,3},{1,0},{2,1},{3,2},{4,7},{5,4},{6,5},{7,6},{8,11},{9,8},{10,9... | collective-permute-start | bytes 1179656 | tf_op jit(solution)/shard_map/ppermute | solution.py:36
  36.6 8.3 %copy-start.3 = (f32[384,512]{1,0:T(8,128)S(1)}, f32[384,512]{1,0:T(8,128)}, u32[]{:S(2)}) copy-start(f32[384,512]{1,0:T(8,128)} %copy-done.2) | copy-start | bytes 2359300
  36.6 8.4 %copy-start.6 = (f32[384,512]{1,0:T(8,128)S(1)}, f32[384,512]{1,0:T(8,128)}, u32[]{:S(2)}) copy-start(f32[384,512]{1,0:T(8,128)} %param.4) | copy-start | bytes 2359300
  37.9 7.1 %copy-start.5 = (f32[384,512]{1,0:T(8,128)S(1)}, f32[384,512]{1,0:T(8,128)}, u32[]{:S(2)}) copy-start(f32[384,512]{1,0:T(8,128)} %copy-done.4) | copy-start | bytes 2359300
  46.2 3.4 %copy-start = (f32[3072,512]{1,0:T(8,128)}, f32[3072,512]{1,0:T(8,128)S(1)}, u32[]{:S(2)}) copy-start(f32[3072,512]{1,0:T(8,128)S(1)} %constant_dynamic-update-slice_fusion) | copy-start | bytes 18874372
  50.5 4.6 %copy-start.8 = (f32[192,512]{1,0:T(8,128)S(1)}, f32[192,512]{1,0:T(8,128)}, u32[]{:S(2)}) copy-start(f32[192,512]{1,0:T(8,128)} %reshape.36) | copy-start | bytes 1179652
  79.2 1.5 collective-permute-start.4
  80.8 8.3 %collective-permute-start.5 = (f32[88,512]{1,0:T(8,128)S(1)}, f32[88,512]{1,0:T(8,128)S(1)}, u32[]{:S(2)}, u32[]{:S(2)}) collective-permute-start(f32[88,512]{1,0:T(8,128)S(1)} %add.18), channel_id=1, source_target_pairs={{0,64},{32,96},{64,0},{96,32},{128,192},{160,224},{192,128},{224,1... | collective-permute-start | bytes 540680 | tf_op jit(solution)/shard_map/ppermute | solution.py:23
  89.2 13.0 %collective-permute-start.6 = (f32[88,512]{1,0:T(8,128)S(1)}, f32[88,512]{1,0:T(8,128)S(1)}, u32[]{:S(2)}, u32[]{:S(2)}) collective-permute-start(f32[88,512]{1,0:T(8,128)S(1)} %add.19), channel_id=1, source_target_pairs={{0,128},{32,160},{64,192},{96,224},{128,0},{160,32},{192,64},{224,... | collective-permute-start | bytes 540680 | tf_op jit(solution)/shard_map/ppermute | solution.py:23
  127.9 1.2 copy-start.1
  132.1 5.2 %copy-start.9 = (f32[4,128,128]{2,1,0:T(8,128)S(1)}, f32[4,128,128]{2,1,0:T(8,128)}, u32[]{:S(2)}) copy-start(f32[4,128,128]{2,1,0:T(8,128)} %param.5) | copy-start | bytes 786436
  132.1 5.5 %copy-start.7 = (f32[128,768]{1,0:T(8,128)S(1)}, f32[128,768]{1,0:T(8,128)}, u32[]{:S(2)}) copy-start(f32[128,768]{1,0:T(8,128)} %reshape.39) | copy-start | bytes 1179652
  148.3 23.6 %all-to-all-start.4 = ((f32[8,32,1536]{2,1,0:T(8,128)}), f32[8,32,1536]{2,1,0:T(8,128)}, u32[]{:S(2)}, u32[]{:S(2)}) async-start(f32[8,32,1536]{2,1,0:T(8,128)} %fusion.7), calls=%async_computation.4 | async-start | bytes 3145728 | tf_op jit(solution)/shard_map/all_to_all | solution.py:80
  171.9 22.8 %all-to-all-start.3 = ((f32[8,32,1536]{2,1,0:T(8,128)}), f32[8,32,1536]{2,1,0:T(8,128)S(1)}, u32[]{:S(2)}, u32[]{:S(2)}) async-start(f32[8,32,1536]{2,1,0:T(8,128)} %fusion.4), calls=%async_computation.3 | async-start | bytes 3145728 | tf_op jit(solution)/shard_map/all_to_all | solution.py:80

commit v10 on v8

--- a/solution.py
+++ b/solution.py
@@ -56,19 +56,24 @@
     packed = jnp.concatenate([products, grams.reshape(-1, lanes)], axis=0)
     packed = all_reduce(packed, GROUP, "prow", ng, nprow)
     span = products.shape[0]
-    products = [packed[:span, k * width : (k + 1) * width] for k in range(count)]
     grams = packed[span:].reshape(grams.shape)
     gram, offset = {}, 0
     for j in range(1, count):
         for k in range(j):
             gram[j, k], offset = grams[:, offset : offset + width], offset + width
 
+    diagonal = jnp.zeros((count * width, count * width), tfactors.dtype)
+    for k in range(count):
+        diagonal = diagonal.at[k * width : (k + 1) * width, k * width : (k + 1) * width].set(tfactors[k].T)
+    products = matmul(packed[:span], diagonal)
     scaled = [None] * count
     for k in reversed(range(count)):
-        part = products[k]
-        for j in range(k + 1, count):
-            part = part - matmul(scaled[j], gram[j, k])
-        scaled[k] = matmul(part, tfactors[k].T)
+        part = products[:, k * width : (k + 1) * width]
+        if k + 1 < count:
+            later = list(range(count - 1, k, -1))
+            weights = matmul(jnp.concatenate([gram[j, k] for j in later], axis=0), tfactors[k].T)
+            part = part - matmul(jnp.concatenate([scaled[j] for j in later], axis=1), weights)
+        scaled[k] = part
     scaled = jnp.concatenate(scaled, axis=1)
 
     work = work - matmul(scaled, basis.T)

time: 191 us -> 193 us (1.010)
  blocking collectives: 86.6 us -> 62.8 us
  waiting for transfers between devices: 38.7 us -> 51 us
  local copies, waits for them, and re-layouts: 19.6 us -> 28.1 us
  starting transfers between devices: 18.2 us -> 25 us
  matrix products: 24 us -> 20.9 us
    all_to_all x1 -> x0, blocking collectives: 25.5 us -> none  [all_reduce(): lax.all_to_all(jnp.broadcast_to(total, (outer_size, chunk, lanes)), outer...]
    all_to_all x0 -> x1, waiting for transfers between devices: none -> 12.3 us  [all_reduce(): lax.all_to_all(jnp.broadcast_to(total, (outer_size, chunk, lanes)), outer...]
    all_to_all x0 -> x1, starting transfers between devices: none -> 6.74 us  [all_reduce(): lax.all_to_all(jnp.broadcast_to(total, (outer_size, chunk, lanes)), outer...]
    scatter x0 -> x4, local copies, waits for them, and re-layouts: none -> 5.6 us  [per_device(): diagonal.at[k * width:(k + 1) * width, k * width:(k + 1) * width]]
    dot_general x15 -> x12, matrix products: 24 us -> 20.9 us  [matmul(): jnp.dot(left, right, precision=lax.Precision.HIGH, preferred_element_type...]
    unnamed x25 -> x31, local copies, waits for them, and re-layouts: 9.34 us -> 8.23 us
  transfers between devices with their start and end apart: 8 -> 9, of which waited for: 6 -> 7; matrix products, arithmetic and copies ran while one was open for 6% -> 10% of each run, Pallas kernels for 0% -> 0%
where the time goes in v10:
time: 193 us; the launch traced here: 190 us
  blocking collectives  62.8 us (33%)
  waiting for transfers between devices  51 us (26%)
  local copies, waits for them, and re-layouts  28.1 us (15%)
  starting transfers between devices  25 us (13%)
  matrix products  20.9 us (11%)
    all_to_all x1, blocking collectives, per_device(): return lax.all_to_all(work, GROUP, 0, 1, tiled=True)  40.4 us
    all_to_all x1, blocking collectives, all_reduce(): total = jnp.sum(lax.all_to_all(packed, outer, 0, 0, tiled=True), axis=0)  22.4 us
    dot_general x12, matrix products, matmul(): jnp.dot(left, right, precision=lax.Precision.HIGH, preferred_element_type...  20.9 us
    ppermute x1, waiting for transfers between devices, gather_ring(): from_left = lax.ppermute(block, axis, right)  17.2 us
    ppermute x3, waiting for transfers between devices, all_reduce(): lax.ppermute(total, inner, [(i, i ^ bit) for i in range(inner_size)])  16.7 us
    all_to_all x1, waiting for transfers between devices, all_reduce(): lax.all_to_all(jnp.broadcast_to(total, (outer_size, chunk, lanes)), outer...  12.3 us
    unnamed x31, local copies, waits for them, and re-layouts  8.23 us
    all_to_all x1, starting transfers between devices, all_reduce(): lax.all_to_all(jnp.broadcast_to(total, (outer_size, chunk, lanes)), outer...  6.74 us
  transfers between devices with their start and end apart: 9, of which 7 were waited for; matrix products, arithmetic and copies ran while one was open for 10% of the time, Pallas kernels for 0%

profile of v10, /device:TPU:64, one launch (start us, length us, event | category | flops | bytes accessed | tf_op | source)
XLA Modules:
  0.0 189.7 jit_solution(1508684718695557595)
XLA Ops:
  0.0 3.8 %copy.11 = f32[8,8,8,1536]{3,2,0,1:T(8,128)} copy(f32[8,8,8,1536]{3,2,1,0:T(8,128)} %bitcast.51) | data formatting | bytes 6291456 | tf_op jit(solution)/shard_map/all_to_all | solution.py:51
  3.8 5.7 %all-to-all-start = ((f32[64,8,1536]{2,0,1:T(8,128)}), f32[64,8,1536]{2,0,1:T(8,128)S(1)}, u32[]{:S(2)}, u32[]{:S(2)}) async-start(f32[64,8,1536]{2,0,1:T(8,128)} %bitcast.41), calls=%async_computation | async-start | bytes 6291456 | tf_op jit(solution)/shard_map/all_to_all | solution.py:51
  9.5 1.6 collective-permute-start.1
  11.1 1.7 collective-permute-start
  12.7 17.2 %collective-permute-done.1 = f32[384,512]{1,0:T(8,128)S(1)} collective-permute-done((f32[384,512]{1,0:T(8,128)}, f32[384,512]{1,0:T(8,128)S(1)}, u32[]{:S(2)}, u32[]{:S(2)}) %collective-permute-start.1) | collective-permute-done | bytes 786464 | tf_op jit(solution)/shard_map/ppermute | solution.py:32
  30.0 0.9 copy-done.3
  30.9 0.8 slice.182
  31.6 0.3 collective-permute-start.2
  31.9 0.0 collective-permute-done
  32.0 0.9 copy-done.5
  32.9 0.8 slice.183
  33.6 2.9 %collective-permute-start.3 = (f32[192,512]{1,0:T(8,128)}, f32[192,512]{1,0:T(8,128)}, u32[]{:S(2)}, u32[]{:S(2)}) collective-permute-start(f32[192,512]{1,0:T(8,128)} %slice.183), channel_id=1, source_target_pairs={{0,3},{1,0},{2,1},{3,2},{4,7},{5,4},{6,5},{7,6},{8,11},{9,8},{10,9... | collective-permute-start | bytes 1179656 | tf_op jit(solution)/shard_map/ppermute | solution.py:36
  36.6 1.3 constant_dynamic-update-slice_fusion.9
  37.9 1.2 constant_dynamic-update-slice_fusion.8
  39.1 3.7 %collective-permute-done.2 = f32[192,512]{1,0:T(8,128)S(1)} collective-permute-done((f32[192,512]{1,0:T(8,128)}, f32[192,512]{1,0:T(8,128)S(1)}, u32[]{:S(2)}, u32[]{:S(2)}) %collective-permute-start.2) | collective-permute-done | bytes 393248 | tf_op jit(solution)/shard_map/ppermute | solution.py:35
  42.8 1.0 collective-permute-done.3
  43.9 1.0 constant_dynamic-update-slice_fusion.6
  44.9 1.2 constant_dynamic-update-slice_fusion.5
  46.1 0.0 copy-done.7
  46.1 0.1 constant_dynamic-update-slice_fusion.4
  46.2 0.0 copy-done.6
  46.2 0.1 constant_dynamic-update-slice_fusion.3
  46.3 1.0 constant_dynamic-update-slice_fusion.1
  47.3 0.0 copy-done.4
  47.3 0.1 constant_dynamic-update-slice_fusion
  47.4 0.0 copy-start
  47.4 1.1 fusion.21
  48.4 1.1 fusion.5
  49.5 0.5 copy-done
  50.0 1.2 fusion.3
  51.3 0.9 reshape.133
  52.1 0.0 all-to-all-done
  52.1 5.7 %fusion.7 = f32[512,512]{1,0:T(8,128)S(1)} fusion(f32[512,1536]{1,0:T(8,128)S(1)} %bitcast.45, f32[3072,512]{1,0:T(8,128)} %copy-done, s32[]{:T(128)S(6)} %select_n.11), kind=kOutput, calls=%fused_computation.10 | convolution fusion | flops 2415919104 | bytes 7340036 | tf_op jit(solution)/shard_map/dot_general | solution.py:13
  57.9 0.1 pad_maximum_fusion
  58.0 22.4 %all_to_all.48 = f32[8,88,512]{2,1,0:T(8,128)} all-to-all(f32[8,88,512]{2,1,0:T(8,128)S(1)} %bitcast.50), channel_id=1, replica_groups=mesh['prow'=8,'x'=4,'zl'=2,'y'=4] {'x','zl'}, dimensions={0} | all-to-all | bytes 2883584 | tf_op jit(solution)/shard_map/all_to_all | solution.py:20
  80.4 1.5 reduce_sum.9
  81.9 0.1 collective-permute-start.4
  82.0 1.4 collective-permute-done.4
  83.5 0.1 collective-permute-start.5
  83.6 8.2 %collective-permute-done.5 = f32[88,512]{1,0:T(8,128)S(1)} collective-permute-done((f32[88,512]{1,0:T(8,128)S(1)}, f32[88,512]{1,0:T(8,128)S(1)}, u32[]{:S(2)}, u32[]{:S(2)}) %collective-permute-start.5) | collective-permute-done | bytes 180256 | tf_op jit(solution)/shard_map/ppermute | solution.py:23
  91.9 5.9 %collective-permute-start.6 = (f32[88,512]{1,0:T(8,128)S(1)}, f32[88,512]{1,0:T(8,128)S(1)}, u32[]{:S(2)}, u32[]{:S(2)}) collective-permute-start(f32[88,512]{1,0:T(8,128)S(1)} %add.29), channel_id=1, source_target_pairs={{0,128},{32,160},{64,192},{96,224},{128,0},{160,32},{192,64},{224,... | collective-permute-start | bytes 540680 | tf_op jit(solution)/shard_map/ppermute | solution.py:23
  97.8 7.1 %collective-permute-done.6 = f32[88,512]{1,0:T(8,128)S(1)} collective-permute-done((f32[88,512]{1,0:T(8,128)S(1)}, f32[88,512]{1,0:T(8,128)S(1)}, u32[]{:S(2)}, u32[]{:S(2)}) %collective-permute-start.6) | collective-permute-done | bytes 180256 | tf_op jit(solution)/shard_map/ppermute | solution.py:23
  104.9 1.3 broadcast_in_dim.4
  106.2 6.7 %all-to-all-start.2 = ((f32[8,88,512]{2,1,0:T(8,128)}), f32[8,88,512]{2,1,0:T(8,128)S(1)}, u32[]{:S(2)}, u32[]{:S(2)}) async-start(f32[8,88,512]{2,1,0:T(8,128)} %broadcast_in_dim.4), calls=%async_computation.2 | async-start | bytes 2883584 | tf_op jit(solution)/shard_map/all_to_all | solution.py:25
  112.9 1.0 slice_bitcast_fusion
  113.9 1.2 scatter.14
  115.1 1.5 bitcast_dynamic-update-slice_fusion.2
  116.6 1.5 bitcast_dynamic-update-slice_fusion.1
  118.0 1.5 bitcast_dynamic-update-slice_fusion
  119.5 12.3 %all-to-all-done.2 = f32[8,88,512]{2,1,0:T(8,128)S(1)} async-done(((f32[8,88,512]{2,1,0:T(8,128)}), f32[8,88,512]{2,1,0:T(8,128)S(1)}, u32[]{:S(2)}, u32[]{:S(2)}) %all-to-all-start.2) | async-done | bytes 1441824 | tf_op jit(solution)/shard_map/all_to_all | solution.py:25
  131.8 0.8 slice.188
  132.5 1.8 reshape.136
  134.4 1.1 fusion.61
  135.5 1.1 fusion.42
  136.6 0.0 slice-start.1
  136.6 2.4 %fusion.10 = f32[512,512]{0,1:T(8,128)S(1)} fusion(f32[512,512]{0,1:T(8,128)} %bitcast_dynamic-update-slice_fusion, f32[704,512]{1,0:T(8,128)S(1)} %bitcast.49), kind=kOutput, calls=%fused_computation.14 | convolution fusion | flops 805306368 | bytes 3145728 | tf_op jit(solution)/shard_map/dot_general | solution.py:13
  139.1 0.3 convolution_subtract_fusion.2
  139.4 1.1 fusion.38
  140.5 1.1 fusion.32
  141.6 0.3 convolution_subtract_fusion.1
  141.9 0.4 convolution_subtract_fusion.3
  142.3 5.1 %convolution_subtract_fusion = f32[512,1536]{1,0:T(8,128)S(1)} fusion(f32[512,1536]{1,0:T(8,128)S(1)} %bitcast.46, f32[3072,512]{1,0:T(8,128)S(1)} %bitcast.43, s32[]{:T(128)S(6)} %select_n.11, f32[512,128]{0,1:T(8,128)S(1)} %slice.186, f32[512,128]{0,1:T(8,128)S(1)} %convolution_subtract_fusion.2, f32[512,128]{0,1:T(8,128)S(1)} %convolution_subtract_fusion.1, ...), kind=kOutput, calls=%fused_computation | convolution fusion | flops 2417491968 | bytes 10485764 | tf_op jit(solution)/shard_map/dot_general | solution.py:13
  147.5 40.4 %all_to_all.49 = f32[8,64,1536]{2,1,0:T(8,128)S(1)} all-to-all(f32[8,64,1536]{2,1,0:T(8,128)S(1)} %bitcast.47), channel_id=1, replica_groups=mesh['prow'=8,'x'=4,'zl'=2,'y'=4] {'x','zl'}, dimensions={0} | all-to-all | bytes 6291456 | tf_op jit(solution)/shard_map/all_to_all | solution.py:80
  187.8 1.9 copy.9
  (22 shorter events, 0.2 us)
Async XLA Ops:
  3.8 48.3 %all-to-all-start = ((f32[64,8,1536]{2,0,1:T(8,128)}), f32[64,8,1536]{2,0,1:T(8,128)S(1)}, u32[]{:S(2)}, u32[]{:S(2)}) async-start(f32[64,8,1536]{2,0,1:T(8,128)} %bitcast.41), calls=%async_computation | async-start | bytes 6291456 | tf_op jit(solution)/shard_map/all_to_all | solution.py:51
  9.5 20.5 %collective-permute-start.1 = (f32[384,512]{1,0:T(8,128)}, f32[384,512]{1,0:T(8,128)S(1)}, u32[]{:S(2)}, u32[]{:S(2)}) collective-permute-start(f32[384,512]{1,0:T(8,128)} %param.12), channel_id=1, source_target_pairs={{0,1},{1,2},{2,3},{3,0},{4,5},{5,6},{6,7},{7,4},{8,9},{9,10},{10,1... | collective-permute-start | bytes 2359304 | tf_op jit(solution)/shard_map/ppermute | solution.py:32
  11.1 20.9 %collective-permute-start = (f32[384,512]{1,0:T(8,128)}, f32[384,512]{1,0:T(8,128)S(1)}, u32[]{:S(2)}, u32[]{:S(2)}) collective-permute-start(f32[384,512]{1,0:T(8,128)} %param.12), channel_id=1, source_target_pairs={{0,3},{1,0},{2,1},{3,2},{4,7},{5,4},{6,5},{7,6},{8,11},{9,8},{10,9... | collective-permute-start | bytes 2359304 | tf_op jit(solution)/shard_map/ppermute | solution.py:33
  30.0 0.9 copy-start.3
  31.6 11.2 %collective-permute-start.2 = (f32[192,512]{1,0:T(8,128)}, f32[192,512]{1,0:T(8,128)S(1)}, u32[]{:S(2)}, u32[]{:S(2)}) collective-permute-start(f32[192,512]{1,0:T(8,128)} %slice.182), channel_id=1, source_target_pairs={{0,1},{1,2},{2,3},{3,0},{4,5},{5,6},{6,7},{7,4},{8,9},{9,10},{10,1... | collective-permute-start | bytes 1179656 | tf_op jit(solution)/shard_map/ppermute | solution.py:35
  31.9 0.9 copy-start.5
  33.6 10.2 %collective-permute-start.3 = (f32[192,512]{1,0:T(8,128)}, f32[192,512]{1,0:T(8,128)}, u32[]{:S(2)}, u32[]{:S(2)}) collective-permute-start(f32[192,512]{1,0:T(8,128)} %slice.183), channel_id=1, source_target_pairs={{0,3},{1,0},{2,1},{3,2},{4,7},{5,4},{6,5},{7,6},{8,11},{9,8},{10,9... | collective-permute-start | bytes 1179656 | tf_op jit(solution)/shard_map/ppermute | solution.py:36
  36.6 9.5 %copy-start.7 = (f32[384,512]{1,0:T(8,128)S(1)}, f32[384,512]{1,0:T(8,128)}, u32[]{:S(2)}) copy-start(f32[384,512]{1,0:T(8,128)} %param.12) | copy-start | bytes 2359300
  36.6 9.6 %copy-start.6 = (f32[384,512]{1,0:T(8,128)S(1)}, f32[384,512]{1,0:T(8,128)}, u32[]{:S(2)}) copy-start(f32[384,512]{1,0:T(8,128)} %copy-done.5) | copy-start | bytes 2359300
  36.6 10.7 %copy-start.4 = (f32[384,512]{1,0:T(8,128)S(1)}, f32[384,512]{1,0:T(8,128)}, u32[]{:S(2)}) copy-start(f32[384,512]{1,0:T(8,128)} %copy-done.3) | copy-start | bytes 2359300
  47.4 2.7 %copy-start = (f32[3072,512]{1,0:T(8,128)}, f32[3072,512]{1,0:T(8,128)S(1)}, u32[]{:S(2)}) copy-start(f32[3072,512]{1,0:T(8,128)S(1)} %constant_dynamic-update-slice_fusion) | copy-start | bytes 18874372
  52.1 5.7 %copy-start.8 = (f32[192,512]{1,0:T(8,128)S(1)}, f32[192,512]{1,0:T(8,128)}, u32[]{:S(2)}) copy-start(f32[192,512]{1,0:T(8,128)} %reshape.133) | copy-start | bytes 1179652
  52.1 28.3 %copy-start.1 = (f32[64,8,1536]{2,0,1:T(8,128)}, f32[64,8,1536]{2,0,1:T(8,128)S(1)}, u32[]{:S(2)}) copy-start(f32[64,8,1536]{2,0,1:T(8,128)S(1)} %all-to-all-done) | copy-start | bytes 9437188
  81.9 1.5 collective-permute-start.4
  83.5 8.3 %collective-permute-start.5 = (f32[88,512]{1,0:T(8,128)S(1)}, f32[88,512]{1,0:T(8,128)S(1)}, u32[]{:S(2)}, u32[]{:S(2)}) collective-permute-start(f32[88,512]{1,0:T(8,128)S(1)} %add.28), channel_id=1, source_target_pairs={{0,64},{32,96},{64,0},{96,32},{128,192},{160,224},{192,128},{224,1... | collective-permute-start | bytes 540680 | tf_op jit(solution)/shard_map/ppermute | solution.py:23
  91.9 13.0 %collective-permute-start.6 = (f32[88,512]{1,0:T(8,128)S(1)}, f32[88,512]{1,0:T(8,128)S(1)}, u32[]{:S(2)}, u32[]{:S(2)}) collective-permute-start(f32[88,512]{1,0:T(8,128)S(1)} %add.29), channel_id=1, source_target_pairs={{0,128},{32,160},{64,192},{96,224},{128,0},{160,32},{192,64},{224,... | collective-permute-start | bytes 540680 | tf_op jit(solution)/shard_map/ppermute | solution.py:23
  106.2 25.6 %all-to-all-start.2 = ((f32[8,88,512]{2,1,0:T(8,128)}), f32[8,88,512]{2,1,0:T(8,128)S(1)}, u32[]{:S(2)}, u32[]{:S(2)}) async-start(f32[8,88,512]{2,1,0:T(8,128)} %broadcast_in_dim.4), calls=%async_computation.2 | async-start | bytes 2883584 | tf_op jit(solution)/shard_map/all_to_all | solution.py:25
  112.9 29.4 %slice-start = ((s8[6291456]{0:T(1024)(128)(4,1)}), s8[2097152]{0:T(1024)(128)(4,1)S(1)}, s32[]{:S(2)}) async-start(s8[6291456]{0:T(1024)(128)(4,1)} %bitcast.42), calls=%async_computation.4 | async-start | bytes 4194304
  134.4 7.9 %copy-start.2 = (f32[64,8,1536]{2,0,1:T(8,128)S(1)}, f32[64,8,1536]{2,0,1:T(8,128)}, u32[]{:S(2)}) copy-start(f32[64,8,1536]{2,0,1:T(8,128)} %copy-done.1) | copy-start | bytes 9437188
  136.6 5.7 %slice-start.1 = ((s8[6291456]{0:T(1024)(128)(4,1)}), s8[4194304]{0:T(1024)(128)(4,1)S(1)}, s32[]{:S(2)}) async-start(s8[6291456]{0:T(1024)(128)(4,1)} %bitcast.42), calls=%async_computation.5 | async-start | bytes 8388608

commit v11 on v8

--- a/solution.py
+++ b/solution.py
@@ -34,10 +34,14 @@
     half = block.shape[0] // 2
     far_first = lax.ppermute(from_left[:half], axis, right)
     far_second = lax.ppermute(from_right[half:], axis, left)
-    ordered = jnp.concatenate([block, from_right, far_first, far_second, from_left], axis=0)
-    shift = lax.axis_index(axis) * block.shape[0]
-    ordered = jnp.concatenate([ordered, ordered], axis=0)
-    return lax.dynamic_slice_in_dim(ordered, (size * block.shape[0] - shift) % (size * block.shape[0]), size * block.shape[0], axis=0)
+    return jnp.concatenate([block, from_right, far_first, far_second, from_left], axis=0)
+
+
+def rotate(chunks, shift, size):
+    width = chunks.shape[-1]
+    doubled = jnp.concatenate([chunks, chunks], axis=-1)
+    start = ((size - shift) % size) * (width // size)
+    return lax.dynamic_slice_in_dim(doubled, start, width, axis=chunks.ndim - 1)
 
 
 def per_device(slab, vectors, tfactors):
@@ -47,8 +51,12 @@
     ng = PCOL_PARTS[0] * PCOL_PARTS[1]
     nprow = PROW_SIZE
 
-    basis = gather_ring(vectors, "y", PCOL_PARTS[2])
-    work = lax.all_to_all(slab, GROUP, 1, 0, tiled=True)
+    ny = PCOL_PARTS[2]
+    depth = vectors.shape[0]
+    turn = lax.axis_index("y")
+    basis = gather_ring(vectors, "y", ny)
+    work = rotate(slab.reshape(rows, ng, ny * depth), -turn, ny).reshape(rows, cols)
+    work = lax.all_to_all(work, GROUP, 1, 0, tiled=True)
 
     products = matmul(work, basis)
     grams = jnp.concatenate([matmul(basis[:, j * width : (j + 1) * width].T, basis[:, : j * width]) for j in range(1, count)], axis=1)
@@ -72,7 +80,8 @@
     scaled = jnp.concatenate(scaled, axis=1)
 
     work = work - matmul(scaled, basis.T)
-    return lax.all_to_all(work, GROUP, 0, 1, tiled=True)
+    work = lax.all_to_all(work, GROUP, 0, 1, tiled=True)
+    return rotate(work.reshape(rows, ng, ny * depth), turn, ny).reshape(rows, cols)
 
 
 def solution(mesh):

time: 191 us -> 188 us (0.984)
  waiting for transfers between devices: 38.7 us -> 79.5 us
  blocking collectives: 86.6 us -> 48.3 us
  local copies, waits for them, and re-layouts: 19.6 us -> 9.48 us
  starting transfers between devices: 18.2 us -> 22.1 us
  other arithmetic: 1.71 us -> 4.81 us
    all_to_all x1 -> x2, waiting for transfers between devices: 0.01 us -> 39.3 us  [the longest x1 36 us: per_device(): work = lax.all_to_all(work, GROUP, 0, 1, tiled=True)]
    all_to_all x1 -> x0, blocking collectives: 38.7 us -> none  [per_device(): return lax.all_to_all(work, GROUP, 0, 1, tiled=True)]
    unnamed x25 -> x12, local copies, waits for them, and re-layouts: 9.34 us -> 2.41 us
    all_to_all x2 -> x0, local copies, waits for them, and re-layouts: 5.76 us -> none  [the longest x1 3.82 us: per_device(): work = lax.all_to_all(slab, GROUP, 1, 0, tiled=True)]
    reshape x0 -> x2, local copies, waits for them, and re-layouts: none -> 4.09 us  [the longest x1 2.15 us: per_device(): slab.reshape(rows, ng, ny * depth)]
    all_to_all x1 -> x2, starting transfers between devices: 5.65 us -> 9.44 us  [the longest x1 5.79 us: per_device(): work = lax.all_to_all(work, GROUP, 1, 0, tiled=True)]
    ppermute x1, waiting for transfers between devices: 3.67 us -> 6.45 us  [gather_ring(): far_first = lax.ppermute(from_left[:half], axis, right)]
    concatenate x0 -> x1, other arithmetic: none -> 2.36 us  [rotate(): doubled = jnp.concatenate([chunks, chunks], axis=-1)]
  transfers between devices with their start and end apart: 8 -> 9, of which waited for: 6 -> 7; matrix products, arithmetic and copies ran while one was open for 6% -> 3% of each run, Pallas kernels for 0% -> 0%
where the time goes in v11:
time: 188 us; the launch traced here: 187 us
  waiting for transfers between devices  79.5 us (42%)
  blocking collectives  48.3 us (26%)
  matrix products  22.4 us (12%)
  starting transfers between devices  22.1 us (12%)
  local copies, waits for them, and re-layouts  9.48 us (5%)
  other arithmetic  4.81 us (3%)
    all_to_all x1, waiting for transfers between devices, per_device(): work = lax.all_to_all(work, GROUP, 0, 1, tiled=True)  36 us
    all_to_all x1, blocking collectives, all_reduce(): lax.all_to_all(jnp.broadcast_to(total, (outer_size, chunk, lanes)), outer...  25.5 us
    all_to_all x1, blocking collectives, all_reduce(): total = jnp.sum(lax.all_to_all(packed, outer, 0, 0, tiled=True), axis=0)  22.8 us
    dot_general x15, matrix products, matmul(): jnp.dot(left, right, precision=lax.Precision.HIGH, preferred_element_type...  22.4 us
    ppermute x1, waiting for transfers between devices, gather_ring(): from_left = lax.ppermute(block, axis, right)  17 us
    ppermute x3, waiting for transfers between devices, all_reduce(): lax.ppermute(total, inner, [(i, i ^ bit) for i in range(inner_size)])  16.7 us
    ppermute x1, waiting for transfers between devices, gather_ring(): far_first = lax.ppermute(from_left[:half], axis, right)  6.45 us
    ppermute x3, starting transfers between devices, all_reduce(): lax.ppermute(total, inner, [(i, i ^ bit) for i in range(inner_size)])  5.93 us
  transfers between devices with their start and end apart: 9, of which 7 were waited for; matrix products, arithmetic and copies ran while one was open for 3% of the time, Pallas kernels for 0%

profile of v11, /device:TPU:64, one launch (start us, length us, event | category | flops | bytes accessed | tf_op | source)
XLA Modules:
  0.0 186.9 jit_solution(16561271043669892040)
XLA Ops:
  0.0 2.2 %copy.12 = f32[8,8,8,1536]{3,2,0,1:T(8,128)S(1)} copy(f32[8,8,8,1536]{3,2,1,0:T(8,128)} %bitcast.46) | data formatting | bytes 6291456 | tf_op jit(solution)/shard_map/reshape | solution.py:58
  2.2 2.4 %fusion.2 = f32[64,8,1536]{2,0,1:T(8,128)} fusion(s32[]{:T(128)S(6)} %select_n.18, f32[64,8,1536]{2,0,1:T(8,128)S(1)} %bitcast.38), kind=kLoop, calls=%fused_computation.7 | loop fusion | flops 786432 | bytes 6291460 | tf_op jit(solution)/shard_map/concatenate | solution.py:42
  4.5 0.0 copy-start.2
  4.5 5.8 %all-to-all-start = ((f32[64,8,1536]{2,0,1:T(8,128)}), f32[64,8,1536]{2,0,1:T(8,128)}, u32[]{:S(2)}, u32[]{:S(2)}) async-start(f32[64,8,1536]{2,0,1:T(8,128)} %fusion.2), calls=%async_computation | async-start | bytes 6291456 | tf_op jit(solution)/shard_map/all_to_all | solution.py:59
  10.3 0.0 copy-done.2
  10.3 1.7 collective-permute-start.1
  12.0 1.7 collective-permute-start
  13.6 17.0 %collective-permute-done.1 = f32[384,512]{1,0:T(8,128)S(1)} collective-permute-done((f32[384,512]{1,0:T(8,128)S(1)}, f32[384,512]{1,0:T(8,128)S(1)}, u32[]{:S(2)}, u32[]{:S(2)}) %collective-permute-start.1) | collective-permute-done | bytes 786464 | tf_op jit(solution)/shard_map/ppermute | solution.py:32
  30.7 0.4 collective-permute-start.2
  31.1 0.0 collective-permute-done
  31.1 3.0 %collective-permute-start.3 = (f32[192,512]{1,0:T(8,128)S(1)}, f32[192,512]{1,0:T(8,128)S(1)}, u32[]{:S(2)}, u32[]{:S(2)}) collective-permute-start(f32[192,512]{1,0:T(8,128)S(1)} %slice.93), channel_id=1, source_target_pairs={{0,3},{1,0},{2,1},{3,2},{4,7},{5,4},{6,5},{7,6},{8,11},{9,8},{10,9... | collective-permute-start | bytes 1179656 | tf_op jit(solution)/shard_map/ppermute | solution.py:36
  34.1 1.2 constant_dynamic-update-slice_fusion.4
  35.3 0.1 constant_dynamic-update-slice_fusion.3
  35.4 6.5 %collective-permute-done.2 = f32[192,512]{1,0:T(8,128)S(1)} collective-permute-done((f32[192,512]{1,0:T(8,128)S(1)}, f32[192,512]{1,0:T(8,128)S(1)}, u32[]{:S(2)}, u32[]{:S(2)}) %collective-permute-start.2) | collective-permute-done | bytes 393248 | tf_op jit(solution)/shard_map/ppermute | solution.py:35
  41.9 0.0 collective-permute-done.3
  41.9 0.1 constant_dynamic-update-slice_fusion
  42.0 0.8 fusion.16
  42.8 0.8 fusion.5
  43.6 0.9 fusion.3
  44.5 0.9 reshape.29
  45.4 3.2 %all-to-all-done = f32[64,8,1536]{2,0,1:T(8,128)} async-done(((f32[64,8,1536]{2,0,1:T(8,128)}), f32[64,8,1536]{2,0,1:T(8,128)}, u32[]{:S(2)}, u32[]{:S(2)}) %all-to-all-start) | async-done | bytes 3145760 | tf_op jit(solution)/shard_map/all_to_all | solution.py:59
  48.6 0.0 copy-start.1
  48.6 4.6 %fusion.42 = f32[512,512]{1,0:T(8,128)S(1)} fusion(f32[512,1536]{1,0:T(8,128)} %bitcast.1, f32[1536,512]{1,0:T(8,128)S(1)} %constant_dynamic-update-slice_fusion), kind=kOutput, calls=%fused_computation.61 | convolution fusion | flops 2415919104 | bytes 7340032 | tf_op jit(solution)/shard_map/dot_general | solution.py:13
  53.3 0.0 copy-done.1
  53.3 0.1 pad_maximum_fusion
  53.4 22.8 %all_to_all.42 = f32[8,88,512]{2,1,0:T(8,128)} all-to-all(f32[8,88,512]{2,1,0:T(8,128)S(1)} %bitcast.45), channel_id=1, replica_groups=mesh['prow'=8,'x'=4,'zl'=2,'y'=4] {'x','zl'}, dimensions={0} | all-to-all | bytes 2883584 | tf_op jit(solution)/shard_map/all_to_all | solution.py:20
  76.2 1.5 reduce_sum.9
  77.7 0.1 collective-permute-start.4
  77.8 1.4 collective-permute-done.4
  79.2 0.1 collective-permute-start.5
  79.3 8.2 %collective-permute-done.5 = f32[88,512]{1,0:T(8,128)S(1)} collective-permute-done((f32[88,512]{1,0:T(8,128)S(1)}, f32[88,512]{1,0:T(8,128)S(1)}, u32[]{:S(2)}, u32[]{:S(2)}) %collective-permute-start.5) | collective-permute-done | bytes 180256 | tf_op jit(solution)/shard_map/ppermute | solution.py:23
  87.6 5.7 %collective-permute-start.6 = (f32[88,512]{1,0:T(8,128)S(1)}, f32[88,512]{1,0:T(8,128)S(1)}, u32[]{:S(2)}, u32[]{:S(2)}) collective-permute-start(f32[88,512]{1,0:T(8,128)S(1)} %add.25), channel_id=1, source_target_pairs={{0,128},{32,160},{64,192},{96,224},{128,0},{160,32},{192,64},{224,... | collective-permute-start | bytes 540680 | tf_op jit(solution)/shard_map/ppermute | solution.py:23
  93.4 7.1 %collective-permute-done.6 = f32[88,512]{1,0:T(8,128)S(1)} collective-permute-done((f32[88,512]{1,0:T(8,128)S(1)}, f32[88,512]{1,0:T(8,128)S(1)}, u32[]{:S(2)}, u32[]{:S(2)}) %collective-permute-start.6) | collective-permute-done | bytes 180256 | tf_op jit(solution)/shard_map/ppermute | solution.py:23
  100.5 0.2 broadcast_in_dim.3
  100.6 25.5 %all_to_all.43 = f32[8,88,512]{2,1,0:T(8,128)S(1)} all-to-all(f32[8,88,512]{2,1,0:T(8,128)S(1)} %broadcast_in_dim.3), channel_id=1, replica_groups=mesh['prow'=8,'x'=4,'zl'=2,'y'=4] {'x','zl'}, dimensions={0} | all-to-all | bytes 2883584 | tf_op jit(solution)/shard_map/all_to_all | solution.py:25
  126.2 0.0 copy-start
  126.2 1.1 copy-done
  127.3 0.8 slice.104
  128.0 1.1 reshape.32
  129.1 0.0 copy-start.3
  129.1 1.3 fusion.19
  130.4 0.4 fusion.29
  130.8 1.2 fusion.21
  132.1 0.4 fusion.27
  132.5 1.3 convolution_subtract_fusion.3
  133.8 0.0 copy-done.3
  133.8 0.3 fusion.33
  134.1 0.4 fusion.24
  134.5 1.3 convolution_subtract_fusion.2
  135.8 0.4 convolution_subtract_fusion.1
  136.2 0.3 fusion.31
  136.5 7.9 %convolution_subtract_fusion = f32[512,1536]{1,0:T(8,128)} fusion(f32[512,1536]{1,0:T(8,128)} %bitcast.1, f32[1536,512]{1,0:T(8,128)S(1)} %constant_dynamic-update-slice_fusion, f32[512,128]{0,1:T(8,128)S(1)} %fusion.19, f32[512,128]{0,1:T(8,128)S(1)} %fusion.21, f32[512,128]{0,1:T(8,128)S(1)} %fusion.33, f32[512,128]{0,1:T(8,128)S(1)} %fusion.31), kind=kOutput, calls=%fused_computation.4 | convolution fusion | flops 2417491968 | bytes 10485760 | tf_op jit(solution)/shard_map/dot_general | solution.py:13
  144.4 3.7 %all-to-all-start.3 = ((f32[8,64,1536]{2,1,0:T(8,128)}), f32[8,64,1536]{2,1,0:T(8,128)S(1)}, u32[]{:S(2)}, u32[]{:S(2)}) async-start(f32[8,64,1536]{2,1,0:T(8,128)} %bitcast.39), calls=%async_computation.3 | async-start | bytes 6291456 | tf_op jit(solution)/shard_map/all_to_all | solution.py:83
  148.1 36.0 %all-to-all-done.3 = f32[8,64,1536]{2,1,0:T(8,128)S(1)} async-done(((f32[8,64,1536]{2,1,0:T(8,128)}), f32[8,64,1536]{2,1,0:T(8,128)S(1)}, u32[]{:S(2)}, u32[]{:S(2)}) %all-to-all-start.3) | async-done | bytes 3145760 | tf_op jit(solution)/shard_map/all_to_all | solution.py:83
  184.2 0.7 fusion.1
  184.9 1.9 %copy.10 = f32[8,8,8,1536]{3,2,0,1:T(8,128)} copy(f32[8,8,8,1536]{3,2,1,0:T(8,128)S(1)} %fusion.1) | data formatting | bytes 6291456 | tf_op jit(solution)/shard_map/reshape | solution.py:84
  (8 shorter events, 0.2 us)
Async XLA Ops:
  4.5 5.8 %copy-start.2 = (f32[384,512]{1,0:T(8,128)S(1)}, f32[384,512]{1,0:T(8,128)}, u32[]{:S(2)}) copy-start(f32[384,512]{1,0:T(8,128)} %param.4) | copy-start | bytes 2359300
  4.5 44.1 %all-to-all-start = ((f32[64,8,1536]{2,0,1:T(8,128)}), f32[64,8,1536]{2,0,1:T(8,128)}, u32[]{:S(2)}, u32[]{:S(2)}) async-start(f32[64,8,1536]{2,0,1:T(8,128)} %fusion.2), calls=%async_computation | async-start | bytes 6291456 | tf_op jit(solution)/shard_map/all_to_all | solution.py:59
  10.3 20.4 %collective-permute-start.1 = (f32[384,512]{1,0:T(8,128)S(1)}, f32[384,512]{1,0:T(8,128)S(1)}, u32[]{:S(2)}, u32[]{:S(2)}) collective-permute-start(f32[384,512]{1,0:T(8,128)S(1)} %copy-done.2), channel_id=1, source_target_pairs={{0,1},{1,2},{2,3},{3,0},{4,5},{5,6},{6,7},{7,4},{8,9},{9,10},{10,1... | collective-permute-start | bytes 2359304 | tf_op jit(solution)/shard_map/ppermute | solution.py:32
  12.0 19.1 %collective-permute-start = (f32[384,512]{1,0:T(8,128)S(1)}, f32[384,512]{1,0:T(8,128)S(1)}, u32[]{:S(2)}, u32[]{:S(2)}) collective-permute-start(f32[384,512]{1,0:T(8,128)S(1)} %copy-done.2), channel_id=1, source_target_pairs={{0,3},{1,0},{2,1},{3,2},{4,7},{5,4},{6,5},{7,6},{8,11},{9,8},{10,9... | collective-permute-start | bytes 2359304 | tf_op jit(solution)/shard_map/ppermute | solution.py:33
  30.7 11.1 %collective-permute-start.2 = (f32[192,512]{1,0:T(8,128)S(1)}, f32[192,512]{1,0:T(8,128)S(1)}, u32[]{:S(2)}, u32[]{:S(2)}) collective-permute-start(f32[192,512]{1,0:T(8,128)S(1)} %slice.92), channel_id=1, source_target_pairs={{0,1},{1,2},{2,3},{3,0},{4,5},{5,6},{6,7},{7,4},{8,9},{9,10},{10,1... | collective-permute-start | bytes 1179656 | tf_op jit(solution)/shard_map/ppermute | solution.py:35
  31.1 10.7 %collective-permute-start.3 = (f32[192,512]{1,0:T(8,128)S(1)}, f32[192,512]{1,0:T(8,128)S(1)}, u32[]{:S(2)}, u32[]{:S(2)}) collective-permute-start(f32[192,512]{1,0:T(8,128)S(1)} %slice.93), channel_id=1, source_target_pairs={{0,3},{1,0},{2,1},{3,2},{4,7},{5,4},{6,5},{7,6},{8,11},{9,8},{10,9... | collective-permute-start | bytes 1179656 | tf_op jit(solution)/shard_map/ppermute | solution.py:36
  48.6 4.7 %copy-start.1 = (f32[192,512]{1,0:T(8,128)S(1)}, f32[192,512]{1,0:T(8,128)}, u32[]{:S(2)}) copy-start(f32[192,512]{1,0:T(8,128)} %reshape.29) | copy-start | bytes 1179652
  77.7 1.5 collective-permute-start.4
  79.2 8.3 %collective-permute-start.5 = (f32[88,512]{1,0:T(8,128)S(1)}, f32[88,512]{1,0:T(8,128)S(1)}, u32[]{:S(2)}, u32[]{:S(2)}) collective-permute-start(f32[88,512]{1,0:T(8,128)S(1)} %add.24), channel_id=1, source_target_pairs={{0,64},{32,96},{64,0},{96,32},{128,192},{160,224},{192,128},{224,1... | collective-permute-start | bytes 540680 | tf_op jit(solution)/shard_map/ppermute | solution.py:23
  87.6 12.8 %collective-permute-start.6 = (f32[88,512]{1,0:T(8,128)S(1)}, f32[88,512]{1,0:T(8,128)S(1)}, u32[]{:S(2)}, u32[]{:S(2)}) collective-permute-start(f32[88,512]{1,0:T(8,128)S(1)} %add.25), channel_id=1, source_target_pairs={{0,128},{32,160},{64,192},{96,224},{128,0},{160,32},{192,64},{224,... | collective-permute-start | bytes 540680 | tf_op jit(solution)/shard_map/ppermute | solution.py:23
  126.2 1.1 copy-start
  129.1 4.7 %copy-start.3 = (f32[4,128,128]{2,1,0:T(8,128)S(1)}, f32[4,128,128]{2,1,0:T(8,128)}, u32[]{:S(2)}) copy-start(f32[4,128,128]{2,1,0:T(8,128)} %param.5) | copy-start | bytes 786436
  144.4 39.7 %all-to-all-start.3 = ((f32[8,64,1536]{2,1,0:T(8,128)}), f32[8,64,1536]{2,1,0:T(8,128)S(1)}, u32[]{:S(2)}, u32[]{:S(2)}) async-start(f32[8,64,1536]{2,1,0:T(8,128)} %bitcast.39), calls=%async_computation.3 | async-start | bytes 6291456 | tf_op jit(solution)/shard_map/all_to_all | solution.py:83

commit v12 on v11

--- a/solution.py
+++ b/solution.py
@@ -18,10 +18,18 @@
     chunk = -(-rows // (8 * outer_size)) * 8
     packed = jnp.pad(packed, ((0, chunk * outer_size - rows), (0, 0))).reshape(outer_size, chunk, lanes)
     total = jnp.sum(lax.all_to_all(packed, outer, 0, 0, tiled=True), axis=0)
-    bit = 1
+    pairs = [(i, i ^ 1) for i in range(inner_size)]
+    first = lax.rem(lax.axis_index(inner), 2) == 0
+    half = lanes // 2
+    keep = jnp.where(first, total[:, :half], total[:, half:])
+    send = jnp.where(first, total[:, half:], total[:, :half])
+    mine = keep + lax.ppermute(send, inner, pairs)
+    bit = 2
     while bit < inner_size:
-        total = total + lax.ppermute(total, inner, [(i, i ^ bit) for i in range(inner_size)])
+        mine = mine + lax.ppermute(mine, inner, [(i, i ^ bit) for i in range(inner_size)])
         bit *= 2
+    other = lax.ppermute(mine, inner, pairs)
+    total = jnp.where(first, jnp.concatenate([mine, other], axis=1), jnp.concatenate([other, mine], axis=1))
     total = lax.all_to_all(jnp.broadcast_to(total, (outer_size, chunk, lanes)), outer, 0, 0, tiled=True)
     return total.reshape(outer_size * chunk, lanes)[:rows]
 
@@ -64,19 +72,24 @@
     packed = jnp.concatenate([products, grams.reshape(-1, lanes)], axis=0)
     packed = all_reduce(packed, GROUP, "prow", ng, nprow)
     span = products.shape[0]
-    products = [packed[:span, k * width : (k + 1) * width] for k in range(count)]
     grams = packed[span:].reshape(grams.shape)
     gram, offset = {}, 0
     for j in range(1, count):
         for k in range(j):
             gram[j, k], offset = grams[:, offset : offset + width], offset + width
 
+    diagonal = jnp.zeros((count * width, count * width), tfactors.dtype)
+    for k in range(count):
+        diagonal = diagonal.at[k * width : (k + 1) * width, k * width : (k + 1) * width].set(tfactors[k].T)
+    products = matmul(packed[:span], diagonal)
     scaled = [None] * count
     for k in reversed(range(count)):
-        part = products[k]
-        for j in range(k + 1, count):
-            part = part - matmul(scaled[j], gram[j, k])
-        scaled[k] = matmul(part, tfactors[k].T)
+        part = products[:, k * width : (k + 1) * width]
+        if k + 1 < count:
+            later = list(range(count - 1, k, -1))
+            weights = matmul(jnp.concatenate([gram[j, k] for j in later], axis=0), tfactors[k].T)
+            part = part - matmul(jnp.concatenate([scaled[j] for j in later], axis=1), weights)
+        scaled[k] = part
     scaled = jnp.concatenate(scaled, axis=1)
 
     work = work - matmul(scaled, basis.T)

time: 188 us -> 186 us (0.989)
  blocking collectives: 48.3 us -> 0 us
  waiting for transfers between devices: 79.5 us -> 115 us
  starting transfers between devices: 22.1 us -> 29.8 us
  local copies, waits for them, and re-layouts: 9.48 us -> 13.6 us
  matrix products: 22.4 us -> 20.2 us
    all_to_all x2 -> x0, blocking collectives: 48.3 us -> none  [the longest x1 25.5 us: all_reduce(): lax.all_to_all(jnp.broadcast_to(total, (outer_size, chunk, lanes)), outer...]
    all_to_all x0 -> x2, waiting for transfers between devices: none -> 36.5 us  [the longest x1 19 us: all_reduce(): total = jnp.sum(lax.all_to_all(packed, outer, 0, 0, tiled=True), axis=0)]
    all_to_all x0 -> x2, starting transfers between devices: none -> 8.59 us  [the longest x1 4.29 us: all_reduce(): lax.all_to_all(jnp.broadcast_to(total, (outer_size, chunk, lanes)), outer...]
    scatter x0 -> x4, local copies, waits for them, and re-layouts: none -> 3.06 us  [per_device(): diagonal.at[k * width:(k + 1) * width, k * width:(k + 1) * width]]
    ppermute x3 -> x4, waiting for transfers between devices: 16.7 us -> 14.2 us  [the longest x2 11.6 us: all_reduce(): lax.ppermute(mine, inner, [(i, i ^ bit) for i in range(inner_size)])]
    dot_general x15 -> x12, matrix products: 22.4 us -> 20.2 us  [matmul(): jnp.dot(left, right, precision=lax.Precision.HIGH, preferred_element_type...]
    ppermute x3 -> x4, starting transfers between devices: 5.93 us -> 5.04 us  [the longest x2 4.67 us: all_reduce(): lax.ppermute(mine, inner, [(i, i ^ bit) for i in range(inner_size)])]
  transfers between devices with their start and end apart: 9 -> 12, of which waited for: 7 -> 10; matrix products, arithmetic and copies ran while one was open for 3% -> 4% of each run, Pallas kernels for 0% -> 0%
where the time goes in v12:
time: 186 us; the launch traced here: 185 us
  waiting for transfers between devices  115 us (62%)
  starting transfers between devices  29.8 us (16%)
  matrix products  20.2 us (11%)
  local copies, waits for them, and re-layouts  13.6 us (7%)
  other arithmetic  5.91 us (3%)
    all_to_all x1, waiting for transfers between devices, per_device(): work = lax.all_to_all(work, GROUP, 0, 1, tiled=True)  37.8 us
    dot_general x12, matrix products, matmul(): jnp.dot(left, right, precision=lax.Precision.HIGH, preferred_element_type...  20.2 us
    all_to_all x1, waiting for transfers between devices, all_reduce(): total = jnp.sum(lax.all_to_all(packed, outer, 0, 0, tiled=True), axis=0)  19 us
    all_to_all x1, waiting for transfers between devices, all_reduce(): lax.all_to_all(jnp.broadcast_to(total, (outer_size, chunk, lanes)), outer...  17.5 us
    ppermute x1, waiting for transfers between devices, gather_ring(): from_left = lax.ppermute(block, axis, right)  17 us
    ppermute x2, waiting for transfers between devices, all_reduce(): lax.ppermute(mine, inner, [(i, i ^ bit) for i in range(inner_size)])  11.6 us
    ppermute x1, waiting for transfers between devices, gather_ring(): far_first = lax.ppermute(from_left[:half], axis, right)  6.45 us
    all_to_all x1, starting transfers between devices, per_device(): work = lax.all_to_all(work, GROUP, 1, 0, tiled=True)  5.79 us
  transfers between devices with their start and end apart: 12, of which 10 were waited for; matrix products, arithmetic and copies ran while one was open for 4% of the time, Pallas kernels for 0%

profile of v12, /device:TPU:64, one launch (start us, length us, event | category | flops | bytes accessed | tf_op | source)
XLA Modules:
  0.0 185.1 jit_solution(9508286726929075309)
XLA Ops:
  0.0 2.2 %copy.12 = f32[8,8,8,1536]{3,2,0,1:T(8,128)S(1)} copy(f32[8,8,8,1536]{3,2,1,0:T(8,128)} %bitcast.47) | data formatting | bytes 6291456 | tf_op jit(solution)/shard_map/reshape | solution.py:66
  2.2 2.4 %fusion.2 = f32[64,8,1536]{2,0,1:T(8,128)} fusion(s32[]{:T(128)S(6)} %select_n.38, f32[64,8,1536]{2,0,1:T(8,128)S(1)} %bitcast.44), kind=kLoop, calls=%fused_computation.7 | loop fusion | flops 786432 | bytes 6291460 | tf_op jit(solution)/shard_map/concatenate | solution.py:50
  4.5 0.0 copy-start.3
  4.5 5.8 %all-to-all-start = ((f32[64,8,1536]{2,0,1:T(8,128)}), f32[64,8,1536]{2,0,1:T(8,128)}, u32[]{:S(2)}, u32[]{:S(2)}) async-start(f32[64,8,1536]{2,0,1:T(8,128)} %fusion.2), calls=%async_computation | async-start | bytes 6291456 | tf_op jit(solution)/shard_map/all_to_all | solution.py:67
  10.3 0.0 copy-done.3
  10.3 1.7 collective-permute-start.1
  12.0 1.7 collective-permute-start
  13.6 17.0 %collective-permute-done.1 = f32[384,512]{1,0:T(8,128)S(1)} collective-permute-done((f32[384,512]{1,0:T(8,128)S(1)}, f32[384,512]{1,0:T(8,128)S(1)}, u32[]{:S(2)}, u32[]{:S(2)}) %collective-permute-start.1) | collective-permute-done | bytes 786464 | tf_op jit(solution)/shard_map/ppermute | solution.py:40
  30.7 0.4 collective-permute-start.2
  31.1 0.0 collective-permute-done
  31.1 3.0 %collective-permute-start.3 = (f32[192,512]{1,0:T(8,128)S(1)}, f32[192,512]{1,0:T(8,128)S(1)}, u32[]{:S(2)}, u32[]{:S(2)}) collective-permute-start(f32[192,512]{1,0:T(8,128)S(1)} %slice.193), channel_id=1, source_target_pairs={{0,3},{1,0},{2,1},{3,2},{4,7},{5,4},{6,5},{7,6},{8,11},{9,8},{10,9... | collective-permute-start | bytes 1179656 | tf_op jit(solution)/shard_map/ppermute | solution.py:44
  34.1 1.2 constant_dynamic-update-slice_fusion.4
  35.3 0.1 constant_dynamic-update-slice_fusion.3
  35.4 6.5 %collective-permute-done.2 = f32[192,512]{1,0:T(8,128)S(1)} collective-permute-done((f32[192,512]{1,0:T(8,128)S(1)}, f32[192,512]{1,0:T(8,128)S(1)}, u32[]{:S(2)}, u32[]{:S(2)}) %collective-permute-start.2) | collective-permute-done | bytes 393248 | tf_op jit(solution)/shard_map/ppermute | solution.py:43
  41.9 0.0 collective-permute-done.3
  41.9 0.1 constant_dynamic-update-slice_fusion
  42.0 0.8 fusion.18
  42.8 0.8 fusion.5
  43.6 0.9 fusion.3
  44.5 0.9 reshape.144
  45.4 3.2 %all-to-all-done = f32[64,8,1536]{2,0,1:T(8,128)} async-done(((f32[64,8,1536]{2,0,1:T(8,128)}), f32[64,8,1536]{2,0,1:T(8,128)}, u32[]{:S(2)}, u32[]{:S(2)}) %all-to-all-start) | async-done | bytes 3145760 | tf_op jit(solution)/shard_map/all_to_all | solution.py:67
  48.6 0.0 copy-start
  48.6 4.6 %fusion.54 = f32[512,512]{1,0:T(8,128)S(1)} fusion(f32[512,1536]{1,0:T(8,128)} %bitcast.1, f32[1536,512]{1,0:T(8,128)S(1)} %constant_dynamic-update-slice_fusion), kind=kOutput, calls=%fused_computation.77 | convolution fusion | flops 2415919104 | bytes 7340032 | tf_op jit(solution)/shard_map/dot_general | solution.py:13
  53.3 0.0 copy-done
  53.3 1.2 pad_maximum_fusion
  54.5 4.3 %all-to-all-start.1 = ((f32[8,88,512]{2,1,0:T(8,128)}), f32[8,88,512]{2,1,0:T(8,128)}, u32[]{:S(2)}, u32[]{:S(2)}) async-start(f32[8,88,512]{2,1,0:T(8,128)} %bitcast.46), calls=%async_computation.1 | async-start | bytes 2883584 | tf_op jit(solution)/shard_map/all_to_all | solution.py:20
  58.8 19.0 %all-to-all-done.1 = f32[8,88,512]{2,1,0:T(8,128)} async-done(((f32[8,88,512]{2,1,0:T(8,128)}), f32[8,88,512]{2,1,0:T(8,128)}, u32[]{:S(2)}, u32[]{:S(2)}) %all-to-all-start.1) | async-done | bytes 1441824 | tf_op jit(solution)/shard_map/all_to_all | solution.py:20
  77.8 1.5 reduce_sum.9
  79.3 0.1 collective-permute-start.4
  79.4 1.3 collective-permute-done.4
  80.7 0.0 copy-start.1
  80.7 0.1 collective-permute-start.5
  80.8 5.7 %collective-permute-done.5 = f32[88,256]{1,0:T(8,128)S(1)} collective-permute-done((f32[88,256]{1,0:T(8,128)S(1)}, f32[88,256]{1,0:T(8,128)S(1)}, u32[]{:S(2)}, u32[]{:S(2)}) %collective-permute-start.5) | collective-permute-done | bytes 90144 | tf_op jit(solution)/shard_map/ppermute | solution.py:29
  86.5 4.6 %collective-permute-start.6 = (f32[88,256]{1,0:T(8,128)S(1)}, f32[88,256]{1,0:T(8,128)S(1)}, u32[]{:S(2)}, u32[]{:S(2)}) collective-permute-start(f32[88,256]{1,0:T(8,128)S(1)} %add.35), channel_id=1, source_target_pairs={{0,128},{32,160},{64,192},{96,224},{128,0},{160,32},{192,64},{224,... | collective-permute-start | bytes 270344 | tf_op jit(solution)/shard_map/ppermute | solution.py:29
  91.1 6.0 %collective-permute-done.6 = f32[88,256]{1,0:T(8,128)S(1)} collective-permute-done((f32[88,256]{1,0:T(8,128)S(1)}, f32[88,256]{1,0:T(8,128)S(1)}, u32[]{:S(2)}, u32[]{:S(2)}) %collective-permute-start.6) | collective-permute-done | bytes 90144 | tf_op jit(solution)/shard_map/ppermute | solution.py:29
  97.1 0.3 collective-permute-start.7
  97.4 1.3 collective-permute-done.7
  98.7 1.3 broadcast_in_dim.4
  100.0 4.3 %all-to-all-start.2 = ((f32[8,88,512]{2,1,0:T(8,128)}), f32[8,88,512]{2,1,0:T(8,128)}, u32[]{:S(2)}, u32[]{:S(2)}) async-start(f32[8,88,512]{2,1,0:T(8,128)} %broadcast_in_dim.4), calls=%async_computation.2 | async-start | bytes 2883584 | tf_op jit(solution)/shard_map/all_to_all | solution.py:33
  104.3 0.0 copy-done.1
  104.3 1.1 scatter.14
  105.4 0.6 bitcast_dynamic-update-slice_fusion.2
  106.1 0.6 bitcast_dynamic-update-slice_fusion.1
  106.7 0.6 bitcast_dynamic-update-slice_fusion
  107.3 17.5 %all-to-all-done.2 = f32[8,88,512]{2,1,0:T(8,128)} async-done(((f32[8,88,512]{2,1,0:T(8,128)}), f32[8,88,512]{2,1,0:T(8,128)}, u32[]{:S(2)}, u32[]{:S(2)}) %all-to-all-start.2) | async-done | bytes 1441824 | tf_op jit(solution)/shard_map/all_to_all | solution.py:33
  124.8 1.8 slice.206
  126.6 1.1 reshape.147
  127.7 0.0 copy-start.2
  127.7 1.1 fusion.39
  128.8 2.6 %fusion.7 = f32[512,512]{0,1:T(8,128)S(1)} fusion(f32[512,512]{0,1:T(8,128)} %bitcast_dynamic-update-slice_fusion, f32[704,512]{1,0:T(8,128)} %bitcast.4), kind=kOutput, calls=%fused_computation.17 | convolution fusion | flops 805306368 | bytes 3145728 | tf_op jit(solution)/shard_map/dot_general | solution.py:13
  131.4 0.3 convolution_subtract_fusion.2
  131.7 0.0 copy-done.2
  131.7 0.2 fusion.35
  132.0 0.2 fusion.29
  132.2 0.3 convolution_subtract_fusion.1
  132.6 0.4 convolution_subtract_fusion.3
  133.0 7.9 %convolution_subtract_fusion = f32[512,1536]{1,0:T(8,128)} fusion(f32[512,1536]{1,0:T(8,128)} %bitcast.1, f32[1536,512]{1,0:T(8,128)S(1)} %constant_dynamic-update-slice_fusion, f32[512,128]{0,1:T(8,128)S(1)} %slice.204, f32[512,128]{0,1:T(8,128)S(1)} %convolution_subtract_fusion.2, f32[512,128]{0,1:T(8,128)S(1)} %convolution_subtract_fusion.1, ...), kind=kOutput, calls=%fused_computation.4 | convolution fusion | flops 2417491968 | bytes 10485760 | tf_op jit(solution)/shard_map/dot_general | solution.py:13
  140.9 3.7 %all-to-all-start.3 = ((f32[8,64,1536]{2,1,0:T(8,128)}), f32[8,64,1536]{2,1,0:T(8,128)S(1)}, u32[]{:S(2)}, u32[]{:S(2)}) async-start(f32[8,64,1536]{2,1,0:T(8,128)} %bitcast.45), calls=%async_computation.3 | async-start | bytes 6291456 | tf_op jit(solution)/shard_map/all_to_all | solution.py:96
  144.6 37.8 %all-to-all-done.3 = f32[8,64,1536]{2,1,0:T(8,128)S(1)} async-done(((f32[8,64,1536]{2,1,0:T(8,128)}), f32[8,64,1536]{2,1,0:T(8,128)S(1)}, u32[]{:S(2)}, u32[]{:S(2)}) %all-to-all-start.3) | async-done | bytes 3145760 | tf_op jit(solution)/shard_map/all_to_all | solution.py:96
  182.4 0.7 fusion.1
  183.2 1.9 %copy.10 = f32[8,8,8,1536]{3,2,0,1:T(8,128)} copy(f32[8,8,8,1536]{3,2,1,0:T(8,128)S(1)} %fusion.1) | data formatting | bytes 6291456 | tf_op jit(solution)/shard_map/reshape | solution.py:97
  (13 shorter events, 0.3 us)
Async XLA Ops:
  4.5 5.8 %copy-start.3 = (f32[384,512]{1,0:T(8,128)S(1)}, f32[384,512]{1,0:T(8,128)}, u32[]{:S(2)}) copy-start(f32[384,512]{1,0:T(8,128)} %param.12) | copy-start | bytes 2359300
  4.5 44.1 %all-to-all-start = ((f32[64,8,1536]{2,0,1:T(8,128)}), f32[64,8,1536]{2,0,1:T(8,128)}, u32[]{:S(2)}, u32[]{:S(2)}) async-start(f32[64,8,1536]{2,0,1:T(8,128)} %fusion.2), calls=%async_computation | async-start | bytes 6291456 | tf_op jit(solution)/shard_map/all_to_all | solution.py:67
  10.3 20.4 %collective-permute-start.1 = (f32[384,512]{1,0:T(8,128)S(1)}, f32[384,512]{1,0:T(8,128)S(1)}, u32[]{:S(2)}, u32[]{:S(2)}) collective-permute-start(f32[384,512]{1,0:T(8,128)S(1)} %copy-done.3), channel_id=1, source_target_pairs={{0,1},{1,2},{2,3},{3,0},{4,5},{5,6},{6,7},{7,4},{8,9},{9,10},{10,1... | collective-permute-start | bytes 2359304 | tf_op jit(solution)/shard_map/ppermute | solution.py:40
  12.0 19.1 %collective-permute-start = (f32[384,512]{1,0:T(8,128)S(1)}, f32[384,512]{1,0:T(8,128)S(1)}, u32[]{:S(2)}, u32[]{:S(2)}) collective-permute-start(f32[384,512]{1,0:T(8,128)S(1)} %copy-done.3), channel_id=1, source_target_pairs={{0,3},{1,0},{2,1},{3,2},{4,7},{5,4},{6,5},{7,6},{8,11},{9,8},{10,9... | collective-permute-start | bytes 2359304 | tf_op jit(solution)/shard_map/ppermute | solution.py:41
  30.7 11.1 %collective-permute-start.2 = (f32[192,512]{1,0:T(8,128)S(1)}, f32[192,512]{1,0:T(8,128)S(1)}, u32[]{:S(2)}, u32[]{:S(2)}) collective-permute-start(f32[192,512]{1,0:T(8,128)S(1)} %slice.192), channel_id=1, source_target_pairs={{0,1},{1,2},{2,3},{3,0},{4,5},{5,6},{6,7},{7,4},{8,9},{9,10},{10,1... | collective-permute-start | bytes 1179656 | tf_op jit(solution)/shard_map/ppermute | solution.py:43
  31.1 10.7 %collective-permute-start.3 = (f32[192,512]{1,0:T(8,128)S(1)}, f32[192,512]{1,0:T(8,128)S(1)}, u32[]{:S(2)}, u32[]{:S(2)}) collective-permute-start(f32[192,512]{1,0:T(8,128)S(1)} %slice.193), channel_id=1, source_target_pairs={{0,3},{1,0},{2,1},{3,2},{4,7},{5,4},{6,5},{7,6},{8,11},{9,8},{10,9... | collective-permute-start | bytes 1179656 | tf_op jit(solution)/shard_map/ppermute | solution.py:44
  48.6 4.7 %copy-start = (f32[192,512]{1,0:T(8,128)S(1)}, f32[192,512]{1,0:T(8,128)}, u32[]{:S(2)}) copy-start(f32[192,512]{1,0:T(8,128)} %reshape.144) | copy-start | bytes 1179652
  54.5 23.3 %all-to-all-start.1 = ((f32[8,88,512]{2,1,0:T(8,128)}), f32[8,88,512]{2,1,0:T(8,128)}, u32[]{:S(2)}, u32[]{:S(2)}) async-start(f32[8,88,512]{2,1,0:T(8,128)} %bitcast.46), calls=%async_computation.1 | async-start | bytes 2883584 | tf_op jit(solution)/shard_map/all_to_all | solution.py:20
  79.3 1.4 collective-permute-start.4
  80.7 23.5 %copy-start.1 = (f32[4,128,128]{2,1,0:T(8,128)S(1)}, f32[4,128,128]{2,1,0:T(8,128)}, u32[]{:S(2)}) copy-start(f32[4,128,128]{2,1,0:T(8,128)} %param.13) | copy-start | bytes 786436
  80.7 5.8 %collective-permute-start.5 = (f32[88,256]{1,0:T(8,128)S(1)}, f32[88,256]{1,0:T(8,128)S(1)}, u32[]{:S(2)}, u32[]{:S(2)}) collective-permute-start(f32[88,256]{1,0:T(8,128)S(1)} %select_add_fusion), channel_id=1, source_target_pairs={{0,64},{32,96},{64,0},{96,32},{128,192},{160,224},{192,128},{224,1... | collective-permute-start | bytes 270344 | tf_op jit(solution)/shard_map/ppermute | solution.py:29
  86.5 10.6 %collective-permute-start.6 = (f32[88,256]{1,0:T(8,128)S(1)}, f32[88,256]{1,0:T(8,128)S(1)}, u32[]{:S(2)}, u32[]{:S(2)}) collective-permute-start(f32[88,256]{1,0:T(8,128)S(1)} %add.35), channel_id=1, source_target_pairs={{0,128},{32,160},{64,192},{96,224},{128,0},{160,32},{192,64},{224,... | collective-permute-start | bytes 270344 | tf_op jit(solution)/shard_map/ppermute | solution.py:29
  97.1 1.6 collective-permute-start.7
  100.0 24.9 %all-to-all-start.2 = ((f32[8,88,512]{2,1,0:T(8,128)}), f32[8,88,512]{2,1,0:T(8,128)}, u32[]{:S(2)}, u32[]{:S(2)}) async-start(f32[8,88,512]{2,1,0:T(8,128)} %broadcast_in_dim.4), calls=%async_computation.2 | async-start | bytes 2883584 | tf_op jit(solution)/shard_map/all_to_all | solution.py:33
  127.7 4.1 %copy-start.2 = (f32[4,128,128]{2,1,0:T(8,128)S(1)}, f32[4,128,128]{2,1,0:T(8,128)}, u32[]{:S(2)}) copy-start(f32[4,128,128]{2,1,0:T(8,128)} %param.13) | copy-start | bytes 786436
  140.9 41.5 %all-to-all-start.3 = ((f32[8,64,1536]{2,1,0:T(8,128)}), f32[8,64,1536]{2,1,0:T(8,128)S(1)}, u32[]{:S(2)}, u32[]{:S(2)}) async-start(f32[8,64,1536]{2,1,0:T(8,128)} %bitcast.45), calls=%async_computation.3 | async-start | bytes 6291456 | tf_op jit(solution)/shard_map/all_to_all | solution.py:96

commit v13 on v12

--- a/solution.py
+++ b/solution.py
@@ -15,23 +15,23 @@
 
 def all_reduce(packed, outer, inner, outer_size, inner_size):
     rows, lanes = packed.shape
-    chunk = -(-rows // (8 * outer_size)) * 8
-    packed = jnp.pad(packed, ((0, chunk * outer_size - rows), (0, 0))).reshape(outer_size, chunk, lanes)
-    total = jnp.sum(lax.all_to_all(packed, outer, 0, 0, tiled=True), axis=0)
     pairs = [(i, i ^ 1) for i in range(inner_size)]
     first = lax.rem(lax.axis_index(inner), 2) == 0
     half = lanes // 2
-    keep = jnp.where(first, total[:, :half], total[:, half:])
-    send = jnp.where(first, total[:, half:], total[:, :half])
+    keep = jnp.where(first, packed[:, :half], packed[:, half:])
+    send = jnp.where(first, packed[:, half:], packed[:, :half])
     mine = keep + lax.ppermute(send, inner, pairs)
+    chunk = -(-rows // (8 * outer_size)) * 8
+    mine = jnp.pad(mine, ((0, chunk * outer_size - rows), (0, 0))).reshape(outer_size, chunk, half)
+    total = jnp.sum(lax.all_to_all(mine, outer, 0, 0, tiled=True), axis=0)
     bit = 2
     while bit < inner_size:
-        mine = mine + lax.ppermute(mine, inner, [(i, i ^ bit) for i in range(inner_size)])
+        total = total + lax.ppermute(total, inner, [(i, i ^ bit) for i in range(inner_size)])
         bit *= 2
+    total = lax.all_to_all(jnp.broadcast_to(total, (outer_size, chunk, half)), outer, 0, 0, tiled=True)
+    mine = total.reshape(outer_size * chunk, half)[:rows]
     other = lax.ppermute(mine, inner, pairs)
-    total = jnp.where(first, jnp.concatenate([mine, other], axis=1), jnp.concatenate([other, mine], axis=1))
-    total = lax.all_to_all(jnp.broadcast_to(total, (outer_size, chunk, lanes)), outer, 0, 0, tiled=True)
-    return total.reshape(outer_size * chunk, lanes)[:rows]
+    return jnp.where(first, jnp.concatenate([mine, other], axis=1), jnp.concatenate([other, mine], axis=1))
 
 
 def gather_ring(block, axis, size):

time: 186 us -> 170 us (0.914)
  waiting for transfers between devices: 115 us -> 73.8 us
  blocking collectives: 0 us -> 30.5 us
  starting transfers between devices: 29.8 us -> 20.8 us
  local copies, waits for them, and re-layouts: 13.6 us -> 16.3 us
    all_to_all x2 -> x0, waiting for transfers between devices: 36.5 us -> none  [the longest x1 19 us: all_reduce(): total = jnp.sum(lax.all_to_all(packed, outer, 0, 0, tiled=True), axis=0)]
    all_to_all x0 -> x2, blocking collectives: none -> 30.5 us  [the longest x1 17.5 us: all_reduce(): total = jnp.sum(lax.all_to_all(mine, outer, 0, 0, tiled=True), axis=0)]
    all_to_all x2 -> x0, starting transfers between devices: 8.59 us -> none  [the longest x1 4.29 us: all_reduce(): lax.all_to_all(jnp.broadcast_to(total, (outer_size, chunk, lanes)), outer...]
    unnamed x12 -> x20, local copies, waits for them, and re-layouts: 1.31 us -> 7.37 us
    all_to_all x1, waiting for transfers between devices: 3.22 us -> 0.01 us  [per_device(): work = lax.all_to_all(work, GROUP, 1, 0, tiled=True)]
    scatter x4, local copies, waits for them, and re-layouts: 3.06 us -> 0.14 us  [per_device(): diagonal.at[k * width:(k + 1) * width, k * width:(k + 1) * width]]
    ppermute x1, waiting for transfers between devices: 6.45 us -> 3.87 us  [gather_ring(): far_first = lax.ppermute(from_left[:half], axis, right)]
  transfers between devices with their start and end apart: 12 -> 10, of which waited for: 10 -> 8; matrix products, arithmetic and copies ran while one was open for 4% -> 6% of each run, Pallas kernels for 0% -> 0%
where the time goes in v13:
time: 170 us; the launch traced here: 167 us
  waiting for transfers between devices  73.8 us (43%)
  blocking collectives  30.5 us (18%)
  starting transfers between devices  20.8 us (12%)
  matrix products  20.2 us (12%)
  local copies, waits for them, and re-layouts  16.3 us (10%)
  other arithmetic  5.61 us (3%)
    all_to_all x1, waiting for transfers between devices, per_device(): work = lax.all_to_all(work, GROUP, 0, 1, tiled=True)  38.7 us
    dot_general x12, matrix products, matmul(): jnp.dot(left, right, precision=lax.Precision.HIGH, preferred_element_type...  20.2 us
    all_to_all x1, blocking collectives, all_reduce(): total = jnp.sum(lax.all_to_all(mine, outer, 0, 0, tiled=True), axis=0)  17.5 us
    ppermute x1, waiting for transfers between devices, gather_ring(): from_left = lax.ppermute(block, axis, right)  17 us
    all_to_all x1, blocking collectives, all_reduce(): lax.all_to_all(jnp.broadcast_to(total, (outer_size, chunk, half)), outer,...  12.9 us
    ppermute x2, waiting for transfers between devices, all_reduce(): lax.ppermute(total, inner, [(i, i ^ bit) for i in range(inner_size)])  9.92 us
    unnamed x20, local copies, waits for them, and re-layouts  7.37 us
    all_to_all x1, starting transfers between devices, per_device(): work = lax.all_to_all(work, GROUP, 1, 0, tiled=True)  5.79 us
  transfers between devices with their start and end apart: 10, of which 8 were waited for; matrix products, arithmetic and copies ran while one was open for 6% of the time, Pallas kernels for 0%

profile of v13, /device:TPU:64, one launch (start us, length us, event | category | flops | bytes accessed | tf_op | source)
XLA Modules:
  0.0 167.4 jit_solution(15768122960817755887)
XLA Ops:
  0.0 2.2 %copy.12 = f32[8,8,8,1536]{3,2,0,1:T(8,128)S(1)} copy(f32[8,8,8,1536]{3,2,1,0:T(8,128)} %bitcast.46) | data formatting | bytes 6291456 | tf_op jit(solution)/shard_map/reshape | solution.py:66
  2.2 2.4 %fusion.2 = f32[64,8,1536]{2,0,1:T(8,128)} fusion(s32[]{:T(128)S(6)} %select_n.38, f32[64,8,1536]{2,0,1:T(8,128)S(1)} %bitcast.44), kind=kLoop, calls=%fused_computation.7 | loop fusion | flops 786432 | bytes 6291460 | tf_op jit(solution)/shard_map/concatenate | solution.py:50
  4.5 5.8 %all-to-all-start = ((f32[64,8,1536]{2,0,1:T(8,128)}), f32[64,8,1536]{2,0,1:T(8,128)}, u32[]{:S(2)}, u32[]{:S(2)}) async-start(f32[64,8,1536]{2,0,1:T(8,128)} %fusion.2), calls=%async_computation | async-start | bytes 6291456 | tf_op jit(solution)/shard_map/all_to_all | solution.py:67
  10.3 0.0 copy-done.7
  10.3 1.7 collective-permute-start.1
  12.0 1.7 collective-permute-start
  13.6 17.0 %collective-permute-done.1 = f32[384,512]{1,0:T(8,128)S(1)} collective-permute-done((f32[384,512]{1,0:T(8,128)S(1)}, f32[384,512]{1,0:T(8,128)S(1)}, u32[]{:S(2)}, u32[]{:S(2)}) %collective-permute-start.1) | collective-permute-done | bytes 786464 | tf_op jit(solution)/shard_map/ppermute | solution.py:40
  30.7 0.9 copy-done.2
  31.6 0.8 slice.192
  32.3 0.3 collective-permute-start.2
  32.6 0.0 collective-permute-done
  32.6 0.9 copy-done.4
  33.5 0.8 slice.193
  34.3 2.9 %collective-permute-start.3 = (f32[192,512]{1,0:T(8,128)}, f32[192,512]{1,0:T(8,128)}, u32[]{:S(2)}, u32[]{:S(2)}) collective-permute-start(f32[192,512]{1,0:T(8,128)} %slice.193), channel_id=1, source_target_pairs={{0,3},{1,0},{2,1},{3,2},{4,7},{5,4},{6,5},{7,6},{8,11},{9,8},{10,9... | collective-permute-start | bytes 1179656 | tf_op jit(solution)/shard_map/ppermute | solution.py:44
  37.3 1.3 constant_dynamic-update-slice_fusion.4
  38.5 1.2 constant_dynamic-update-slice_fusion.3
  39.7 3.9 %collective-permute-done.2 = f32[192,512]{1,0:T(8,128)S(1)} collective-permute-done((f32[192,512]{1,0:T(8,128)}, f32[192,512]{1,0:T(8,128)S(1)}, u32[]{:S(2)}, u32[]{:S(2)}) %collective-permute-start.2) | collective-permute-done | bytes 393248 | tf_op jit(solution)/shard_map/ppermute | solution.py:43
  43.6 1.0 collective-permute-done.3
  44.7 1.0 constant_dynamic-update-slice_fusion.1
  45.7 0.0 copy-done.3
  45.7 0.1 constant_dynamic-update-slice_fusion
  45.8 0.8 fusion.18
  46.6 0.8 fusion.5
  47.4 0.9 fusion.3
  48.3 0.8 pad_maximum_fusion.1
  49.1 1.1 reshape.144
  50.2 0.0 all-to-all-done
  50.2 4.6 %fusion.64 = f32[512,512]{1,0:T(8,128)S(1)} fusion(f32[512,1536]{1,0:T(8,128)} %bitcast.1, f32[1536,512]{1,0:T(8,128)S(1)} %constant_dynamic-update-slice_fusion), kind=kOutput, calls=%fused_computation.83 | convolution fusion | flops 2415919104 | bytes 7340032 | tf_op jit(solution)/shard_map/dot_general | solution.py:13
  54.8 0.1 broadcast_select_fusion
  54.9 0.1 collective-permute-start.4
  55.0 2.2 %collective-permute-done.4 = f32[704,256]{1,0:T(8,128)S(1)} collective-permute-done((f32[704,256]{1,0:T(8,128)S(1)}, f32[704,256]{1,0:T(8,128)S(1)}, u32[]{:S(2)}, u32[]{:S(2)}) %collective-permute-start.4) | collective-permute-done | bytes 720928 | tf_op jit(solution)/shard_map/ppermute | solution.py:23
  57.2 0.2 select_add_fusion
  57.4 0.0 copy-start.5
  57.4 17.5 %all_to_all.42 = f32[8,88,256]{2,1,0:T(8,128)} all-to-all(f32[8,88,256]{2,1,0:T(8,128)S(1)} %bitcast.49), channel_id=1, replica_groups=mesh['prow'=8,'x'=4,'zl'=2,'y'=4] {'x','zl'}, dimensions={0} | all-to-all | bytes 1441792 | tf_op jit(solution)/shard_map/all_to_all | solution.py:26
  74.9 1.2 reduce_sum.9
  76.1 0.1 collective-permute-start.5
  76.2 5.5 %collective-permute-done.5 = f32[88,256]{1,0:T(8,128)S(1)} collective-permute-done((f32[88,256]{1,0:T(8,128)S(1)}, f32[88,256]{1,0:T(8,128)S(1)}, u32[]{:S(2)}, u32[]{:S(2)}) %collective-permute-start.5) | collective-permute-done | bytes 90144 | tf_op jit(solution)/shard_map/ppermute | solution.py:29
  81.7 4.6 %collective-permute-start.6 = (f32[88,256]{1,0:T(8,128)S(1)}, f32[88,256]{1,0:T(8,128)S(1)}, u32[]{:S(2)}, u32[]{:S(2)}) collective-permute-start(f32[88,256]{1,0:T(8,128)S(1)} %add.35), channel_id=1, source_target_pairs={{0,128},{32,160},{64,192},{96,224},{128,0},{160,32},{192,64},{224,... | collective-permute-start | bytes 270344 | tf_op jit(solution)/shard_map/ppermute | solution.py:29
  86.3 4.4 %collective-permute-done.6 = f32[88,256]{1,0:T(8,128)S(1)} collective-permute-done((f32[88,256]{1,0:T(8,128)S(1)}, f32[88,256]{1,0:T(8,128)S(1)}, u32[]{:S(2)}, u32[]{:S(2)}) %collective-permute-start.6) | collective-permute-done | bytes 90144 | tf_op jit(solution)/shard_map/ppermute | solution.py:29
  90.8 12.9 %all_to_all.43 = f32[8,88,256]{2,1,0:T(8,128)S(1)} all-to-all(f32[8,88,256]{2,1,0:T(8,128)S(1)} %broadcast_in_dim.4), channel_id=1, replica_groups=mesh['prow'=8,'x'=4,'zl'=2,'y'=4] {'x','zl'}, dimensions={0} | all-to-all | bytes 1441792 | tf_op jit(solution)/shard_map/all_to_all | solution.py:31
  103.7 0.0 collective-permute-start.7
  103.7 0.0 copy-done.5
  103.8 0.1 scatter.14
  103.9 0.0 copy-start.1
  103.9 1.0 copy-done.1
  104.9 1.0 collective-permute-done.7
  105.9 0.2 maximum_select_fusion
  106.2 0.0 copy-start
  106.2 1.1 copy-done
  107.3 0.8 slice.206
  108.0 1.1 reshape.147
  109.1 0.0 copy-start.6
  109.2 1.1 fusion.42
  110.3 2.6 %fusion.7 = f32[512,512]{0,1:T(8,128)S(1)} fusion(f32[512,512]{0,1:T(8,128)} %copy-done.1, f32[704,512]{1,0:T(8,128)} %copy-done), kind=kOutput, calls=%fused_computation.16 | convolution fusion | flops 805306368 | bytes 3145728 | tf_op jit(solution)/shard_map/dot_general | solution.py:13
  112.9 0.3 slice_subtract_fusion.1
  113.2 0.2 fusion.38
  113.4 0.2 fusion.32
  113.7 0.3 slice_subtract_fusion
  114.0 0.4 slice_subtract_fusion.2
  114.4 7.9 %convolution_subtract_fusion = f32[512,1536]{1,0:T(8,128)} fusion(f32[512,1536]{1,0:T(8,128)} %bitcast.1, f32[1536,512]{1,0:T(8,128)S(1)} %constant_dynamic-update-slice_fusion, f32[512,128]{0,1:T(8,128)S(1)} %slice.204, f32[512,128]{0,1:T(8,128)S(1)} %slice_subtract_fusion.1, f32[512,128]{0,1:T(8,128)S(1)} %slice_subtract_fusion, ...), kind=kOutput, calls=%fused_computation.4 | convolution fusion | flops 2417491968 | bytes 10485760 | tf_op jit(solution)/shard_map/dot_general | solution.py:13
  122.4 3.7 %all-to-all-start.3 = ((f32[8,64,1536]{2,1,0:T(8,128)}), f32[8,64,1536]{2,1,0:T(8,128)S(1)}, u32[]{:S(2)}, u32[]{:S(2)}) async-start(f32[8,64,1536]{2,1,0:T(8,128)} %bitcast.45), calls=%async_computation.3 | async-start | bytes 6291456 | tf_op jit(solution)/shard_map/all_to_all | solution.py:96
  126.0 38.7 %all-to-all-done.3 = f32[8,64,1536]{2,1,0:T(8,128)S(1)} async-done(((f32[8,64,1536]{2,1,0:T(8,128)}), f32[8,64,1536]{2,1,0:T(8,128)S(1)}, u32[]{:S(2)}, u32[]{:S(2)}) %all-to-all-start.3) | async-done | bytes 3145760 | tf_op jit(solution)/shard_map/all_to_all | solution.py:96
  164.8 0.7 fusion.1
  165.5 1.9 %copy.10 = f32[8,8,8,1536]{3,2,0,1:T(8,128)} copy(f32[8,8,8,1536]{3,2,1,0:T(8,128)S(1)} %fusion.1) | data formatting | bytes 6291456 | tf_op jit(solution)/shard_map/reshape | solution.py:97
  (15 shorter events, 0.2 us)
Async XLA Ops:
  4.5 5.8 %copy-start.7 = (f32[384,512]{1,0:T(8,128)S(1)}, f32[384,512]{1,0:T(8,128)}, u32[]{:S(2)}) copy-start(f32[384,512]{1,0:T(8,128)} %param.12) | copy-start | bytes 2359300
  4.5 45.7 %all-to-all-start = ((f32[64,8,1536]{2,0,1:T(8,128)}), f32[64,8,1536]{2,0,1:T(8,128)}, u32[]{:S(2)}, u32[]{:S(2)}) async-start(f32[64,8,1536]{2,0,1:T(8,128)} %fusion.2), calls=%async_computation | async-start | bytes 6291456 | tf_op jit(solution)/shard_map/all_to_all | solution.py:67
  10.3 20.4 %collective-permute-start.1 = (f32[384,512]{1,0:T(8,128)S(1)}, f32[384,512]{1,0:T(8,128)S(1)}, u32[]{:S(2)}, u32[]{:S(2)}) collective-permute-start(f32[384,512]{1,0:T(8,128)S(1)} %copy-done.7), channel_id=1, source_target_pairs={{0,1},{1,2},{2,3},{3,0},{4,5},{5,6},{6,7},{7,4},{8,9},{9,10},{10,1... | collective-permute-start | bytes 2359304 | tf_op jit(solution)/shard_map/ppermute | solution.py:40
  12.0 20.7 %collective-permute-start = (f32[384,512]{1,0:T(8,128)S(1)}, f32[384,512]{1,0:T(8,128)S(1)}, u32[]{:S(2)}, u32[]{:S(2)}) collective-permute-start(f32[384,512]{1,0:T(8,128)S(1)} %copy-done.7), channel_id=1, source_target_pairs={{0,3},{1,0},{2,1},{3,2},{4,7},{5,4},{6,5},{7,6},{8,11},{9,8},{10,9... | collective-permute-start | bytes 2359304 | tf_op jit(solution)/shard_map/ppermute | solution.py:41
  30.7 0.9 copy-start.2
  32.3 11.3 %collective-permute-start.2 = (f32[192,512]{1,0:T(8,128)}, f32[192,512]{1,0:T(8,128)S(1)}, u32[]{:S(2)}, u32[]{:S(2)}) collective-permute-start(f32[192,512]{1,0:T(8,128)} %slice.192), channel_id=1, source_target_pairs={{0,1},{1,2},{2,3},{3,0},{4,5},{5,6},{6,7},{7,4},{8,9},{9,10},{10,1... | collective-permute-start | bytes 1179656 | tf_op jit(solution)/shard_map/ppermute | solution.py:43
  32.6 0.9 copy-start.4
  34.3 10.3 %collective-permute-start.3 = (f32[192,512]{1,0:T(8,128)}, f32[192,512]{1,0:T(8,128)}, u32[]{:S(2)}, u32[]{:S(2)}) collective-permute-start(f32[192,512]{1,0:T(8,128)} %slice.193), channel_id=1, source_target_pairs={{0,3},{1,0},{2,1},{3,2},{4,7},{5,4},{6,5},{7,6},{8,11},{9,8},{10,9... | collective-permute-start | bytes 1179656 | tf_op jit(solution)/shard_map/ppermute | solution.py:44
  37.3 8.4 %copy-start.3 = (f32[384,512]{1,0:T(8,128)S(1)}, f32[384,512]{1,0:T(8,128)}, u32[]{:S(2)}) copy-start(f32[384,512]{1,0:T(8,128)} %copy-done.2) | copy-start | bytes 2359300
  54.9 2.3 %collective-permute-start.4 = (f32[704,256]{1,0:T(8,128)S(1)}, f32[704,256]{1,0:T(8,128)S(1)}, u32[]{:S(2)}, u32[]{:S(2)}) collective-permute-start(f32[704,256]{1,0:T(8,128)S(1)} %broadcast_select_fusion), channel_id=1, source_target_pairs={{0,32},{32,0},{64,96},{96,64},{128,160},{160,128},{192,224},{224,1... | collective-permute-start | bytes 2162696 | tf_op jit(solution)/shard_map/ppermute | solution.py:23
  57.4 46.3 %copy-start.5 = (f32[4,128,128]{2,1,0:T(8,128)S(1)}, f32[4,128,128]{2,1,0:T(8,128)}, u32[]{:S(2)}) copy-start(f32[4,128,128]{2,1,0:T(8,128)} %param.13) | copy-start | bytes 786436
  76.1 5.6 %collective-permute-start.5 = (f32[88,256]{1,0:T(8,128)S(1)}, f32[88,256]{1,0:T(8,128)S(1)}, u32[]{:S(2)}, u32[]{:S(2)}) collective-permute-start(f32[88,256]{1,0:T(8,128)S(1)} %reduce_sum.9), channel_id=1, source_target_pairs={{0,64},{32,96},{64,0},{96,32},{128,192},{160,224},{192,128},{224,1... | collective-permute-start | bytes 270344 | tf_op jit(solution)/shard_map/ppermute | solution.py:29
  81.7 9.0 %collective-permute-start.6 = (f32[88,256]{1,0:T(8,128)S(1)}, f32[88,256]{1,0:T(8,128)S(1)}, u32[]{:S(2)}, u32[]{:S(2)}) collective-permute-start(f32[88,256]{1,0:T(8,128)S(1)} %add.35), channel_id=1, source_target_pairs={{0,128},{32,160},{64,192},{96,224},{128,0},{160,32},{192,64},{224,... | collective-permute-start | bytes 270344 | tf_op jit(solution)/shard_map/ppermute | solution.py:29
  103.7 2.2 %collective-permute-start.7 = (f32[704,256]{1,0:T(8,128)S(1)}, f32[704,256]{1,0:T(8,128)S(1)}, u32[]{:S(2)}, u32[]{:S(2)}) collective-permute-start(f32[704,256]{1,0:T(8,128)S(1)} %bitcast.47), channel_id=1, source_target_pairs={{0,32},{32,0},{64,96},{96,64},{128,160},{160,128},{192,224},{224,1... | collective-permute-start | bytes 2162696 | tf_op jit(solution)/shard_map/ppermute | solution.py:33
  103.9 1.0 copy-start.1
  106.2 1.1 copy-start
  109.1 4.1 %copy-start.6 = (f32[4,128,128]{2,1,0:T(8,128)S(1)}, f32[4,128,128]{2,1,0:T(8,128)}, u32[]{:S(2)}) copy-start(f32[4,128,128]{2,1,0:T(8,128)} %param.13) | copy-start | bytes 786436
  122.4 42.4 %all-to-all-start.3 = ((f32[8,64,1536]{2,1,0:T(8,128)}), f32[8,64,1536]{2,1,0:T(8,128)S(1)}, u32[]{:S(2)}, u32[]{:S(2)}) async-start(f32[8,64,1536]{2,1,0:T(8,128)} %bitcast.45), calls=%async_computation.3 | async-start | bytes 6291456 | tf_op jit(solution)/shard_map/all_to_all | solution.py:96

commit v14 on v13

--- a/solution.py
+++ b/solution.py
@@ -24,10 +24,11 @@
     chunk = -(-rows // (8 * outer_size)) * 8
     mine = jnp.pad(mine, ((0, chunk * outer_size - rows), (0, 0))).reshape(outer_size, chunk, half)
     total = jnp.sum(lax.all_to_all(mine, outer, 0, 0, tiled=True), axis=0)
-    bit = 2
-    while bit < inner_size:
-        total = total + lax.ppermute(total, inner, [(i, i ^ bit) for i in range(inner_size)])
-        bit *= 2
+    peers = inner_size // 2
+    terms = [total]
+    for step in range(1, peers):
+        terms.append(lax.ppermute(total, inner, [(i, ((i // 2 + step) % peers) * 2 + i % 2) for i in range(inner_size)]))
+    total = sum(terms[1:], terms[0])
     total = lax.all_to_all(jnp.broadcast_to(total, (outer_size, chunk, half)), outer, 0, 0, tiled=True)
     mine = total.reshape(outer_size * chunk, half)[:rows]
     other = lax.ppermute(mine, inner, pairs)

time: 170 us -> 171 us (level)
  starting transfers between devices: 20.8 us -> 23.6 us
  waiting for transfers between devices: 73.8 us -> 71.2 us
    ppermute x2 -> x3, starting transfers between devices: 4.67 us -> 7.49 us  [all_reduce(): lax.ppermute(total, inner, [(i, (i // 2 + step) % peers * 2 + i % 2) for...]
    ppermute x2 -> x3, waiting for transfers between devices: 9.92 us -> 7.34 us  [all_reduce(): lax.ppermute(total, inner, [(i, (i // 2 + step) % peers * 2 + i % 2) for...]
  transfers between devices with their start and end apart: 10 -> 11, of which waited for: 8 -> 9; matrix products, arithmetic and copies ran while one was open for 6% -> 6% of each run, Pallas kernels for 0% -> 0%
where the time goes in v14:
time: 171 us; the launch traced here: 169 us
  waiting for transfers between devices  71.2 us (42%)
  blocking collectives  31.6 us (18%)
  starting transfers between devices  23.6 us (14%)
  matrix products  20.2 us (12%)
  local copies, waits for them, and re-layouts  16.3 us (10%)
  other arithmetic  5.62 us (3%)
    all_to_all x1, waiting for transfers between devices, per_device(): work = lax.all_to_all(work, GROUP, 0, 1, tiled=True)  38.7 us
    dot_general x12, matrix products, matmul(): jnp.dot(left, right, precision=lax.Precision.HIGH, preferred_element_type...  20.2 us
    all_to_all x1, blocking collectives, all_reduce(): total = jnp.sum(lax.all_to_all(mine, outer, 0, 0, tiled=True), axis=0)  17.5 us
    ppermute x1, waiting for transfers between devices, gather_ring(): from_left = lax.ppermute(block, axis, right)  17 us
    all_to_all x1, blocking collectives, all_reduce(): lax.all_to_all(jnp.broadcast_to(total, (outer_size, chunk, half)), outer,...  14.1 us
    ppermute x3, starting transfers between devices, all_reduce(): lax.ppermute(total, inner, [(i, (i // 2 + step) % peers * 2 + i % 2) for...  7.49 us
    unnamed x20, local copies, waits for them, and re-layouts  7.37 us
    ppermute x3, waiting for transfers between devices, all_reduce(): lax.ppermute(total, inner, [(i, (i // 2 + step) % peers * 2 + i % 2) for...  7.34 us
  transfers between devices with their start and end apart: 11, of which 9 were waited for; matrix products, arithmetic and copies ran while one was open for 6% of the time, Pallas kernels for 0%

profile of v14, /device:TPU:64, one launch (start us, length us, event | category | flops | bytes accessed | tf_op | source)
XLA Modules:
  0.0 168.8 jit_solution(1339855741351984479)
XLA Ops:
  0.0 2.2 %copy.12 = f32[8,8,8,1536]{3,2,0,1:T(8,128)S(1)} copy(f32[8,8,8,1536]{3,2,1,0:T(8,128)} %bitcast.46) | data formatting | bytes 6291456 | tf_op jit(solution)/shard_map/reshape | solution.py:67
  2.2 2.4 %fusion.2 = f32[64,8,1536]{2,0,1:T(8,128)} fusion(s32[]{:T(128)S(6)} %select_n.38, f32[64,8,1536]{2,0,1:T(8,128)S(1)} %bitcast.44), kind=kLoop, calls=%fused_computation.7 | loop fusion | flops 786432 | bytes 6291460 | tf_op jit(solution)/shard_map/concatenate | solution.py:51
  4.5 5.8 %all-to-all-start = ((f32[64,8,1536]{2,0,1:T(8,128)}), f32[64,8,1536]{2,0,1:T(8,128)}, u32[]{:S(2)}, u32[]{:S(2)}) async-start(f32[64,8,1536]{2,0,1:T(8,128)} %fusion.2), calls=%async_computation | async-start | bytes 6291456 | tf_op jit(solution)/shard_map/all_to_all | solution.py:68
  10.3 0.0 copy-done.7
  10.3 1.7 collective-permute-start.1
  12.0 1.7 collective-permute-start
  13.6 17.0 %collective-permute-done.1 = f32[384,512]{1,0:T(8,128)S(1)} collective-permute-done((f32[384,512]{1,0:T(8,128)S(1)}, f32[384,512]{1,0:T(8,128)S(1)}, u32[]{:S(2)}, u32[]{:S(2)}) %collective-permute-start.1) | collective-permute-done | bytes 786464 | tf_op jit(solution)/shard_map/ppermute | solution.py:41
  30.7 0.9 copy-done.2
  31.6 0.8 slice.192
  32.3 0.3 collective-permute-start.2
  32.6 0.0 collective-permute-done
  32.7 0.9 copy-done.4
  33.5 0.8 slice.193
  34.3 2.9 %collective-permute-start.3 = (f32[192,512]{1,0:T(8,128)}, f32[192,512]{1,0:T(8,128)}, u32[]{:S(2)}, u32[]{:S(2)}) collective-permute-start(f32[192,512]{1,0:T(8,128)} %slice.193), channel_id=1, source_target_pairs={{0,3},{1,0},{2,1},{3,2},{4,7},{5,4},{6,5},{7,6},{8,11},{9,8},{10,9... | collective-permute-start | bytes 1179656 | tf_op jit(solution)/shard_map/ppermute | solution.py:45
  37.3 1.3 constant_dynamic-update-slice_fusion.4
  38.5 1.2 constant_dynamic-update-slice_fusion.3
  39.7 3.9 %collective-permute-done.2 = f32[192,512]{1,0:T(8,128)S(1)} collective-permute-done((f32[192,512]{1,0:T(8,128)}, f32[192,512]{1,0:T(8,128)S(1)}, u32[]{:S(2)}, u32[]{:S(2)}) %collective-permute-start.2) | collective-permute-done | bytes 393248 | tf_op jit(solution)/shard_map/ppermute | solution.py:44
  43.6 1.0 collective-permute-done.3
  44.7 1.0 constant_dynamic-update-slice_fusion.1
  45.7 0.1 constant_dynamic-update-slice_fusion
  45.8 0.8 fusion.18
  46.5 0.8 fusion.5
  47.4 0.9 fusion.3
  48.3 0.8 pad_maximum_fusion.1
  49.1 1.1 reshape.144
  50.2 0.0 all-to-all-done
  50.2 4.6 %fusion.64 = f32[512,512]{1,0:T(8,128)S(1)} fusion(f32[512,1536]{1,0:T(8,128)} %bitcast.1, f32[1536,512]{1,0:T(8,128)S(1)} %constant_dynamic-update-slice_fusion), kind=kOutput, calls=%fused_computation.84 | convolution fusion | flops 2415919104 | bytes 7340032 | tf_op jit(solution)/shard_map/dot_general | solution.py:13
  54.8 0.1 broadcast_select_fusion
  54.9 0.1 collective-permute-start.4
  55.0 2.2 %collective-permute-done.4 = f32[704,256]{1,0:T(8,128)S(1)} collective-permute-done((f32[704,256]{1,0:T(8,128)S(1)}, f32[704,256]{1,0:T(8,128)S(1)}, u32[]{:S(2)}, u32[]{:S(2)}) %collective-permute-start.4) | collective-permute-done | bytes 720928 | tf_op jit(solution)/shard_map/ppermute | solution.py:23
  57.2 0.2 select_add_fusion
  57.4 0.0 copy-start.5
  57.4 17.5 %all_to_all.42 = f32[8,88,256]{2,1,0:T(8,128)} all-to-all(f32[8,88,256]{2,1,0:T(8,128)S(1)} %bitcast.49), channel_id=1, replica_groups=mesh['prow'=8,'x'=4,'zl'=2,'y'=4] {'x','zl'}, dimensions={0} | all-to-all | bytes 1441792 | tf_op jit(solution)/shard_map/all_to_all | solution.py:26
  74.9 1.2 reduce_sum.9
  76.1 3.7 %collective-permute-start.5 = (f32[88,256]{1,0:T(8,128)S(1)}, f32[88,256]{1,0:T(8,128)S(1)}, u32[]{:S(2)}, u32[]{:S(2)}) collective-permute-start(f32[88,256]{1,0:T(8,128)S(1)} %reduce_sum.9), channel_id=1, source_target_pairs={{0,64},{32,96},{64,128},{96,160},{128,192},{160,224},{192,0},{224,... | collective-permute-start | bytes 270344 | tf_op jit(solution)/shard_map/ppermute | solution.py:30
  79.7 1.0 collective-permute-start.6
  80.8 2.8 %collective-permute-start.7 = (f32[88,256]{1,0:T(8,128)S(1)}, f32[88,256]{1,0:T(8,128)S(1)}, u32[]{:S(2)}, u32[]{:S(2)}) collective-permute-start(f32[88,256]{1,0:T(8,128)S(1)} %reduce_sum.9), channel_id=1, source_target_pairs={{0,192},{32,224},{64,0},{96,32},{128,64},{160,96},{192,128},{224,1... | collective-permute-start | bytes 270344 | tf_op jit(solution)/shard_map/ppermute | solution.py:30
  83.6 0.3 collective-permute-done.5
  83.9 5.3 %collective-permute-done.6 = f32[88,256]{1,0:T(8,128)S(1)} collective-permute-done((f32[88,256]{1,0:T(8,128)S(1)}, f32[88,256]{1,0:T(8,128)S(1)}, u32[]{:S(2)}, u32[]{:S(2)}) %collective-permute-start.6) | collective-permute-done | bytes 90144 | tf_op jit(solution)/shard_map/ppermute | solution.py:30
  89.1 1.8 %collective-permute-done.7 = f32[88,256]{1,0:T(8,128)S(1)} collective-permute-done((f32[88,256]{1,0:T(8,128)S(1)}, f32[88,256]{1,0:T(8,128)S(1)}, u32[]{:S(2)}, u32[]{:S(2)}) %collective-permute-start.7) | collective-permute-done | bytes 90144 | tf_op jit(solution)/shard_map/ppermute | solution.py:30
  91.0 14.1 %all_to_all.43 = f32[8,88,256]{2,1,0:T(8,128)S(1)} all-to-all(f32[8,88,256]{2,1,0:T(8,128)S(1)} %broadcast_in_dim.4), channel_id=1, replica_groups=mesh['prow'=8,'x'=4,'zl'=2,'y'=4] {'x','zl'}, dimensions={0} | all-to-all | bytes 1441792 | tf_op jit(solution)/shard_map/all_to_all | solution.py:32
  105.1 0.0 collective-permute-start.8
  105.2 0.1 scatter.14
  105.3 1.0 copy-done.1
  106.3 1.0 collective-permute-done.8
  107.3 0.2 maximum_select_fusion
  107.5 0.0 copy-start
  107.6 1.1 copy-done
  108.6 0.8 slice.206
  109.4 1.1 reshape.147
  110.5 0.0 copy-start.6
  110.6 1.1 fusion.42
  111.7 2.6 %fusion.7 = f32[512,512]{0,1:T(8,128)S(1)} fusion(f32[512,512]{0,1:T(8,128)} %copy-done.1, f32[704,512]{1,0:T(8,128)} %copy-done), kind=kOutput, calls=%fused_computation.16 | convolution fusion | flops 805306368 | bytes 3145728 | tf_op jit(solution)/shard_map/dot_general | solution.py:13
  114.3 0.3 slice_subtract_fusion.1
  114.6 0.0 copy-done.6
  114.6 0.2 fusion.38
  114.8 0.2 fusion.32
  115.1 0.3 slice_subtract_fusion
  115.4 0.4 slice_subtract_fusion.2
  115.8 7.9 %convolution_subtract_fusion = f32[512,1536]{1,0:T(8,128)} fusion(f32[512,1536]{1,0:T(8,128)} %bitcast.1, f32[1536,512]{1,0:T(8,128)S(1)} %constant_dynamic-update-slice_fusion, f32[512,128]{0,1:T(8,128)S(1)} %slice.204, f32[512,128]{0,1:T(8,128)S(1)} %slice_subtract_fusion.1, f32[512,128]{0,1:T(8,128)S(1)} %slice_subtract_fusion, ...), kind=kOutput, calls=%fused_computation.4 | convolution fusion | flops 2417491968 | bytes 10485760 | tf_op jit(solution)/shard_map/dot_general | solution.py:13
  123.8 3.7 %all-to-all-start.3 = ((f32[8,64,1536]{2,1,0:T(8,128)}), f32[8,64,1536]{2,1,0:T(8,128)S(1)}, u32[]{:S(2)}, u32[]{:S(2)}) async-start(f32[8,64,1536]{2,1,0:T(8,128)} %bitcast.45), calls=%async_computation.3 | async-start | bytes 6291456 | tf_op jit(solution)/shard_map/all_to_all | solution.py:97
  127.4 38.7 %all-to-all-done.3 = f32[8,64,1536]{2,1,0:T(8,128)S(1)} async-done(((f32[8,64,1536]{2,1,0:T(8,128)}), f32[8,64,1536]{2,1,0:T(8,128)S(1)}, u32[]{:S(2)}, u32[]{:S(2)}) %all-to-all-start.3) | async-done | bytes 3145760 | tf_op jit(solution)/shard_map/all_to_all | solution.py:97
  166.1 0.7 fusion.1
  166.9 1.9 %copy.10 = f32[8,8,8,1536]{3,2,0,1:T(8,128)} copy(f32[8,8,8,1536]{3,2,1,0:T(8,128)S(1)} %fusion.1) | data formatting | bytes 6291456 | tf_op jit(solution)/shard_map/reshape | solution.py:98
  (16 shorter events, 0.2 us)
Async XLA Ops:
  4.5 5.8 %copy-start.7 = (f32[384,512]{1,0:T(8,128)S(1)}, f32[384,512]{1,0:T(8,128)}, u32[]{:S(2)}) copy-start(f32[384,512]{1,0:T(8,128)} %param.12) | copy-start | bytes 2359300
  4.5 45.7 %all-to-all-start = ((f32[64,8,1536]{2,0,1:T(8,128)}), f32[64,8,1536]{2,0,1:T(8,128)}, u32[]{:S(2)}, u32[]{:S(2)}) async-start(f32[64,8,1536]{2,0,1:T(8,128)} %fusion.2), calls=%async_computation | async-start | bytes 6291456 | tf_op jit(solution)/shard_map/all_to_all | solution.py:68
  10.3 20.4 %collective-permute-start.1 = (f32[384,512]{1,0:T(8,128)S(1)}, f32[384,512]{1,0:T(8,128)S(1)}, u32[]{:S(2)}, u32[]{:S(2)}) collective-permute-start(f32[384,512]{1,0:T(8,128)S(1)} %copy-done.7), channel_id=1, source_target_pairs={{0,1},{1,2},{2,3},{3,0},{4,5},{5,6},{6,7},{7,4},{8,9},{9,10},{10,1... | collective-permute-start | bytes 2359304 | tf_op jit(solution)/shard_map/ppermute | solution.py:41
  12.0 20.7 %collective-permute-start = (f32[384,512]{1,0:T(8,128)S(1)}, f32[384,512]{1,0:T(8,128)S(1)}, u32[]{:S(2)}, u32[]{:S(2)}) collective-permute-start(f32[384,512]{1,0:T(8,128)S(1)} %copy-done.7), channel_id=1, source_target_pairs={{0,3},{1,0},{2,1},{3,2},{4,7},{5,4},{6,5},{7,6},{8,11},{9,8},{10,9... | collective-permute-start | bytes 2359304 | tf_op jit(solution)/shard_map/ppermute | solution.py:42
  30.7 0.9 copy-start.2
  32.3 11.3 %collective-permute-start.2 = (f32[192,512]{1,0:T(8,128)}, f32[192,512]{1,0:T(8,128)S(1)}, u32[]{:S(2)}, u32[]{:S(2)}) collective-permute-start(f32[192,512]{1,0:T(8,128)} %slice.192), channel_id=1, source_target_pairs={{0,1},{1,2},{2,3},{3,0},{4,5},{5,6},{6,7},{7,4},{8,9},{9,10},{10,1... | collective-permute-start | bytes 1179656 | tf_op jit(solution)/shard_map/ppermute | solution.py:44
  32.7 0.9 copy-start.4
  34.3 10.3 %collective-permute-start.3 = (f32[192,512]{1,0:T(8,128)}, f32[192,512]{1,0:T(8,128)}, u32[]{:S(2)}, u32[]{:S(2)}) collective-permute-start(f32[192,512]{1,0:T(8,128)} %slice.193), channel_id=1, source_target_pairs={{0,3},{1,0},{2,1},{3,2},{4,7},{5,4},{6,5},{7,6},{8,11},{9,8},{10,9... | collective-permute-start | bytes 1179656 | tf_op jit(solution)/shard_map/ppermute | solution.py:45
  37.3 8.4 %copy-start.3 = (f32[384,512]{1,0:T(8,128)S(1)}, f32[384,512]{1,0:T(8,128)}, u32[]{:S(2)}) copy-start(f32[384,512]{1,0:T(8,128)} %copy-done.2) | copy-start | bytes 2359300
  54.9 2.3 %collective-permute-start.4 = (f32[704,256]{1,0:T(8,128)S(1)}, f32[704,256]{1,0:T(8,128)S(1)}, u32[]{:S(2)}, u32[]{:S(2)}) collective-permute-start(f32[704,256]{1,0:T(8,128)S(1)} %broadcast_select_fusion), channel_id=1, source_target_pairs={{0,32},{32,0},{64,96},{96,64},{128,160},{160,128},{192,224},{224,1... | collective-permute-start | bytes 2162696 | tf_op jit(solution)/shard_map/ppermute | solution.py:23
  57.4 47.7 %copy-start.5 = (f32[4,128,128]{2,1,0:T(8,128)S(1)}, f32[4,128,128]{2,1,0:T(8,128)}, u32[]{:S(2)}) copy-start(f32[4,128,128]{2,1,0:T(8,128)} %param.13) | copy-start | bytes 786436
  76.1 7.8 %collective-permute-start.5 = (f32[88,256]{1,0:T(8,128)S(1)}, f32[88,256]{1,0:T(8,128)S(1)}, u32[]{:S(2)}, u32[]{:S(2)}) collective-permute-start(f32[88,256]{1,0:T(8,128)S(1)} %reduce_sum.9), channel_id=1, source_target_pairs={{0,64},{32,96},{64,128},{96,160},{128,192},{160,224},{192,0},{224,... | collective-permute-start | bytes 270344 | tf_op jit(solution)/shard_map/ppermute | solution.py:30
  79.7 9.4 %collective-permute-start.6 = (f32[88,256]{1,0:T(8,128)S(1)}, f32[88,256]{1,0:T(8,128)S(1)}, u32[]{:S(2)}, u32[]{:S(2)}) collective-permute-start(f32[88,256]{1,0:T(8,128)S(1)} %reduce_sum.9), channel_id=1, source_target_pairs={{0,128},{32,160},{64,192},{96,224},{128,0},{160,32},{192,64},{224,... | collective-permute-start | bytes 270344 | tf_op jit(solution)/shard_map/ppermute | solution.py:30
  80.8 10.2 %collective-permute-start.7 = (f32[88,256]{1,0:T(8,128)S(1)}, f32[88,256]{1,0:T(8,128)S(1)}, u32[]{:S(2)}, u32[]{:S(2)}) collective-permute-start(f32[88,256]{1,0:T(8,128)S(1)} %reduce_sum.9), channel_id=1, source_target_pairs={{0,192},{32,224},{64,0},{96,32},{128,64},{160,96},{192,128},{224,1... | collective-permute-start | bytes 270344 | tf_op jit(solution)/shard_map/ppermute | solution.py:30
  105.1 2.2 %collective-permute-start.8 = (f32[704,256]{1,0:T(8,128)S(1)}, f32[704,256]{1,0:T(8,128)S(1)}, u32[]{:S(2)}, u32[]{:S(2)}) collective-permute-start(f32[704,256]{1,0:T(8,128)S(1)} %bitcast.47), channel_id=1, source_target_pairs={{0,32},{32,0},{64,96},{96,64},{128,160},{160,128},{192,224},{224,1... | collective-permute-start | bytes 2162696 | tf_op jit(solution)/shard_map/ppermute | solution.py:34
  105.3 1.0 copy-start.1
  107.5 1.1 copy-start
  110.5 4.1 %copy-start.6 = (f32[4,128,128]{2,1,0:T(8,128)S(1)}, f32[4,128,128]{2,1,0:T(8,128)}, u32[]{:S(2)}) copy-start(f32[4,128,128]{2,1,0:T(8,128)} %param.13) | copy-start | bytes 786436
  123.8 42.4 %all-to-all-start.3 = ((f32[8,64,1536]{2,1,0:T(8,128)}), f32[8,64,1536]{2,1,0:T(8,128)S(1)}, u32[]{:S(2)}, u32[]{:S(2)}) async-start(f32[8,64,1536]{2,1,0:T(8,128)} %bitcast.45), calls=%async_computation.3 | async-start | bytes 6291456 | tf_op jit(solution)/shard_map/all_to_all | solution.py:97

commit v15 on v13

--- a/solution.py
+++ b/solution.py
@@ -67,16 +67,15 @@
     work = lax.all_to_all(work, GROUP, 1, 0, tiled=True)
 
     products = matmul(work, basis)
-    grams = jnp.concatenate([matmul(basis[:, j * width : (j + 1) * width].T, basis[:, : j * width]) for j in range(1, count)], axis=1)
-    lanes = products.shape[1]
-    packed = jnp.concatenate([products, grams.reshape(-1, lanes)], axis=0)
+    top = jnp.concatenate([matmul(basis[:, 3 * width : 4 * width].T, basis[:, : 3 * width]), matmul(basis[:, 2 * width : 3 * width].T, basis[:, width : 2 * width])], axis=1)
+    low = matmul(jnp.concatenate([basis[:, 2 * width : 3 * width], basis[:, width : 2 * width]], axis=1).T, basis[:, :width])
+    low = jnp.concatenate([low[:width], low[width:], jnp.zeros((width, 2 * width), low.dtype)], axis=1)
+    packed = jnp.concatenate([products, top, low], axis=0)
     packed = all_reduce(packed, GROUP, "prow", ng, nprow)
     span = products.shape[0]
-    grams = packed[span:].reshape(grams.shape)
-    gram, offset = {}, 0
-    for j in range(1, count):
-        for k in range(j):
-            gram[j, k], offset = grams[:, offset : offset + width], offset + width
+    top, low = packed[span : span + width], packed[span + width :]
+    gram = {(3, 0): top[:, :width], (3, 1): top[:, width : 2 * width], (3, 2): top[:, 2 * width : 3 * width], (2, 1): top[:, 3 * width :],
+            (2, 0): low[:, :width], (1, 0): low[:, width : 2 * width]}
 
     diagonal = jnp.zeros((count * width, count * width), tfactors.dtype)
     for k in range(count):

time: 170 us -> 169 us (level)
  blocking collectives: 30.5 us -> 36.6 us
  local copies, waits for them, and re-layouts: 16.3 us -> 11.4 us
  matrix products: 20.2 us -> 18.4 us
    all_to_all x1, blocking collectives: 12.9 us -> 18.5 us  [all_reduce(): lax.all_to_all(jnp.broadcast_to(total, (outer_size, chunk, half)), outer,...]
    reshape x2 -> x0, local copies, waits for them, and re-layouts: 2.2 us -> none  [the longest x1 1.11 us: per_device(): packed = jnp.concatenate([products, grams.reshape(-1, lanes)], axis=0)]
    unnamed x20 -> x14, local copies, waits for them, and re-layouts: 7.37 us -> 5.29 us
    dot_general x12, matrix products: 20.2 us -> 18.4 us  [matmul(): jnp.dot(left, right, precision=lax.Precision.HIGH, preferred_element_type...]
  transfers between devices with their start and end apart: 10 -> 10, of which waited for: 8 -> 8; matrix products, arithmetic and copies ran while one was open for 6% -> 5% of each run, Pallas kernels for 0% -> 0%
where the time goes in v15:
time: 169 us; the launch traced here: 168 us
  waiting for transfers between devices  74.8 us (44%)
  blocking collectives  36.6 us (22%)
  starting transfers between devices  20.9 us (12%)
  matrix products  18.4 us (11%)
  local copies, waits for them, and re-layouts  11.4 us (7%)
  other arithmetic  5.06 us (3%)
    all_to_all x1, waiting for transfers between devices, per_device(): work = lax.all_to_all(work, GROUP, 0, 1, tiled=True)  38.7 us
    all_to_all x1, blocking collectives, all_reduce(): lax.all_to_all(jnp.broadcast_to(total, (outer_size, chunk, half)), outer,...  18.5 us
    dot_general x12, matrix products, matmul(): jnp.dot(left, right, precision=lax.Precision.HIGH, preferred_element_type...  18.4 us
    all_to_all x1, blocking collectives, all_reduce(): total = jnp.sum(lax.all_to_all(mine, outer, 0, 0, tiled=True), axis=0)  18.2 us
    ppermute x1, waiting for transfers between devices, gather_ring(): from_left = lax.ppermute(block, axis, right)  17 us
    ppermute x2, waiting for transfers between devices, all_reduce(): lax.ppermute(total, inner, [(i, i ^ bit) for i in range(inner_size)])  9.8 us
    all_to_all x1, starting transfers between devices, per_device(): work = lax.all_to_all(work, GROUP, 1, 0, tiled=True)  5.79 us
    unnamed x14, local copies, waits for them, and re-layouts  5.29 us
  transfers between devices with their start and end apart: 10, of which 8 were waited for; matrix products, arithmetic and copies ran while one was open for 5% of the time, Pallas kernels for 0%

profile of v15, /device:TPU:64, one launch (start us, length us, event | category | flops | bytes accessed | tf_op | source)
XLA Modules:
  0.0 167.5 jit_solution(10543819155198262392)
XLA Ops:
  0.0 2.2 %copy.15 = f32[8,8,8,1536]{3,2,0,1:T(8,128)S(1)} copy(f32[8,8,8,1536]{3,2,1,0:T(8,128)} %bitcast.46) | data formatting | bytes 6291456 | tf_op jit(solution)/shard_map/reshape | solution.py:66
  2.2 2.4 %fusion.2 = f32[64,8,1536]{2,0,1:T(8,128)} fusion(s32[]{:T(128)S(6)} %select_n.38, f32[64,8,1536]{2,0,1:T(8,128)S(1)} %bitcast.44), kind=kLoop, calls=%fused_computation.7 | loop fusion | flops 786432 | bytes 6291460 | tf_op jit(solution)/shard_map/concatenate | solution.py:50
  4.5 0.0 copy-start.4
  4.5 5.8 %all-to-all-start = ((f32[64,8,1536]{2,0,1:T(8,128)}), f32[64,8,1536]{2,0,1:T(8,128)}, u32[]{:S(2)}, u32[]{:S(2)}) async-start(f32[64,8,1536]{2,0,1:T(8,128)} %fusion.2), calls=%async_computation | async-start | bytes 6291456 | tf_op jit(solution)/shard_map/all_to_all | solution.py:67
  10.3 0.0 copy-done.4
  10.3 1.7 collective-permute-start.1
  12.0 1.7 collective-permute-start
  13.6 17.0 %collective-permute-done.1 = f32[384,512]{1,0:T(8,128)S(1)} collective-permute-done((f32[384,512]{1,0:T(8,128)S(1)}, f32[384,512]{1,0:T(8,128)S(1)}, u32[]{:S(2)}, u32[]{:S(2)}) %collective-permute-start.1) | collective-permute-done | bytes 786464 | tf_op jit(solution)/shard_map/ppermute | solution.py:40
  30.7 0.0 copy-start
  30.7 0.9 copy-done
  31.6 0.8 slice.200
  32.3 0.3 collective-permute-start.2
  32.6 0.0 collective-permute-done
  32.6 0.0 copy-start.2
  32.6 0.9 copy-done.2
  33.5 0.8 slice.201
  34.3 2.9 %collective-permute-start.3 = (f32[192,512]{1,0:T(8,128)}, f32[192,512]{1,0:T(8,128)}, u32[]{:S(2)}, u32[]{:S(2)}) collective-permute-start(f32[192,512]{1,0:T(8,128)} %slice.201), channel_id=1, source_target_pairs={{0,3},{1,0},{2,1},{3,2},{4,7},{5,4},{6,5},{7,6},{8,11},{9,8},{10,9... | collective-permute-start | bytes 1179656 | tf_op jit(solution)/shard_map/ppermute | solution.py:44
  37.3 0.0 copy-start.1
  37.3 1.3 constant_dynamic-update-slice_fusion.4
  38.5 1.2 constant_dynamic-update-slice_fusion.3
  39.7 3.9 %collective-permute-done.2 = f32[192,512]{1,0:T(8,128)S(1)} collective-permute-done((f32[192,512]{1,0:T(8,128)}, f32[192,512]{1,0:T(8,128)S(1)}, u32[]{:S(2)}, u32[]{:S(2)}) %collective-permute-start.2) | collective-permute-done | bytes 393248 | tf_op jit(solution)/shard_map/ppermute | solution.py:43
  43.6 1.0 collective-permute-done.3
  44.7 1.0 constant_dynamic-update-slice_fusion.1
  45.7 0.0 copy-done.1
  45.7 0.1 constant_dynamic-update-slice_fusion
  45.7 0.1 fusion.63
  45.9 1.4 fusion.5
  47.3 0.8 fusion.60
  48.1 0.9 fusion.3
  49.0 0.0 all-to-all-done
  49.0 4.6 %fusion.66 = f32[512,512]{1,0:T(8,128)S(1)} fusion(f32[512,1536]{1,0:T(8,128)} %bitcast.1, f32[1536,512]{1,0:T(8,128)S(1)} %constant_dynamic-update-slice_fusion), kind=kOutput, calls=%fused_computation.82 | convolution fusion | flops 2415919104 | bytes 7340032 | tf_op jit(solution)/shard_map/dot_general | solution.py:13
  53.6 0.2 maximum_maximum_fusion
  53.8 0.1 slice_select_fusion
  53.9 0.1 collective-permute-start.4
  54.0 2.3 %collective-permute-done.4 = f32[768,256]{1,0:T(8,128)S(1)} collective-permute-done((f32[768,256]{1,0:T(8,128)S(1)}, f32[768,256]{1,0:T(8,128)S(1)}, u32[]{:S(2)}, u32[]{:S(2)}) %collective-permute-start.4) | collective-permute-done | bytes 786464 | tf_op jit(solution)/shard_map/ppermute | solution.py:23
  56.3 0.2 select_add_fusion
  56.5 0.0 copy-start.3
  56.5 18.2 %all_to_all.42 = f32[8,96,256]{2,1,0:T(8,128)} all-to-all(f32[8,96,256]{2,1,0:T(8,128)S(1)} %bitcast.49), channel_id=1, replica_groups=mesh['prow'=8,'x'=4,'zl'=2,'y'=4] {'x','zl'}, dimensions={0} | all-to-all | bytes 1572864 | tf_op jit(solution)/shard_map/all_to_all | solution.py:26
  74.7 1.2 reduce_sum.9
  75.9 0.1 collective-permute-start.5
  76.0 5.6 %collective-permute-done.5 = f32[96,256]{1,0:T(8,128)S(1)} collective-permute-done((f32[96,256]{1,0:T(8,128)S(1)}, f32[96,256]{1,0:T(8,128)S(1)}, u32[]{:S(2)}, u32[]{:S(2)}) %collective-permute-start.5) | collective-permute-done | bytes 98336 | tf_op jit(solution)/shard_map/ppermute | solution.py:29
  81.6 4.8 %collective-permute-start.6 = (f32[96,256]{1,0:T(8,128)S(1)}, f32[96,256]{1,0:T(8,128)S(1)}, u32[]{:S(2)}, u32[]{:S(2)}) collective-permute-start(f32[96,256]{1,0:T(8,128)S(1)} %add.35), channel_id=1, source_target_pairs={{0,128},{32,160},{64,192},{96,224},{128,0},{160,32},{192,64},{224,... | collective-permute-start | bytes 294920 | tf_op jit(solution)/shard_map/ppermute | solution.py:29
  86.4 4.2 %collective-permute-done.6 = f32[96,256]{1,0:T(8,128)S(1)} collective-permute-done((f32[96,256]{1,0:T(8,128)S(1)}, f32[96,256]{1,0:T(8,128)S(1)}, u32[]{:S(2)}, u32[]{:S(2)}) %collective-permute-start.6) | collective-permute-done | bytes 98336 | tf_op jit(solution)/shard_map/ppermute | solution.py:29
  90.6 0.1 broadcast_in_dim.8
  90.6 18.5 %all_to_all.43 = f32[8,96,256]{2,1,0:T(8,128)S(1)} all-to-all(f32[8,96,256]{2,1,0:T(8,128)S(1)} %broadcast_in_dim.8), channel_id=1, replica_groups=mesh['prow'=8,'x'=4,'zl'=2,'y'=4] {'x','zl'}, dimensions={0} | all-to-all | bytes 1572864 | tf_op jit(solution)/shard_map/all_to_all | solution.py:31
  109.1 0.0 collective-permute-start.7
  109.1 0.0 copy-done.3
  109.1 0.1 scatter.14
  109.3 2.1 %collective-permute-done.7 = f32[768,256]{1,0:T(8,128)S(1)} collective-permute-done((f32[768,256]{1,0:T(8,128)S(1)}, f32[768,256]{1,0:T(8,128)S(1)}, u32[]{:S(2)}, u32[]{:S(2)}) %collective-permute-start.7) | collective-permute-done | bytes 786464 | tf_op jit(solution)/shard_map/ppermute | solution.py:33
  111.4 0.2 maximum_select_fusion
  111.7 0.2 fusion.38
  111.9 1.0 fusion.9
  113.0 0.3 slice_subtract_fusion.1
  113.3 0.2 fusion.30
  113.5 0.2 fusion.34
  113.8 0.3 slice_subtract_fusion
  114.1 0.4 slice_subtract_fusion.2
  114.5 7.9 %convolution_subtract_fusion = f32[512,1536]{1,0:T(8,128)} fusion(f32[512,1536]{1,0:T(8,128)} %bitcast.1, f32[1536,512]{1,0:T(8,128)S(1)} %constant_dynamic-update-slice_fusion, f32[512,128]{0,1:T(8,128)S(1)} %slice.213, f32[512,128]{0,1:T(8,128)S(1)} %slice_subtract_fusion.1, f32[512,128]{0,1:T(8,128)S(1)} %slice_subtract_fusion, ...), kind=kOutput, calls=%fused_computation.4 | convolution fusion | flops 2417491968 | bytes 10485760 | tf_op jit(solution)/shard_map/dot_general | solution.py:13
  122.5 3.7 %all-to-all-start.3 = ((f32[8,64,1536]{2,1,0:T(8,128)}), f32[8,64,1536]{2,1,0:T(8,128)S(1)}, u32[]{:S(2)}, u32[]{:S(2)}) async-start(f32[8,64,1536]{2,1,0:T(8,128)} %bitcast.45), calls=%async_computation.3 | async-start | bytes 6291456 | tf_op jit(solution)/shard_map/all_to_all | solution.py:95
  126.1 38.7 %all-to-all-done.3 = f32[8,64,1536]{2,1,0:T(8,128)S(1)} async-done(((f32[8,64,1536]{2,1,0:T(8,128)}), f32[8,64,1536]{2,1,0:T(8,128)S(1)}, u32[]{:S(2)}, u32[]{:S(2)}) %all-to-all-start.3) | async-done | bytes 3145760 | tf_op jit(solution)/shard_map/all_to_all | solution.py:95
  164.9 0.7 fusion.1
  165.6 1.9 %copy.13 = f32[8,8,8,1536]{3,2,0,1:T(8,128)} copy(f32[8,8,8,1536]{3,2,1,0:T(8,128)S(1)} %fusion.1) | data formatting | bytes 6291456 | tf_op jit(solution)/shard_map/reshape | solution.py:96
  (12 shorter events, 0.2 us)
Async XLA Ops:
  4.5 5.8 %copy-start.4 = (f32[384,512]{1,0:T(8,128)S(1)}, f32[384,512]{1,0:T(8,128)}, u32[]{:S(2)}) copy-start(f32[384,512]{1,0:T(8,128)} %param.12) | copy-start | bytes 2359300
  4.5 44.5 %all-to-all-start = ((f32[64,8,1536]{2,0,1:T(8,128)}), f32[64,8,1536]{2,0,1:T(8,128)}, u32[]{:S(2)}, u32[]{:S(2)}) async-start(f32[64,8,1536]{2,0,1:T(8,128)} %fusion.2), calls=%async_computation | async-start | bytes 6291456 | tf_op jit(solution)/shard_map/all_to_all | solution.py:67
  10.3 20.4 %collective-permute-start.1 = (f32[384,512]{1,0:T(8,128)S(1)}, f32[384,512]{1,0:T(8,128)S(1)}, u32[]{:S(2)}, u32[]{:S(2)}) collective-permute-start(f32[384,512]{1,0:T(8,128)S(1)} %copy-done.4), channel_id=1, source_target_pairs={{0,1},{1,2},{2,3},{3,0},{4,5},{5,6},{6,7},{7,4},{8,9},{9,10},{10,1... | collective-permute-start | bytes 2359304 | tf_op jit(solution)/shard_map/ppermute | solution.py:40
  12.0 20.7 %collective-permute-start = (f32[384,512]{1,0:T(8,128)S(1)}, f32[384,512]{1,0:T(8,128)S(1)}, u32[]{:S(2)}, u32[]{:S(2)}) collective-permute-start(f32[384,512]{1,0:T(8,128)S(1)} %copy-done.4), channel_id=1, source_target_pairs={{0,3},{1,0},{2,1},{3,2},{4,7},{5,4},{6,5},{7,6},{8,11},{9,8},{10,9... | collective-permute-start | bytes 2359304 | tf_op jit(solution)/shard_map/ppermute | solution.py:41
  30.7 0.9 copy-start
  32.3 11.3 %collective-permute-start.2 = (f32[192,512]{1,0:T(8,128)}, f32[192,512]{1,0:T(8,128)S(1)}, u32[]{:S(2)}, u32[]{:S(2)}) collective-permute-start(f32[192,512]{1,0:T(8,128)} %slice.200), channel_id=1, source_target_pairs={{0,1},{1,2},{2,3},{3,0},{4,5},{5,6},{6,7},{7,4},{8,9},{9,10},{10,1... | collective-permute-start | bytes 1179656 | tf_op jit(solution)/shard_map/ppermute | solution.py:43
  32.6 0.9 copy-start.2
  34.3 10.3 %collective-permute-start.3 = (f32[192,512]{1,0:T(8,128)}, f32[192,512]{1,0:T(8,128)}, u32[]{:S(2)}, u32[]{:S(2)}) collective-permute-start(f32[192,512]{1,0:T(8,128)} %slice.201), channel_id=1, source_target_pairs={{0,3},{1,0},{2,1},{3,2},{4,7},{5,4},{6,5},{7,6},{8,11},{9,8},{10,9... | collective-permute-start | bytes 1179656 | tf_op jit(solution)/shard_map/ppermute | solution.py:44
  37.3 8.4 %copy-start.1 = (f32[384,512]{1,0:T(8,128)S(1)}, f32[384,512]{1,0:T(8,128)}, u32[]{:S(2)}) copy-start(f32[384,512]{1,0:T(8,128)} %copy-done) | copy-start | bytes 2359300
  53.9 2.4 %collective-permute-start.4 = (f32[768,256]{1,0:T(8,128)S(1)}, f32[768,256]{1,0:T(8,128)S(1)}, u32[]{:S(2)}, u32[]{:S(2)}) collective-permute-start(f32[768,256]{1,0:T(8,128)S(1)} %slice_select_fusion), channel_id=1, source_target_pairs={{0,32},{32,0},{64,96},{96,64},{128,160},{160,128},{192,224},{224,1... | collective-permute-start | bytes 2359304 | tf_op jit(solution)/shard_map/ppermute | solution.py:23
  56.5 52.6 %copy-start.3 = (f32[4,128,128]{2,1,0:T(8,128)S(1)}, f32[4,128,128]{2,1,0:T(8,128)}, u32[]{:S(2)}) copy-start(f32[4,128,128]{2,1,0:T(8,128)} %param.13) | copy-start | bytes 786436
  75.9 5.7 %collective-permute-start.5 = (f32[96,256]{1,0:T(8,128)S(1)}, f32[96,256]{1,0:T(8,128)S(1)}, u32[]{:S(2)}, u32[]{:S(2)}) collective-permute-start(f32[96,256]{1,0:T(8,128)S(1)} %reduce_sum.9), channel_id=1, source_target_pairs={{0,64},{32,96},{64,0},{96,32},{128,192},{160,224},{192,128},{224,1... | collective-permute-start | bytes 294920 | tf_op jit(solution)/shard_map/ppermute | solution.py:29
  81.6 9.0 %collective-permute-start.6 = (f32[96,256]{1,0:T(8,128)S(1)}, f32[96,256]{1,0:T(8,128)S(1)}, u32[]{:S(2)}, u32[]{:S(2)}) collective-permute-start(f32[96,256]{1,0:T(8,128)S(1)} %add.35), channel_id=1, source_target_pairs={{0,128},{32,160},{64,192},{96,224},{128,0},{160,32},{192,64},{224,... | collective-permute-start | bytes 294920 | tf_op jit(solution)/shard_map/ppermute | solution.py:29
  109.1 2.3 %collective-permute-start.7 = (f32[768,256]{1,0:T(8,128)S(1)}, f32[768,256]{1,0:T(8,128)S(1)}, u32[]{:S(2)}, u32[]{:S(2)}) collective-permute-start(f32[768,256]{1,0:T(8,128)S(1)} %bitcast.47), channel_id=1, source_target_pairs={{0,32},{32,0},{64,96},{96,64},{128,160},{160,128},{192,224},{224,1... | collective-permute-start | bytes 2359304 | tf_op jit(solution)/shard_map/ppermute | solution.py:33
  122.5 42.4 %all-to-all-start.3 = ((f32[8,64,1536]{2,1,0:T(8,128)}), f32[8,64,1536]{2,1,0:T(8,128)S(1)}, u32[]{:S(2)}, u32[]{:S(2)}) async-start(f32[8,64,1536]{2,1,0:T(8,128)} %bitcast.45), calls=%async_computation.3 | async-start | bytes 6291456 | tf_op jit(solution)/shard_map/all_to_all | solution.py:95
